TPU v7x, 512 devices: a whole 4x4x16 slice. The times are simulated.
512 devices in a mesh: req: 32 (over y, x, core), mlp: 16 (over z).
Axes of the slice: x: 4, y: 4, z: 16, core: 2. Of those that a mesh axis runs over, the one named last changes fastest.
Arguments:
- queries: bfloat16 [12288, 4096], P('req', 'mlp')
- new_keys: bfloat16 [12288, 1024], P(('req', 'mlp')), may hold values from -5 to 5
- new_values: bfloat16 [12288, 1024], P(('req', 'mlp')), may hold values from -6 to 6
- cache_keys: bfloat16 [32, 4096, 1024], P('req', 'mlp')
- cache_values: bfloat16 [32, 4096, 1024], P('req', 'mlp'), may hold values from -6 to 6
- cache_len: int32 [32], P('req'), may hold values from 256 to 4096, as said below
- residual: bfloat16 [12288, 2560], P('req')
- out_weight: bfloat16 [4096, 2560], P('mlp'), may hold values from -0.1796875 to 0.1796875
- norm_gain: bfloat16 [2560], replicated, may hold values from 0.099609375 to 1.8984375
- gate_weight: bfloat16 [2560, 9728], P('req', 'mlp'), may hold values from -0.125 to 0.125
- up_weight: bfloat16 [2560, 9728], P('req', 'mlp'), may hold values from -0.125 to 0.125
- down_weight: bfloat16 [2560, 9728], P('req', 'mlp'), may hold values from -0.0625 to 0.0625
Outputs:
- layer_out: bfloat16 [12288, 2560], P(('req', 'mlp'))
Inputs may be any that keep to these rules, and one draw needn't show every extreme that they name: cache_len[r] counts request r's valid cached positions from the first; some request has exactly 4096.
All inputs are finite; a program needn't handle non-finite values.
Results may differ from a plain program's by a relative error of at most 0.012.
Values may be sent and summed in bfloat16 or wider, within the bound.
No kernel may reach another device: no remote copies, remote signals or barrier semaphores. Data moves between devices by JAX's collectives and lax.ppermute only.
A program may use at most 64 MiB of HBM per device.

v0:
```python
import jax
import jax.numpy as jnp
from jax import lax
from jax.sharding import PartitionSpec as P

H = 32
KVH = 8
HD = 128


norm_eps = 1e-06


def shards(
    queries,
    new_keys,
    new_values,
    cache_keys,
    cache_values,
    cache_len,
    residual,
    out_weight,
    norm_gain,
    gate_weight,
    up_weight,
    down_weight,
):
    n_mlp = lax.axis_size("mlp")
    heads_dev = H // n_mlp
    group_size = H // KVH
    kv_dev = max(1, heads_dev // group_size)
    per_kv = heads_dev // kv_dev
    query_rows = queries.shape[0]
    rows_dev = new_keys.shape[0]
    cache_total = cache_keys.shape[1] * n_mlp

    def to_slots(rows_block):
        row_count = rows_block.shape[0]
        copies = n_mlp // KVH
        spread = jnp.broadcast_to(
            rows_block.reshape(row_count, KVH, 1, HD), (row_count, KVH, copies, HD)
        )
        return spread.reshape(row_count, n_mlp, HD)

    arrived = (
        lax.all_to_all(to_slots(cache_keys[0]), "mlp", split_axis=1, concat_axis=0, tiled=True),
        lax.all_to_all(to_slots(cache_values[0]), "mlp", split_axis=1, concat_axis=0, tiled=True),
        lax.all_to_all(to_slots(new_keys), "mlp", split_axis=1, concat_axis=0, tiled=True),
        lax.all_to_all(to_slots(new_values), "mlp", split_axis=1, concat_axis=0, tiled=True),
    )
    keys_old = arrived[0]
    values_old = arrived[1]
    keys_new = arrived[2]
    values_new = arrived[3]
    grouped = queries.reshape(query_rows, kv_dev, per_kv, HD)
    score_scale = HD ** (-0.5)

    def absorb(running, key_part, value_part, allowed):
        row_max, row_sum, weighted = running
        scores = (
            jnp.einsum("tgqd,kgd->gqtk", grouped, key_part, preferred_element_type=jnp.float32)
            * score_scale
        )
        scores = jnp.where(allowed, scores, -jnp.inf)
        new_max = jnp.maximum(row_max, jnp.max(scores, axis=-1))
        shrink = jnp.exp(row_max - new_max)
        weights = jnp.exp(scores - new_max[..., None])
        row_sum = row_sum * shrink + jnp.sum(weights, axis=-1)
        weighted = weighted * shrink[..., None] + jnp.einsum(
            "gqtk,kgd->gqtd",
            weights.astype(jnp.bfloat16),
            value_part,
            preferred_element_type=jnp.float32,
        )
        return (new_max, row_sum, weighted)

    start_state = (
        jnp.full((kv_dev, per_kv, query_rows), -jnp.inf, jnp.float32),
        jnp.zeros((kv_dev, per_kv, query_rows), jnp.float32),
        jnp.zeros((kv_dev, per_kv, query_rows, HD), jnp.float32),
    )
    token_ids = lax.iota(jnp.int32, query_rows)
    causal = token_ids[None, :] <= token_ids[:, None]
    running = absorb(start_state, keys_new, values_new, causal)
    length = cache_len[0]
    key_block = min(512, cache_total)

    def visit(turn_index, running):
        offset = turn_index * key_block
        key_part = lax.dynamic_slice_in_dim(keys_old, offset, key_block, 0)
        value_part = lax.dynamic_slice_in_dim(values_old, offset, key_block, 0)
        positions = offset + lax.iota(jnp.int32, key_block)
        return absorb(running, key_part, value_part, (positions < length)[None, :])

    block_count = cache_total // key_block
    row_max, row_sum, weighted = lax.fori_loop(0, block_count, visit, running)
    attended = (weighted / row_sum[..., None]).astype(jnp.bfloat16)
    attended = attended.transpose(2, 0, 1, 3).reshape(query_rows, heads_dev * HD)
    partial_value = jnp.dot(attended, out_weight, preferred_element_type=jnp.float32)
    row_start = lax.axis_index("mlp") * rows_dev
    head_sum = lax.psum(partial_value.astype(jnp.bfloat16), "mlp").astype(jnp.float32)
    stream = (residual.astype(jnp.float32) + head_sum).astype(jnp.bfloat16)
    stream_full = stream.astype(jnp.float32)
    factor = lax.rsqrt(jnp.mean(stream_full * stream_full, axis=-1, keepdims=True) + norm_eps)
    normed = (stream_full * factor * norm_gain.astype(jnp.float32)).astype(jnp.bfloat16)
    stream_rows = lax.dynamic_slice_in_dim(stream, row_start, rows_dev, 0)
    gate_sum = jnp.dot(
        normed,
        lax.all_gather(gate_weight, "req", axis=0, tiled=True),
        preferred_element_type=jnp.float32,
    )
    up_sum = jnp.dot(
        normed,
        lax.all_gather(up_weight, "req", axis=0, tiled=True),
        preferred_element_type=jnp.float32,
    )
    hidden = (jax.nn.silu(gate_sum) * up_sum).astype(jnp.bfloat16)
    mlp_part = lax.dot_general(
        hidden,
        lax.all_gather(down_weight, "req", axis=0, tiled=True),
        (((1,), (1,)), ((), ())),
        preferred_element_type=jnp.float32,
    )
    mlp_rows = lax.psum_scatter(
        mlp_part.astype(jnp.bfloat16), "mlp", scatter_dimension=0, tiled=True
    ).astype(jnp.float32)
    return (stream_rows.astype(jnp.float32) + mlp_rows).astype(jnp.bfloat16)


def solution(mesh):
    in_specs = (
        P("req", "mlp"),
        P(("req", "mlp"), None),
        P(("req", "mlp"), None),
        P("req", "mlp", None),
        P("req", "mlp", None),
        P("req"),
        P("req", None),
        P("mlp", None),
        P(),
        P("req", "mlp"),
        P("req", "mlp"),
        P("req", "mlp"),
    )
    out_specs = P(("req", "mlp"), None)
    return jax.shard_map(shards, mesh=mesh, in_specs=in_specs, out_specs=out_specs, check_vma=False)
```

profile of v0, /device:TPU:6, one launch (start us, length us, event | category | flops | bytes accessed | tf_op | source)
XLA Modules:
  0.0 472.2 jit_solution(10438826310127697672)
XLA Ops:
  8.9 15.2 %all-to-all-start = ((bf16[24,16,128]{2,0,1:T(8,128)(2,1)}), bf16[24,16,128]{2,0,1:T(8,128)(2,1)S(1)}, u32[]{:S(2)}, u32[]{:S(2)}) async-start(bf16[24,16,128]{2,0,1:T(8,128)(2,1)} %bitcast.13), calls=%async_computation | async-start | bytes 196608 | tf_op jit(solution)/shard_map/all_to_all | solution.py:48
  25.0 12.7 %all-to-all-done = bf16[24,16,128]{2,0,1:T(8,128)(2,1)S(1)} async-done(((bf16[24,16,128]{2,0,1:T(8,128)(2,1)}), bf16[24,16,128]{2,0,1:T(8,128)(2,1)S(1)}, u32[]{:S(2)}, u32[]{:S(2)}) %all-to-all-start) | async-done | bytes 98336 | tf_op jit(solution)/shard_map/all_to_all | solution.py:48
  38.4 3.6 all-to-all-start.1
  43.2 11.9 %all-to-all-done.1 = bf16[24,16,128]{2,0,1:T(8,128)(2,1)S(1)} async-done(((bf16[24,16,128]{2,0,1:T(8,128)(2,1)}), bf16[24,16,128]{2,0,1:T(8,128)(2,1)S(1)}, u32[]{:S(2)}, u32[]{:S(2)}) %all-to-all-start.1) | async-done | bytes 98336 | tf_op jit(solution)/shard_map/all_to_all | solution.py:49
  56.3 3.7 all-to-all-start.2
  60.1 48.7 %all-to-all-done.2 = bf16[256,16,128]{2,0,1:T(8,128)(2,1)S(1)} async-done(((bf16[256,16,128]{2,0,1:T(8,128)(2,1)}), bf16[256,16,128]{2,0,1:T(8,128)(2,1)S(1)}, u32[]{:S(2)}, u32[]{:S(2)}) %all-to-all-start.2) | async-done | bytes 1048608 | tf_op jit(solution)/shard_map/all_to_all | solution.py:46
  108.9 1.3 broadcast_in_dim.100
  110.2 7.9 %all-to-all-start.3 = ((bf16[256,16,128]{2,0,1:T(8,128)(2,1)}), bf16[256,16,128]{2,0,1:T(8,128)(2,1)S(1)}, u32[]{:S(2)}, u32[]{:S(2)}) async-start(bf16[256,16,128]{2,0,1:T(8,128)(2,1)} %bitcast.35), calls=%async_computation.3 | async-start | bytes 2097152 | tf_op jit(solution)/shard_map/all_to_all | solution.py:47
  119.5 48.7 %all-to-all-done.3 = bf16[256,16,128]{2,0,1:T(8,128)(2,1)S(1)} async-done(((bf16[256,16,128]{2,0,1:T(8,128)(2,1)}), bf16[256,16,128]{2,0,1:T(8,128)(2,1)S(1)}, u32[]{:S(2)}, u32[]{:S(2)}) %all-to-all-start.3) | async-done | bytes 1048608 | tf_op jit(solution)/shard_map/all_to_all | solution.py:47
  168.2 22.4 %while.17 = (s32[]{:T(128)}, f32[1,2,384]{2,1,0:T(2,128)S(1)}, f32[1,2,384]{2,1,0:T(2,128)S(1)}, f32[1,2,384,128]{3,2,1,0:T(8,128)S(1)}, s32[]{:T(128)}, /*index...) while((s32[]{:T(128)}, f32[1,2,384]{2,1,0:T(2,128)S(1)}, ...), condition=%wide.region_5.6_spmd, body=%wide.region_2.5_spmd.sunk | while | flops 204279040 | bytes 6014131 | solution.py:96
  168.8 1.3 bitcast_reduce_fusion.2
  171.6 1.3 bitcast_reduce_fusion.2
  174.5 1.3 bitcast_reduce_fusion.2
  177.3 1.3 bitcast_reduce_fusion.2
  182.9 1.3 bitcast_reduce_fusion.2
  188.5 1.3 bitcast_reduce_fusion.2
  190.8 2.1 convolution_convert_fusion.1
  194.8 139.0 %all-reduce.2.cloned.1.call-done = bf16[384,2560]{1,0:T(8,128)(2,1)} async-done(((bf16[384,2560]{1,0:T(8,128)(2,1)}), bf16[384,2560]{1,0:T(8,128)(2,1)}) %all-reduce.2.cloned.1.call-update) | async-done | bytes 1966096 | tf_op jit(solution)/shard_map/psum | solution.py:101
  333.8 3.0 fusion.15
  336.8 4.8 %fusion.29 = f32[384,608]{0,1:T(8,128)} fusion(bf16[2560,608]{1,0:T(8,128)(2,1)} %all-gather.4.cloned.1.call-done, bf16[384,2560]{1,0:T(8,128)(2,1)S(1)} %get-tuple-element.174, f32[2560]{0:T(1024)S(1)} %convert_element_type.57, f32[384]{0:T(512)S(1)} %add_rsqrt_fusion), kind=kOutput, calls=%fused_computation.43 | convolution fusion | flops 1199308800 | bytes 6024704 | tf_op jit(solution)/shard_map/dot_general | solution.py:107
  341.6 40.2 %all-gather.8.cloned.1.call-done = bf16[2560,608]{1,0:T(8,128)(2,1)} async-done(((bf16[80,608]{1,0:T(8,128)(2,1)}), bf16[2560,608]{1,0:T(8,128)(2,1)}) %all-gather.8.cloned.1.call-update) | async-done | bytes 3112976 | tf_op jit(solution)/shard_map/all_gather | solution.py:120
  381.7 8.1 %convolution_convert_fusion = bf16[384,2560]{1,0:T(8,128)(2,1)} fusion(bf16[2560,608]{1,0:T(8,128)(2,1)} %all-gather.8.cloned.1.call-done, bf16[2560,608]{1,0:T(8,128)(2,1)} %all-gather.6.cloned.1.call-done, f32[384,608]{0,1:T(8,128)} %fusion.29, bf16[384,2560]{1,0:T(8,128)(2,1)S(1)} %get-tuple-element.174, f32[2560]{0:T(1024)S(1)} %convert_element_type.57, ...), kind=kOutput, calls=%fused_computation.24 | convolution fusion | flops 2397069312 | bytes 11103744 | tf_op jit(solution)/shard_map/dot_general | solution.py:118
  389.9 73.1 %reduce-scatter.2.cloned.1.call-done = bf16[24,2560]{1,0:T(8,128)(2,1)} async-done(((bf16[384,2560]{1,0:T(8,128)(2,1)}), bf16[24,2560]{1,0:T(8,128)(2,1)}) %reduce-scatter.2.cloned.1.call-update) | async-done | bytes 122896 | tf_op jit(solution)/shard_map/reduce_scatter | solution.py:124
  463.0 1.6 add_convert_fusion.1
  (93 shorter events, 23.2 us)
Async XLA Ops:
  7.4 183.5 %copy-start = (bf16[256,2560]{1,0:T(8,128)(2,1)S(1)}, bf16[256,2560]{1,0:T(8,128)(2,1)}, u32[]{:S(2)}) copy-start(bf16[256,2560]{1,0:T(8,128)(2,1)} %param.21) | copy-start | bytes 3932164
  8.9 28.8 %all-to-all-start = ((bf16[24,16,128]{2,0,1:T(8,128)(2,1)}), bf16[24,16,128]{2,0,1:T(8,128)(2,1)S(1)}, u32[]{:S(2)}, u32[]{:S(2)}) async-start(bf16[24,16,128]{2,0,1:T(8,128)(2,1)} %bitcast.13), calls=%async_computation | async-start | bytes 196608 | tf_op jit(solution)/shard_map/all_to_all | solution.py:48
  38.4 16.8 %all-to-all-start.1 = ((bf16[24,16,128]{2,0,1:T(8,128)(2,1)}), bf16[24,16,128]{2,0,1:T(8,128)(2,1)S(1)}, u32[]{:S(2)}, u32[]{:S(2)}) async-start(bf16[24,16,128]{2,0,1:T(8,128)(2,1)} %bitcast.23), calls=%async_computation.1 | async-start | bytes 196608 | tf_op jit(solution)/shard_map/all_to_all | solution.py:49
  43.2 16.8 %copy-start.2 = (bf16[1,256,1024]{2,1,0:T(8,128)(2,1)S(1)}, bf16[1,256,1024]{2,1,0:T(8,128)(2,1)}, u32[]{:S(2)}) copy-start(bf16[1,256,1024]{2,1,0:T(8,128)(2,1)} %param.18) | copy-start | bytes 1572868
  56.3 52.6 %all-to-all-start.2 = ((bf16[256,16,128]{2,0,1:T(8,128)(2,1)}), bf16[256,16,128]{2,0,1:T(8,128)(2,1)S(1)}, u32[]{:S(2)}, u32[]{:S(2)}) async-start(bf16[256,16,128]{2,0,1:T(8,128)(2,1)} %bitcast.30), calls=%async_computation.2 | async-start | bytes 2097152 | tf_op jit(solution)/shard_map/all_to_all | solution.py:46
  60.1 58.0 %copy-start.3 = (bf16[384,256]{1,0:T(8,128)(2,1)S(1)}, bf16[384,256]{1,0:T(8,128)(2,1)}, u32[]{:S(2)}) copy-start(bf16[384,256]{1,0:T(8,128)(2,1)} %param.14) | copy-start | bytes 589828
  108.8 1.3 copy-start.1
  110.2 58.0 %all-to-all-start.3 = ((bf16[256,16,128]{2,0,1:T(8,128)(2,1)}), bf16[256,16,128]{2,0,1:T(8,128)(2,1)S(1)}, u32[]{:S(2)}, u32[]{:S(2)}) async-start(bf16[256,16,128]{2,0,1:T(8,128)(2,1)} %bitcast.35), calls=%async_computation.3 | async-start | bytes 2097152 | tf_op jit(solution)/shard_map/all_to_all | solution.py:47
  118.1 215.7 %all-reduce.2.cloned.1.call-start = ((), (), s32[]{:S(2)}) async-start(), calls=%async_computation.5 | async-start | bytes 3932160 | tf_op jit(solution)/shard_map/psum | solution.py:101
  192.9 1.8 copy-start.4
  193.0 143.8 %all-gather.4.cloned.1.call-start = ((), (), s32[]{:S(2)}) async-start(), calls=%async_computation.6 | async-start | bytes 3379200 | tf_op jit(solution)/shard_map/all_gather | solution.py:109
  193.5 148.0 %all-gather.6.cloned.1.call-start = ((), (), s32[]{:S(2)}) async-start(), calls=%async_computation.7 | async-start | bytes 3379200 | tf_op jit(solution)/shard_map/all_gather | solution.py:114
  194.1 187.6 %all-gather.8.cloned.1.call-start = ((), (), s32[]{:S(2)}) async-start(), calls=%async_computation.8 | async-start | bytes 3379200 | tf_op jit(solution)/shard_map/all_gather | solution.py:120
  194.7 268.3 %reduce-scatter.2.cloned.1.call-start = ((), (), s32[]{:S(2)}) async-start(), calls=%async_computation.9 | async-start | bytes 2088960 | tf_op jit(solution)/shard_map/reduce_scatter | solution.py:124
Sparse Core Ops, SparseCore 0:
  193.1 140.6 all-reduce.1
  390.0 72.9 reduce-scatter.1
Sparse Core Ops, SparseCore 1:
  197.1 57.5 all-gather.3
  258.2 59.9 all-gather.5
  321.8 59.9 all-gather.7
where the time goes:
time: 473 us; the launch traced here: 472 us
  waiting for transfers between devices  376 us (79%)
  starting transfers between devices  30.5 us (6%)
  matrix products  30.4 us (6%)
  between operations  15.2 us (3%)
  other arithmetic  12.1 us (3%)
  local copies, waits for them, and re-layouts  7.44 us (2%)
    psum x1, waiting for transfers between devices, shards(): lax.psum(partial_value.astype(jnp.bfloat16), 'mlp').astype(jnp.float32)  139 us
    reduce_scatter x1, waiting for transfers between devices, shards(): lax.psum_scatter(mlp_part.astype(jnp.bfloat16), 'mlp', scatter_dimension=...  73.1 us
    all_to_all x1, waiting for transfers between devices, shards(): lax.all_to_all(to_slots(cache_keys[0]), 'mlp', split_axis=1, concat_axis=...  48.7 us
    all_to_all x1, waiting for transfers between devices, shards(): lax.all_to_all(to_slots(cache_values[0]), 'mlp', split_axis=1, concat_axi...  48.7 us
    all_gather x1, waiting for transfers between devices, shards(): lax.all_gather(down_weight, 'req', axis=0, tiled=True)  40.2 us
    all_to_all x1, starting transfers between devices, shards(): lax.all_to_all(to_slots(new_keys), 'mlp', split_axis=1, concat_axis=0, ti...  15.2 us
    all_to_all x1, waiting for transfers between devices, shards(): lax.all_to_all(to_slots(new_keys), 'mlp', split_axis=1, concat_axis=0, ti...  12.7 us
    all_to_all x1, waiting for transfers between devices, shards(): lax.all_to_all(to_slots(new_values), 'mlp', split_axis=1, concat_axis=0,...  11.9 us
  transfers between devices with their start and end apart: 9, of which 7 were waited for; matrix products, arithmetic and copies ran while one was open for 2% of the time, Pallas kernels for 0%

commit v1 on v0

v1 whole, which is shorter than its diff:
```python
import jax
import jax.numpy as jnp
from jax import lax
from jax.sharding import PartitionSpec as P

H = 32
KVH = 8
HD = 128


norm_eps = 1e-06


def shards(
    queries,
    new_keys,
    new_values,
    cache_keys,
    cache_values,
    cache_len,
    residual,
    out_weight,
    norm_gain,
    gate_weight,
    up_weight,
    down_weight,
):
    n_mlp = lax.axis_size("mlp")
    heads_dev = H // n_mlp
    group_size = H // KVH
    copies = n_mlp // KVH
    assert copies == 2 and heads_dev * copies == group_size
    query_rows = queries.shape[0]
    rows_dev = new_keys.shape[0]
    cache_dev = cache_keys.shape[1]
    cache_half = cache_dev // copies
    new_half = rows_dev // copies
    my_index = lax.axis_index("mlp")
    my_half = my_index % copies

    def to_slots(rows_block, half_rows):
        spread = rows_block.reshape(copies, half_rows, KVH, HD).transpose(1, 2, 0, 3)
        return spread.reshape(half_rows, KVH * copies, HD)

    send = jnp.concatenate(
        [
            to_slots(cache_keys[0], cache_half),
            to_slots(cache_values[0], cache_half),
            to_slots(new_keys, new_half),
            to_slots(new_values, new_half),
        ],
        axis=0,
    )
    arrived = lax.all_to_all(send, "mlp", split_axis=1, concat_axis=0, tiled=True)
    per_src = 2 * cache_half + 2 * new_half
    arrived = arrived.reshape(n_mlp, per_src, HD)
    keys_old = arrived[:, :cache_half].reshape(n_mlp * cache_half, HD)
    values_old = arrived[:, cache_half : 2 * cache_half].reshape(n_mlp * cache_half, HD)
    keys_new = arrived[:, 2 * cache_half : 2 * cache_half + new_half].reshape(n_mlp * new_half, HD)
    values_new = arrived[:, 2 * cache_half + new_half :].reshape(n_mlp * new_half, HD)

    pair = [(d, d ^ 1) for d in range(n_mlp)]
    partner_q = lax.ppermute(queries, "mlp", pair)
    grouped = jnp.concatenate([queries, partner_q], axis=1).reshape(query_rows, group_size, HD)
    score_scale = HD ** (-0.5)

    def absorb(running, key_part, value_part, allowed):
        row_max, row_sum, weighted = running
        scores = (
            jnp.einsum("tqd,kd->qtk", grouped, key_part, preferred_element_type=jnp.float32)
            * score_scale
        )
        scores = jnp.where(allowed, scores, -jnp.inf)
        new_max = jnp.maximum(row_max, jnp.max(scores, axis=-1))
        shrink = jnp.exp(row_max - new_max)
        weights = jnp.exp(scores - new_max[..., None])
        row_sum = row_sum * shrink + jnp.sum(weights, axis=-1)
        weighted = weighted * shrink[..., None] + jnp.einsum(
            "qtk,kd->qtd",
            weights.astype(jnp.bfloat16),
            value_part,
            preferred_element_type=jnp.float32,
        )
        return (new_max, row_sum, weighted)

    start_state = (
        jnp.full((group_size, query_rows), -jnp.inf, jnp.float32),
        jnp.zeros((group_size, query_rows), jnp.float32),
        jnp.zeros((group_size, query_rows, HD), jnp.float32),
    )
    length = cache_len[0]
    cache_count = n_mlp * cache_half
    key_block = min(512, cache_count)

    def cached_positions(idx):
        return (idx // cache_half) * cache_dev + my_half * cache_half + idx % cache_half

    def visit(turn_index, running):
        offset = turn_index * key_block
        key_part = lax.dynamic_slice_in_dim(keys_old, offset, key_block, 0)
        value_part = lax.dynamic_slice_in_dim(values_old, offset, key_block, 0)
        positions = cached_positions(offset + lax.iota(jnp.int32, key_block))
        return absorb(running, key_part, value_part, (positions < length)[None, :])

    running = lax.fori_loop(0, cache_count // key_block, visit, start_state)
    new_idx = lax.iota(jnp.int32, n_mlp * new_half)
    new_pos = (new_idx // new_half) * rows_dev + my_half * new_half + new_idx % new_half
    token_ids = lax.iota(jnp.int32, query_rows)
    causal = new_pos[None, :] <= token_ids[:, None]
    row_max, row_sum, weighted = absorb(running, keys_new, values_new, causal)

    sent = lax.ppermute(
        (weighted[heads_dev:], row_max[heads_dev:], row_sum[heads_dev:]), "mlp", pair
    )
    other_weighted, other_max, other_sum = sent
    mine_max = row_max[:heads_dev]
    top = jnp.maximum(mine_max, other_max)
    scale_a = jnp.exp(mine_max - top)
    scale_b = jnp.exp(other_max - top)
    total = row_sum[:heads_dev] * scale_a + other_sum * scale_b
    mixed = weighted[:heads_dev] * scale_a[..., None] + other_weighted * scale_b[..., None]
    attended = (mixed / total[..., None]).astype(jnp.bfloat16)
    attended = attended.transpose(1, 0, 2).reshape(query_rows, heads_dev * HD)
    partial_value = jnp.dot(attended, out_weight, preferred_element_type=jnp.float32)
    row_start = my_index * rows_dev
    head_sum = lax.psum(partial_value.astype(jnp.bfloat16), "mlp").astype(jnp.float32)
    stream = (residual.astype(jnp.float32) + head_sum).astype(jnp.bfloat16)
    stream_full = stream.astype(jnp.float32)
    factor = lax.rsqrt(jnp.mean(stream_full * stream_full, axis=-1, keepdims=True) + norm_eps)
    normed = (stream_full * factor * norm_gain.astype(jnp.float32)).astype(jnp.bfloat16)
    stream_rows = lax.dynamic_slice_in_dim(stream, row_start, rows_dev, 0)
    gate_sum = jnp.dot(
        normed,
        lax.all_gather(gate_weight, "req", axis=0, tiled=True),
        preferred_element_type=jnp.float32,
    )
    up_sum = jnp.dot(
        normed,
        lax.all_gather(up_weight, "req", axis=0, tiled=True),
        preferred_element_type=jnp.float32,
    )
    hidden = (jax.nn.silu(gate_sum) * up_sum).astype(jnp.bfloat16)
    mlp_part = lax.dot_general(
        hidden,
        lax.all_gather(down_weight, "req", axis=0, tiled=True),
        (((1,), (1,)), ((), ())),
        preferred_element_type=jnp.float32,
    )
    mlp_rows = lax.psum_scatter(
        mlp_part.astype(jnp.bfloat16), "mlp", scatter_dimension=0, tiled=True
    ).astype(jnp.float32)
    return (stream_rows.astype(jnp.float32) + mlp_rows).astype(jnp.bfloat16)


def solution(mesh):
    in_specs = (
        P("req", "mlp"),
        P(("req", "mlp"), None),
        P(("req", "mlp"), None),
        P("req", "mlp", None),
        P("req", "mlp", None),
        P("req"),
        P("req", None),
        P("mlp", None),
        P(),
        P("req", "mlp"),
        P("req", "mlp"),
        P("req", "mlp"),
    )
    out_specs = P(("req", "mlp"), None)
    return jax.shard_map(shards, mesh=mesh, in_specs=in_specs, out_specs=out_specs, check_vma=False)
```

time: 473 us -> 423 us (0.89)
  waiting for transfers between devices: 376 us -> 313 us
  other arithmetic: 12.1 us -> 19.9 us
  matrix products: 30.4 us -> 37.6 us
    all_to_all x4 -> x1, waiting for transfers between devices: 122 us -> 0.01 us  [shards(): lax.all_to_all(send, 'mlp', split_axis=1, concat_axis=0, tiled=True)]
    ppermute x0 -> x4, waiting for transfers between devices: none -> 55.5 us  [the longest x1 51.5 us: shards(): partner_q = lax.ppermute(queries, 'mlp', pair)]
    all_to_all x4 -> x1, starting transfers between devices: 30.3 us -> 15.2 us  [shards(): lax.all_to_all(send, 'mlp', split_axis=1, concat_axis=0, tiled=True)]
    ppermute x0 -> x4, starting transfers between devices: none -> 11.9 us  [the longest x3 8.09 us: shards(): lax.ppermute((weighted[heads_dev:], row_max[heads_dev:], row_sum[heads_de...]
    reduce_sum x9 -> x5, other arithmetic: 2.01 us -> 11.2 us  [absorb(): row_sum = row_sum * shrink + jnp.sum(weights, axis=-1)]
    dot_general x18 -> x10, matrix products: 15.4 us -> 22.6 us  [the longest x5 13.1 us: absorb(): jnp.einsum('tqd,kd->qtk', grouped, key_part, preferred_element_type=jnp.f...]
    broadcast_in_dim x8 -> x0, local copies, waits for them, and re-layouts: 5.68 us -> none  [to_slots(): jnp.broadcast_to(rows_block.reshape(row_count, KVH, 1, HD), (row_count, K...]
  transfers between devices with their start and end apart: 9 -> 10, of which waited for: 7 -> 5; matrix products, arithmetic and copies ran while one was open for 2% -> 2% of each run, Pallas kernels for 0% -> 0%
where the time goes in v1:
time: 423 us; the launch traced here: 422 us
  waiting for transfers between devices  313 us (74%)
  matrix products  37.6 us (9%)
  starting transfers between devices  27.5 us (7%)
  other arithmetic  19.9 us (5%)
  between operations  15.4 us (4%)
  local copies, waits for them, and re-layouts  8.76 us (2%)
    psum x1, waiting for transfers between devices, shards(): lax.psum(partial_value.astype(jnp.bfloat16), 'mlp').astype(jnp.float32)  142 us
    reduce_scatter x1, waiting for transfers between devices, shards(): lax.psum_scatter(mlp_part.astype(jnp.bfloat16), 'mlp', scatter_dimension=...  73.1 us
    ppermute x1, waiting for transfers between devices, shards(): partner_q = lax.ppermute(queries, 'mlp', pair)  51.5 us
    all_gather x1, waiting for transfers between devices, shards(): lax.all_gather(down_weight, 'req', axis=0, tiled=True)  40.3 us
    all_to_all x1, starting transfers between devices, shards(): lax.all_to_all(send, 'mlp', split_axis=1, concat_axis=0, tiled=True)  15.2 us
    dot_general x5, matrix products, absorb(): jnp.einsum('tqd,kd->qtk', grouped, key_part, preferred_element_type=jnp.f...  13.1 us
    reduce_sum x5, other arithmetic, absorb(): row_sum = row_sum * shrink + jnp.sum(weights, axis=-1)  11.2 us
    dot_general x5, matrix products, absorb(): jnp.einsum('qtk,kd->qtd', weights.astype(jnp.bfloat16), value_part, prefe...  9.5 us
  transfers between devices with their start and end apart: 10, of which 5 were waited for; matrix products, arithmetic and copies ran while one was open for 2% of the time, Pallas kernels for 0%

profile of v1, /device:TPU:6, one launch (start us, length us, event | category | flops | bytes accessed | tf_op | source)
XLA Modules:
  0.0 422.1 jit_solution(15669107477665778246)
XLA Ops:
  10.7 15.2 %all-to-all-start = ((bf16[280,16,128]{2,0,1:T(8,128)(2,1)}), bf16[280,16,128]{2,0,1:T(8,128)(2,1)S(1)}, u32[]{:S(2)}, u32[]{:S(2)}) async-start(bf16[280,16,128]{2,0,1:T(8,128)(2,1)} %pad_maximum_fusion), calls=%async_computation | async-start | bytes 2293760 | tf_op jit(solution)/shard_map/all_to_all | solution.py:54
  26.1 3.8 collective-permute-start
  30.2 51.5 %collective-permute-done = bf16[384,256]{0,1:T(8,128)(2,1)S(1)} collective-permute-done((bf16[384,256]{0,1:T(8,128)(2,1)S(1)}, bf16[384,256]{0,1:T(8,128)(2,1)S(1)}, u32[]{:S(2)}, u32[]{:S(2)}) %collective-permute-start) | collective-permute-done | bytes 196640 | tf_op jit(solution)/shard_map/ppermute | solution.py:63
  83.1 39.6 %while.20 = (s32[]{:T(128)}, f32[4,384]{1,0:T(4,128)S(1)}, f32[4,384]{1,0:T(4,128)S(1)}, f32[4,384,128]{2,1,0:T(8,128)}, s32[]{:T(128)}, /*index=5*/s32[]{:T(128...) while((s32[]{:T(128)}, f32[4,384]{1,0:T(4,128)S(1)}, ...), condition=%wide.region_3.4_spmd.clone, body=%wide.region_0.3_spmd.clone.sunk | while | flops 411913728 | bytes 30640412 | solution.py:105
  83.8 3.2 bitcast_reduce_fusion.2
  87.0 2.8 fusion.80
  89.9 2.3 fusion.82
  93.7 3.2 bitcast_reduce_fusion.2
  96.9 2.8 fusion.80
  99.8 2.3 fusion.82
  103.6 3.2 bitcast_reduce_fusion.2
  106.9 2.8 fusion.80
  109.7 2.3 fusion.82
  113.5 3.2 bitcast_reduce_fusion.2
  116.7 2.8 fusion.80
  119.6 2.3 fusion.82
  127.4 3.6 collective-permute-start.3
  133.3 3.9 collective-permute-done.3
  141.5 142.0 %all-reduce.2.cloned.1.call-done = bf16[384,2560]{1,0:T(8,128)(2,1)} async-done(((bf16[384,2560]{1,0:T(8,128)(2,1)}), bf16[384,2560]{1,0:T(8,128)(2,1)}) %all-reduce.2.cloned.1.call-update) | async-done | bytes 1966096 | tf_op jit(solution)/shard_map/psum | solution.py:126
  283.5 3.0 fusion.28
  286.5 4.8 %fusion.40 = f32[384,608]{0,1:T(8,128)} fusion(bf16[2560,608]{1,0:T(8,128)(2,1)} %all-gather.4.cloned.1.call-done, bf16[384,2560]{1,0:T(8,128)(2,1)S(1)} %get-tuple-element.295, f32[2560]{0:T(1024)S(1)} %convert_element_type.60, f32[384]{0:T(512)S(1)} %add_rsqrt_fusion), kind=kOutput, calls=%fused_computation.58 | convolution fusion | flops 1199308800 | bytes 6024704 | tf_op jit(solution)/shard_map/dot_general | solution.py:132
  291.3 40.3 %all-gather.8.cloned.1.call-done = bf16[2560,608]{1,0:T(8,128)(2,1)} async-done(((bf16[80,608]{1,0:T(8,128)(2,1)}), bf16[2560,608]{1,0:T(8,128)(2,1)}) %all-gather.8.cloned.1.call-update) | async-done | bytes 3112976 | tf_op jit(solution)/shard_map/all_gather | solution.py:145
  331.6 8.1 %convolution_convert_fusion = bf16[384,2560]{1,0:T(8,128)(2,1)} fusion(bf16[2560,608]{1,0:T(8,128)(2,1)} %all-gather.8.cloned.1.call-done, bf16[2560,608]{1,0:T(8,128)(2,1)} %all-gather.6.cloned.1.call-done, f32[384,608]{0,1:T(8,128)} %fusion.40, bf16[384,2560]{1,0:T(8,128)(2,1)S(1)} %get-tuple-element.295, f32[2560]{0:T(1024)S(1)} %convert_element_type.60, ...), kind=kOutput, calls=%fused_computation.41 | convolution fusion | flops 2397069312 | bytes 11103744 | tf_op jit(solution)/shard_map/dot_general | solution.py:143
  339.8 73.1 %reduce-scatter.2.cloned.1.call-done = bf16[24,2560]{1,0:T(8,128)(2,1)} async-done(((bf16[384,2560]{1,0:T(8,128)(2,1)}), bf16[24,2560]{1,0:T(8,128)(2,1)}) %reduce-scatter.2.cloned.1.call-update) | async-done | bytes 122896 | tf_op jit(solution)/shard_map/reduce_scatter | solution.py:149
  (107 shorter events, 24.0 us)
Async XLA Ops:
  7.4 130.0 %copy-start = (bf16[256,2560]{1,0:T(8,128)(2,1)S(1)}, bf16[256,2560]{1,0:T(8,128)(2,1)}, u32[]{:S(2)}) copy-start(bf16[256,2560]{1,0:T(8,128)(2,1)} %param.21) | copy-start | bytes 3932164
  7.4 1.4 copy-start.4
  9.6 16.4 %copy-start.5 = (bf16[384,256]{1,0:T(8,128)(2,1)S(1)}, bf16[384,256]{1,0:T(8,128)(2,1)}, u32[]{:S(2)}) copy-start(bf16[384,256]{1,0:T(8,128)(2,1)} %param.14) | copy-start | bytes 589828
  10.7 71.3 %all-to-all-start = ((bf16[280,16,128]{2,0,1:T(8,128)(2,1)}), bf16[280,16,128]{2,0,1:T(8,128)(2,1)S(1)}, u32[]{:S(2)}, u32[]{:S(2)}) async-start(bf16[280,16,128]{2,0,1:T(8,128)(2,1)} %pad_maximum_fusion), calls=%async_computation | async-start | bytes 2293760 | tf_op jit(solution)/shard_map/all_to_all | solution.py:54
  25.9 257.6 %all-reduce.2.cloned.1.call-start = ((), (), s32[]{:S(2)}) async-start(), calls=%async_computation.2 | async-start | bytes 3932160 | tf_op jit(solution)/shard_map/psum | solution.py:126
  26.1 55.6 %collective-permute-start = (bf16[384,256]{0,1:T(8,128)(2,1)S(1)}, bf16[384,256]{0,1:T(8,128)(2,1)S(1)}, u32[]{:S(2)}, u32[]{:S(2)}) collective-permute-start(bf16[384,256]{0,1:T(8,128)(2,1)S(1)} %copy.25), channel_id=1, source_target_pairs={{0,1},{1,0},{2,3},{3,2},{4,5},{5,4},{6,7},{7,6},{8,9},{9,8},{10,11... | collective-permute-start | bytes 589832 | tf_op jit(solution)/shard_map/ppermute | solution.py:63
  83.8 6.0 %copy-start.2 = (f32[4,384,128]{2,1,0:T(8,128)S(1)}, f32[4,384,128]{2,1,0:T(8,128)}, u32[]{:S(2)}) copy-start(f32[4,384,128]{2,1,0:T(8,128)} %get-tuple-element.388) | copy-start | bytes 2359300 | tf_op jit(solution)/shard_map/while
  87.0 2.8 copy-start.1
  93.7 6.0 %copy-start.2 = (f32[4,384,128]{2,1,0:T(8,128)S(1)}, f32[4,384,128]{2,1,0:T(8,128)}, u32[]{:S(2)}) copy-start(f32[4,384,128]{2,1,0:T(8,128)} %get-tuple-element.388) | copy-start | bytes 2359300 | tf_op jit(solution)/shard_map/while
  96.9 2.8 copy-start.1
  102.1 0.9 copy-start.3
  103.6 6.0 %copy-start.2 = (f32[4,384,128]{2,1,0:T(8,128)S(1)}, f32[4,384,128]{2,1,0:T(8,128)}, u32[]{:S(2)}) copy-start(f32[4,384,128]{2,1,0:T(8,128)} %get-tuple-element.388) | copy-start | bytes 2359300 | tf_op jit(solution)/shard_map/while
  106.8 2.8 copy-start.1
  113.5 6.0 %copy-start.2 = (f32[4,384,128]{2,1,0:T(8,128)S(1)}, f32[4,384,128]{2,1,0:T(8,128)}, u32[]{:S(2)}) copy-start(f32[4,384,128]{2,1,0:T(8,128)} %get-tuple-element.388) | copy-start | bytes 2359300 | tf_op jit(solution)/shard_map/while
  116.7 2.8 copy-start.1
  121.9 0.9 copy-start.3
  125.1 12.1 %collective-permute-start.2 = (f32[2,384,128]{1,2,0:T(8,128)S(1)}, f32[2,384,128]{1,2,0:T(8,128)S(1)}, u32[]{:S(2)}, u32[]{:S(2)}) collective-permute-start(f32[2,384,128]{1,2,0:T(8,128)S(1)} %slice.47), channel_id=1, source_target_pairs={{0,1},{1,0},{2,3},{3,2},{4,5},{5,4},{6,7},{7,6},{8,9},{9,8},{10,11... | collective-permute-start | bytes 1179656 | tf_op jit(solution)/shard_map/ppermute | solution.py:112
  127.4 9.8 %collective-permute-start.3 = (f32[2,384]{1,0:T(2,128)S(1)}, f32[2,384]{1,0:T(2,128)S(1)}, u32[]{:S(2)}, u32[]{:S(2)}) collective-permute-start(f32[2,384]{1,0:T(2,128)S(1)} %slice.49), channel_id=1, source_target_pairs={{0,1},{1,0},{2,3},{3,2},{4,5},{5,4},{6,7},{7,6},{8,9},{9,8},{10,11... | collective-permute-start | bytes 9224 | tf_op jit(solution)/shard_map/ppermute | solution.py:112
  131.0 6.2 %collective-permute-start.1 = (f32[2,384]{1,0:T(2,128)S(1)}, f32[2,384]{1,0:T(2,128)S(1)}, u32[]{:S(2)}, u32[]{:S(2)}) collective-permute-start(f32[2,384]{1,0:T(2,128)S(1)} %slice.46), channel_id=1, source_target_pairs={{0,1},{1,0},{2,3},{3,2},{4,5},{5,4},{6,7},{7,6},{8,9},{9,8},{10,11... | collective-permute-start | bytes 9224 | tf_op jit(solution)/shard_map/ppermute | solution.py:112
  137.4 4.1 copy-start.8
  139.5 147.0 %all-gather.4.cloned.1.call-start = ((), (), s32[]{:S(2)}) async-start(), calls=%async_computation.3 | async-start | bytes 3379200 | tf_op jit(solution)/shard_map/all_gather | solution.py:134
  140.1 151.2 %all-gather.6.cloned.1.call-start = ((), (), s32[]{:S(2)}) async-start(), calls=%async_computation.4 | async-start | bytes 3379200 | tf_op jit(solution)/shard_map/all_gather | solution.py:139
  140.7 191.0 %all-gather.8.cloned.1.call-start = ((), (), s32[]{:S(2)}) async-start(), calls=%async_computation.5 | async-start | bytes 3379200 | tf_op jit(solution)/shard_map/all_gather | solution.py:145
  141.2 271.7 %reduce-scatter.2.cloned.1.call-start = ((), (), s32[]{:S(2)}) async-start(), calls=%async_computation.6 | async-start | bytes 2088960 | tf_op jit(solution)/shard_map/reduce_scatter | solution.py:149
  (4 other events, 3.4 us)
Sparse Core Ops, SparseCore 0:
  139.6 143.8 all-reduce.1
  339.9 72.9 reduce-scatter.1
Sparse Core Ops, SparseCore 1:
  143.6 60.9 all-gather.3
  208.2 59.8 all-gather.5
  271.6 60.0 all-gather.7

commit v2 on v1

--- a/solution.py
+++ b/solution.py
@@ -129,20 +129,16 @@
     factor = lax.rsqrt(jnp.mean(stream_full * stream_full, axis=-1, keepdims=True) + norm_eps)
     normed = (stream_full * factor * norm_gain.astype(jnp.float32)).astype(jnp.bfloat16)
     stream_rows = lax.dynamic_slice_in_dim(stream, row_start, rows_dev, 0)
-    gate_sum = jnp.dot(
-        normed,
-        lax.all_gather(gate_weight, "req", axis=0, tiled=True),
-        preferred_element_type=jnp.float32,
+    units = gate_weight.shape[1]
+    weights_full = lax.all_gather(
+        jnp.concatenate([gate_weight, up_weight, down_weight], axis=1), "req", axis=0, tiled=True
     )
-    up_sum = jnp.dot(
-        normed,
-        lax.all_gather(up_weight, "req", axis=0, tiled=True),
-        preferred_element_type=jnp.float32,
-    )
+    gate_sum = jnp.dot(normed, weights_full[:, :units], preferred_element_type=jnp.float32)
+    up_sum = jnp.dot(normed, weights_full[:, units : 2 * units], preferred_element_type=jnp.float32)
     hidden = (jax.nn.silu(gate_sum) * up_sum).astype(jnp.bfloat16)
     mlp_part = lax.dot_general(
         hidden,
-        lax.all_gather(down_weight, "req", axis=0, tiled=True),
+        weights_full[:, 2 * units :],
         (((1,), (1,)), ((), ())),
         preferred_element_type=jnp.float32,
     )

time: 423 us -> 380 us (0.90)
  waiting for transfers between devices: 313 us -> 267 us
    all_gather x3 -> x1, waiting for transfers between devices: 40.4 us -> 0.03 us  [shards(): lax.all_gather(jnp.concatenate([gate_weight, up_weight, down_weight], axi...]
  transfers between devices with their start and end apart: 10 -> 8, of which waited for: 5 -> 4; matrix products, arithmetic and copies ran while one was open for 2% -> 1% of each run, Pallas kernels for 0% -> 0%
where the time goes in v2:
time: 380 us
  waiting for transfers between devices  267 us (70%)
  matrix products  39.8 us (10%)
  starting transfers between devices  27.4 us (7%)
  other arithmetic  19.9 us (5%)
  between operations  15.3 us (4%)
  local copies, waits for them, and re-layouts  9.76 us (3%)
    psum x1, waiting for transfers between devices, shards(): lax.psum(partial_value.astype(jnp.bfloat16), 'mlp').astype(jnp.float32)  143 us
    reduce_scatter x1, waiting for transfers between devices, shards(): lax.psum_scatter(mlp_part.astype(jnp.bfloat16), 'mlp', scatter_dimension=...  69 us
    ppermute x1, waiting for transfers between devices, shards(): partner_q = lax.ppermute(queries, 'mlp', pair)  51.5 us
    all_to_all x1, starting transfers between devices, shards(): lax.all_to_all(send, 'mlp', split_axis=1, concat_axis=0, tiled=True)  15.2 us
    dot_general x5, matrix products, absorb(): jnp.einsum('tqd,kd->qtk', grouped, key_part, preferred_element_type=jnp.f...  13.1 us
    reduce_sum x5, other arithmetic, absorb(): row_sum = row_sum * shrink + jnp.sum(weights, axis=-1)  11.2 us
    dot_general x1, matrix products, shards(): lax.dot_general(hidden, weights_full[:, 2 * units:], (((1,), (1,)), ((),...  10.3 us
    dot_general x5, matrix products, absorb(): jnp.einsum('qtk,kd->qtd', weights.astype(jnp.bfloat16), value_part, prefe...  9.5 us
  transfers between devices with their start and end apart: 8, of which 4 were waited for; matrix products, arithmetic and copies ran while one was open for 1% of the time, Pallas kernels for 0%

profile of v2, /device:TPU:6, one launch (start us, length us, event | category | flops | bytes accessed | tf_op | source)
XLA Modules:
  0.0 379.7 jit_solution(3073792401432842731)
XLA Ops:
  10.7 15.2 %all-to-all-start = ((bf16[280,16,128]{2,0,1:T(8,128)(2,1)}), bf16[280,16,128]{2,0,1:T(8,128)(2,1)S(1)}, u32[]{:S(2)}, u32[]{:S(2)}) async-start(bf16[280,16,128]{2,0,1:T(8,128)(2,1)} %pad_maximum_fusion), calls=%async_computation | async-start | bytes 2293760 | tf_op jit(solution)/shard_map/all_to_all | solution.py:54
  26.1 3.8 %collective-permute-start = (bf16[384,256]{0,1:T(8,128)(2,1)S(1)}, bf16[384,256]{0,1:T(8,128)(2,1)S(1)}, u32[]{:S(2)}, u32[]{:S(2)}) collective-permute-start(bf16[384,256]{0,1:T(8,128)(2,1)S(1)} %copy.25), channel_id=1, source_target_pairs={{0,1},{1,0},{2,3},{3,2},{4,5},{5,4},{6,7},{7,6},{8,9},{9,8},{10,11... | collective-permute-start | bytes 589832 | tf_op jit(solution)/shard_map/ppermute | solution.py:63
  30.2 51.5 %collective-permute-done = bf16[384,256]{0,1:T(8,128)(2,1)S(1)} collective-permute-done((bf16[384,256]{0,1:T(8,128)(2,1)S(1)}, bf16[384,256]{0,1:T(8,128)(2,1)S(1)}, u32[]{:S(2)}, u32[]{:S(2)}) %collective-permute-start) | collective-permute-done | bytes 196640 | tf_op jit(solution)/shard_map/ppermute | solution.py:63
  83.1 39.7 %while.20 = (s32[]{:T(128)}, f32[4,384]{1,0:T(4,128)S(1)}, f32[4,384]{1,0:T(4,128)S(1)}, f32[4,384,128]{2,1,0:T(8,128)}, s32[]{:T(128)}, /*index=5*/s32[]{:T(128...) while((s32[]{:T(128)}, f32[4,384]{1,0:T(4,128)S(1)}, ...), condition=%wide.region_3.4_spmd.clone, body=%wide.region_0.3_spmd.clone.sunk | while | flops 411913728 | bytes 30640412 | solution.py:105
  83.8 3.2 bitcast_reduce_fusion.2
  87.0 2.8 fusion.93
  89.9 2.3 fusion.95
  93.7 3.2 bitcast_reduce_fusion.2
  97.0 2.8 fusion.93
  99.8 2.3 fusion.95
  103.7 3.2 bitcast_reduce_fusion.2
  106.9 2.8 fusion.93
  109.7 2.3 fusion.95
  113.6 3.2 bitcast_reduce_fusion.2
  116.8 2.8 fusion.93
  119.6 2.3 fusion.95
  125.2 2.2 collective-permute-start.2
  127.5 3.6 collective-permute-start.3
  133.3 3.9 %collective-permute-done.3 = f32[2,384]{1,0:T(2,128)S(1)} collective-permute-done((f32[2,384]{1,0:T(2,128)S(1)}, f32[2,384]{1,0:T(2,128)S(1)}, u32[]{:S(2)}, u32[]{:S(2)}) %collective-permute-start.3) | collective-permute-done | bytes 3104 | tf_op jit(solution)/shard_map/ppermute | solution.py:112
  140.8 142.8 %all-reduce.2.cloned.1.call-done = bf16[384,2560]{1,0:T(8,128)(2,1)} async-done(((bf16[384,2560]{1,0:T(8,128)(2,1)}), bf16[384,2560]{1,0:T(8,128)(2,1)}) %all-reduce.2.cloned.1.call-update) | async-done | bytes 1966096 | tf_op jit(solution)/shard_map/psum | solution.py:126
  283.6 3.0 fusion.28
  286.6 4.8 %fusion.34 = f32[384,608]{0,1:T(8,128)} fusion(bf16[2560,1824]{1,0:T(8,128)(2,1)} %all-gather.2.cloned.1.call-done, bf16[384,2560]{1,0:T(8,128)(2,1)S(1)} %get-tuple-element.295, f32[2560]{0:T(1024)S(1)} %convert_element_type.60, f32[384]{0:T(512)S(1)} %add_rsqrt_fusion), kind=kOutput, calls=%fused_computation.50 | convolution fusion | flops 1199308800 | bytes 6188544 | tf_op jit(solution)/shard_map/dot_general | solution.py:136
  291.4 10.3 %convolution_convert_fusion = bf16[384,2560]{1,0:T(8,128)(2,1)} fusion(bf16[2560,1824]{1,0:T(8,128)(2,1)} %all-gather.2.cloned.1.call-done, f32[384,608]{0,1:T(8,128)} %fusion.34, bf16[384,2560]{1,0:T(8,128)(2,1)S(1)} %get-tuple-element.295, f32[2560]{0:T(1024)S(1)} %convert_element_type.60, f32[384]{0:T(512)S(1)} %add_rsqrt_fusion), kind=kOutput, calls=%fused_computation.41 | convolution fusion | flops 2397069312 | bytes 11431424 | tf_op jit(solution)/shard_map/dot_general | solution.py:139
  301.7 69.0 %reduce-scatter.2.cloned.1.call-done = bf16[24,2560]{1,0:T(8,128)(2,1)} async-done(((bf16[384,2560]{1,0:T(8,128)(2,1)}), bf16[24,2560]{1,0:T(8,128)(2,1)}) %reduce-scatter.2.cloned.1.call-update) | async-done | bytes 122896 | tf_op jit(solution)/shard_map/reduce_scatter | solution.py:145
  (108 shorter events, 21.1 us)
Async XLA Ops:
  7.4 130.0 %copy-start = (bf16[256,2560]{1,0:T(8,128)(2,1)S(1)}, bf16[256,2560]{1,0:T(8,128)(2,1)}, u32[]{:S(2)}) copy-start(bf16[256,2560]{1,0:T(8,128)(2,1)} %param.21) | copy-start | bytes 3932164
  7.4 1.4 copy-start.4
  9.6 16.4 %copy-start.5 = (bf16[384,256]{1,0:T(8,128)(2,1)S(1)}, bf16[384,256]{1,0:T(8,128)(2,1)}, u32[]{:S(2)}) copy-start(bf16[384,256]{1,0:T(8,128)(2,1)} %param.14) | copy-start | bytes 589828
  10.7 71.3 %all-to-all-start = ((bf16[280,16,128]{2,0,1:T(8,128)(2,1)}), bf16[280,16,128]{2,0,1:T(8,128)(2,1)S(1)}, u32[]{:S(2)}, u32[]{:S(2)}) async-start(bf16[280,16,128]{2,0,1:T(8,128)(2,1)} %pad_maximum_fusion), calls=%async_computation | async-start | bytes 2293760 | tf_op jit(solution)/shard_map/all_to_all | solution.py:54
  25.9 257.7 %all-reduce.2.cloned.1.call-start = ((), (), s32[]{:S(2)}) async-start(), calls=%async_computation.2 | async-start | bytes 3932160 | tf_op jit(solution)/shard_map/psum | solution.py:126
  26.1 55.6 %collective-permute-start = (bf16[384,256]{0,1:T(8,128)(2,1)S(1)}, bf16[384,256]{0,1:T(8,128)(2,1)S(1)}, u32[]{:S(2)}, u32[]{:S(2)}) collective-permute-start(bf16[384,256]{0,1:T(8,128)(2,1)S(1)} %copy.25), channel_id=1, source_target_pairs={{0,1},{1,0},{2,3},{3,2},{4,5},{5,4},{6,7},{7,6},{8,9},{9,8},{10,11... | collective-permute-start | bytes 589832 | tf_op jit(solution)/shard_map/ppermute | solution.py:63
  83.8 6.0 %copy-start.2 = (f32[4,384,128]{2,1,0:T(8,128)S(1)}, f32[4,384,128]{2,1,0:T(8,128)}, u32[]{:S(2)}) copy-start(f32[4,384,128]{2,1,0:T(8,128)} %get-tuple-element.388) | copy-start | bytes 2359300 | tf_op jit(solution)/shard_map/while
  87.0 2.8 copy-start.1
  93.7 6.0 %copy-start.2 = (f32[4,384,128]{2,1,0:T(8,128)S(1)}, f32[4,384,128]{2,1,0:T(8,128)}, u32[]{:S(2)}) copy-start(f32[4,384,128]{2,1,0:T(8,128)} %get-tuple-element.388) | copy-start | bytes 2359300 | tf_op jit(solution)/shard_map/while
  96.9 2.8 copy-start.1
  103.6 6.0 %copy-start.2 = (f32[4,384,128]{2,1,0:T(8,128)S(1)}, f32[4,384,128]{2,1,0:T(8,128)}, u32[]{:S(2)}) copy-start(f32[4,384,128]{2,1,0:T(8,128)} %get-tuple-element.388) | copy-start | bytes 2359300 | tf_op jit(solution)/shard_map/while
  106.9 2.8 copy-start.1
  113.6 6.0 %copy-start.2 = (f32[4,384,128]{2,1,0:T(8,128)S(1)}, f32[4,384,128]{2,1,0:T(8,128)}, u32[]{:S(2)}) copy-start(f32[4,384,128]{2,1,0:T(8,128)} %get-tuple-element.388) | copy-start | bytes 2359300 | tf_op jit(solution)/shard_map/while
  116.8 2.8 copy-start.1
  121.9 0.9 copy-start.3
  125.2 12.1 %collective-permute-start.2 = (f32[2,384,128]{1,2,0:T(8,128)S(1)}, f32[2,384,128]{1,2,0:T(8,128)S(1)}, u32[]{:S(2)}, u32[]{:S(2)}) collective-permute-start(f32[2,384,128]{1,2,0:T(8,128)S(1)} %slice.59), channel_id=1, source_target_pairs={{0,1},{1,0},{2,3},{3,2},{4,5},{5,4},{6,7},{7,6},{8,9},{9,8},{10,11... | collective-permute-start | bytes 1179656 | tf_op jit(solution)/shard_map/ppermute | solution.py:112
  127.5 9.8 %collective-permute-start.3 = (f32[2,384]{1,0:T(2,128)S(1)}, f32[2,384]{1,0:T(2,128)S(1)}, u32[]{:S(2)}, u32[]{:S(2)}) collective-permute-start(f32[2,384]{1,0:T(2,128)S(1)} %slice.61), channel_id=1, source_target_pairs={{0,1},{1,0},{2,3},{3,2},{4,5},{5,4},{6,7},{7,6},{8,9},{9,8},{10,11... | collective-permute-start | bytes 9224 | tf_op jit(solution)/shard_map/ppermute | solution.py:112
  131.1 6.2 %collective-permute-start.1 = (f32[2,384]{1,0:T(2,128)S(1)}, f32[2,384]{1,0:T(2,128)S(1)}, u32[]{:S(2)}, u32[]{:S(2)}) collective-permute-start(f32[2,384]{1,0:T(2,128)S(1)} %slice.58), channel_id=1, source_target_pairs={{0,1},{1,0},{2,3},{3,2},{4,5},{5,4},{6,7},{7,6},{8,9},{9,8},{10,11... | collective-permute-start | bytes 9224 | tf_op jit(solution)/shard_map/ppermute | solution.py:112
  137.4 2.2 copy-start.6
  137.4 2.2 copy-start.7
  137.4 2.2 copy-start.8
  139.5 1.3 copy-start.11
  139.5 147.1 %all-gather.2.cloned.1.call-start = ((), (), s32[]{:S(2)}) async-start(), calls=%async_computation.3 | async-start | bytes 10137600 | tf_op jit(solution)/shard_map/all_gather | solution.py:133
  140.6 230.1 %reduce-scatter.2.cloned.1.call-start = ((), (), s32[]{:S(2)}) async-start(), calls=%async_computation.4 | async-start | bytes 2088960 | tf_op jit(solution)/shard_map/reduce_scatter | solution.py:145
  (5 other events, 4.3 us)
Sparse Core Ops, SparseCore 0:
  139.7 143.9 all-reduce.1
  301.8 68.8 reduce-scatter.1
Sparse Core Ops, SparseCore 1:
  143.7 72.1 all-gather.1

commit v3 on v2

v3 whole, which is shorter than its diff:
```python
import jax
import jax.numpy as jnp
from jax import lax
from jax.sharding import PartitionSpec as P

H = 32
KVH = 8
HD = 128


norm_eps = 1e-06


def shards(
    queries,
    new_keys,
    new_values,
    cache_keys,
    cache_values,
    cache_len,
    residual,
    out_weight,
    norm_gain,
    gate_weight,
    up_weight,
    down_weight,
):
    n_mlp = lax.axis_size("mlp")
    heads_dev = H // n_mlp
    group_size = H // KVH
    copies = n_mlp // KVH
    assert copies == 2 and heads_dev * copies == group_size
    query_rows = queries.shape[0]
    rows_dev = new_keys.shape[0]
    cache_dev = cache_keys.shape[1]
    cache_half = cache_dev // copies
    new_half = rows_dev // copies
    my_index = lax.axis_index("mlp")
    my_half = my_index % copies

    def to_slots(rows_block, half_rows):
        spread = rows_block.reshape(copies, half_rows, KVH, HD).transpose(1, 2, 0, 3)
        return spread.reshape(half_rows, KVH * copies, HD)

    send = jnp.concatenate(
        [
            to_slots(cache_keys[0], cache_half),
            to_slots(cache_values[0], cache_half),
            to_slots(new_keys, new_half),
            to_slots(new_values, new_half),
        ],
        axis=0,
    )
    arrived = lax.all_to_all(send, "mlp", split_axis=1, concat_axis=0, tiled=True)
    per_src = 2 * cache_half + 2 * new_half
    arrived = arrived.reshape(n_mlp, per_src, HD)
    keys_old = arrived[:, :cache_half].reshape(n_mlp * cache_half, HD)
    values_old = arrived[:, cache_half : 2 * cache_half].reshape(n_mlp * cache_half, HD)
    keys_new = arrived[:, 2 * cache_half : 2 * cache_half + new_half].reshape(n_mlp * new_half, HD)
    values_new = arrived[:, 2 * cache_half + new_half :].reshape(n_mlp * new_half, HD)

    pair = [(d, d ^ 1) for d in range(n_mlp)]
    partner_q = lax.ppermute(queries, "mlp", pair)
    score_scale = HD ** (-0.5)
    chunk_spans = [(0, 16), (16, rows_dev - 16)] if rows_dev > 16 else [(0, rows_dev)]
    n_chunks = len(chunk_spans)

    def chunk_of(rows, c):
        first, size = chunk_spans[c]
        split = rows.reshape((n_mlp, rows_dev) + rows.shape[1:])[:, first : first + size]
        return split.reshape((n_mlp * size,) + rows.shape[1:])

    def absorb(grouped, running, key_part, value_part, allowed):
        row_max, row_sum, weighted = running
        scores = (
            jnp.einsum("tqd,kd->qtk", grouped, key_part, preferred_element_type=jnp.float32)
            * score_scale
        )
        scores = jnp.where(allowed, scores, -jnp.inf)
        new_max = jnp.maximum(row_max, jnp.max(scores, axis=-1))
        shrink = jnp.exp(row_max - new_max)
        weights = jnp.exp(scores - new_max[..., None])
        row_sum = row_sum * shrink + jnp.sum(weights, axis=-1)
        weighted = weighted * shrink[..., None] + jnp.einsum(
            "qtk,kd->qtd",
            weights.astype(jnp.bfloat16),
            value_part,
            preferred_element_type=jnp.float32,
        )
        return (new_max, row_sum, weighted)

    length = cache_len[0]
    cache_count = n_mlp * cache_half
    key_block = min(512, cache_count)

    def cached_positions(idx):
        return (idx // cache_half) * cache_dev + my_half * cache_half + idx % cache_half

    new_idx = lax.iota(jnp.int32, n_mlp * new_half)
    new_pos = (new_idx // new_half) * rows_dev + my_half * new_half + new_idx % new_half
    token_all = lax.iota(jnp.int32, query_rows)
    units = gate_weight.shape[1]
    weights_full = lax.all_gather(
        jnp.concatenate([gate_weight, up_weight, down_weight], axis=1), "req", axis=0, tiled=True
    )
    gain = norm_gain.astype(jnp.float32)
    outs = []
    for c in range(n_chunks):
        chunk_q = jnp.concatenate([chunk_of(queries, c), chunk_of(partner_q, c)], axis=1)
        chunk_rows = chunk_q.shape[0]
        grouped = chunk_q.reshape(chunk_rows, group_size, HD)
        start_state = (
            jnp.full((group_size, chunk_rows), -jnp.inf, jnp.float32),
            jnp.zeros((group_size, chunk_rows), jnp.float32),
            jnp.zeros((group_size, chunk_rows, HD), jnp.float32),
        )

        def visit(turn_index, running, grouped=grouped):
            offset = turn_index * key_block
            key_part = lax.dynamic_slice_in_dim(keys_old, offset, key_block, 0)
            value_part = lax.dynamic_slice_in_dim(values_old, offset, key_block, 0)
            positions = cached_positions(offset + lax.iota(jnp.int32, key_block))
            return absorb(grouped, running, key_part, value_part, (positions < length)[None, :])

        running = lax.fori_loop(0, cache_count // key_block, visit, start_state)
        causal = new_pos[None, :] <= chunk_of(token_all, c)[:, None]
        row_max, row_sum, weighted = absorb(grouped, running, keys_new, values_new, causal)

        sent = lax.ppermute(
            (weighted[heads_dev:], row_max[heads_dev:], row_sum[heads_dev:]), "mlp", pair
        )
        other_weighted, other_max, other_sum = sent
        mine_max = row_max[:heads_dev]
        top = jnp.maximum(mine_max, other_max)
        scale_a = jnp.exp(mine_max - top)
        scale_b = jnp.exp(other_max - top)
        total = row_sum[:heads_dev] * scale_a + other_sum * scale_b
        mixed = weighted[:heads_dev] * scale_a[..., None] + other_weighted * scale_b[..., None]
        attended = (mixed / total[..., None]).astype(jnp.bfloat16)
        attended = attended.transpose(1, 0, 2).reshape(chunk_rows, heads_dev * HD)
        partial_value = jnp.dot(attended, out_weight, preferred_element_type=jnp.float32)
        head_rows = lax.psum_scatter(
            partial_value.astype(jnp.bfloat16), "mlp", scatter_dimension=0, tiled=True
        ).astype(jnp.float32)
        first, size = chunk_spans[c]
        res_rows = lax.dynamic_slice_in_dim(residual, my_index * rows_dev + first, size, 0)
        stream = (res_rows.astype(jnp.float32) + head_rows).astype(jnp.bfloat16)
        stream_full = stream.astype(jnp.float32)
        factor = lax.rsqrt(jnp.mean(stream_full * stream_full, axis=-1, keepdims=True) + norm_eps)
        normed = (stream_full * factor * gain).astype(jnp.bfloat16)
        normed_all = lax.all_gather(normed, "mlp", axis=0, tiled=True)
        gate_sum = jnp.dot(normed_all, weights_full[:, :units], preferred_element_type=jnp.float32)
        up_sum = jnp.dot(
            normed_all, weights_full[:, units : 2 * units], preferred_element_type=jnp.float32
        )
        hidden = (jax.nn.silu(gate_sum) * up_sum).astype(jnp.bfloat16)
        mlp_part = lax.dot_general(
            hidden,
            weights_full[:, 2 * units :],
            (((1,), (1,)), ((), ())),
            preferred_element_type=jnp.float32,
        )
        mlp_rows = lax.psum_scatter(
            mlp_part.astype(jnp.bfloat16), "mlp", scatter_dimension=0, tiled=True
        ).astype(jnp.float32)
        outs.append((stream_full + mlp_rows).astype(jnp.bfloat16))
    return jnp.concatenate(outs, axis=0)


def solution(mesh):
    in_specs = (
        P("req", "mlp"),
        P(("req", "mlp"), None),
        P(("req", "mlp"), None),
        P("req", "mlp", None),
        P("req", "mlp", None),
        P("req"),
        P("req", None),
        P("mlp", None),
        P(),
        P("req", "mlp"),
        P("req", "mlp"),
        P("req", "mlp"),
    )
    out_specs = P(("req", "mlp"), None)
    return jax.shard_map(shards, mesh=mesh, in_specs=in_specs, out_specs=out_specs, check_vma=False)
```

time: 380 us -> 466 us (1.23)
  blocking collectives: 0 us -> 32.5 us
  waiting for transfers between devices: 267 us -> 293 us
  matrix products: 39.8 us -> 53.4 us
  starting transfers between devices: 27.4 us -> 35.7 us
    psum x1 -> x0, waiting for transfers between devices: 143 us -> none  [shards(): lax.psum(partial_value.astype(jnp.bfloat16), 'mlp').astype(jnp.float32)]
    reduce_scatter x0 -> x2, waiting for transfers between devices: none -> 109 us  [shards(): lax.psum_scatter(partial_value.astype(jnp.bfloat16), 'mlp', scatter_dimen...]
    reduce_scatter x1 -> x2, waiting for transfers between devices: 69 us -> 126 us  [shards(): lax.psum_scatter(mlp_part.astype(jnp.bfloat16), 'mlp', scatter_dimension=...]
    all_gather x0 -> x1, blocking collectives: none -> 32.5 us  [shards(): normed_all = lax.all_gather(normed, 'mlp', axis=0, tiled=True)]
    ppermute x3 -> x6, starting transfers between devices: 8.09 us -> 16.2 us  [shards(): lax.ppermute((weighted[heads_dev:], row_max[heads_dev:], row_sum[heads_de...]
    dot_general x1 -> x2, matrix products: 10.3 us -> 18.2 us  [shards(): lax.dot_general(hidden, weights_full[:, 2 * units:], (((1,), (1,)), ((),...]
    reduce_sum x5 -> x10, other arithmetic: 11.2 us -> 5.59 us  [absorb(): row_sum = row_sum * shrink + jnp.sum(weights, axis=-1)]
    lt x4 -> x8, other arithmetic: 2.65 us -> 7.48 us  [visit(): positions < length]
  transfers between devices with their start and end apart: 8 -> 14, of which waited for: 4 -> 8; matrix products, arithmetic and copies ran while one was open for 1% -> 11% of each run, Pallas kernels for 0% -> 0%
where the time goes in v3:
time: 466 us; the launch traced here: 465 us
  waiting for transfers between devices  293 us (63%)
  matrix products  53.4 us (11%)
  starting transfers between devices  35.7 us (8%)
  blocking collectives  32.5 us (7%)
  other arithmetic  21.1 us (5%)
  between operations  15.2 us (3%)
  local copies, waits for them, and re-layouts  13.7 us (3%)
    reduce_scatter x2, waiting for transfers between devices, shards(): lax.psum_scatter(mlp_part.astype(jnp.bfloat16), 'mlp', scatter_dimension=...  126 us
    reduce_scatter x2, waiting for transfers between devices, shards(): lax.psum_scatter(partial_value.astype(jnp.bfloat16), 'mlp', scatter_dimen...  109 us
    ppermute x1, waiting for transfers between devices, shards(): partner_q = lax.ppermute(queries, 'mlp', pair)  49.4 us
    all_gather x1, blocking collectives, shards(): normed_all = lax.all_gather(normed, 'mlp', axis=0, tiled=True)  32.5 us
    dot_general x2, matrix products, shards(): lax.dot_general(hidden, weights_full[:, 2 * units:], (((1,), (1,)), ((),...  18.2 us
    ppermute x6, starting transfers between devices, shards(): lax.ppermute((weighted[heads_dev:], row_max[heads_dev:], row_sum[heads_de...  16.2 us
    all_to_all x1, starting transfers between devices, shards(): lax.all_to_all(send, 'mlp', split_axis=1, concat_axis=0, tiled=True)  15.2 us
    dot_general x10, matrix products, absorb(): jnp.einsum('qtk,kd->qtd', weights.astype(jnp.bfloat16), value_part, prefe...  13.2 us
  transfers between devices with their start and end apart: 14, of which 8 were waited for; matrix products, arithmetic and copies ran while one was open for 11% of the time, Pallas kernels for 0%

profile of v3, /device:TPU:6, one launch (start us, length us, event | category | flops | bytes accessed | tf_op | source)
XLA Modules:
  0.0 464.7 jit_solution(2003113825369053206)
XLA Ops:
  11.9 15.2 %all-to-all-start = ((bf16[280,16,128]{2,0,1:T(8,128)(2,1)}), bf16[280,16,128]{2,0,1:T(8,128)(2,1)S(1)}, u32[]{:S(2)}, u32[]{:S(2)}) async-start(bf16[280,16,128]{2,0,1:T(8,128)(2,1)} %pad_maximum_fusion), calls=%async_computation | async-start | bytes 2293760 | tf_op jit(solution)/shard_map/all_to_all | solution.py:54
  27.1 3.8 collective-permute-start
  33.5 49.4 %collective-permute-done = bf16[384,256]{1,0:T(8,128)(2,1)S(1)} collective-permute-done((bf16[384,256]{1,0:T(8,128)(2,1)S(1)}, bf16[384,256]{1,0:T(8,128)(2,1)S(1)}, u32[]{:S(2)}, u32[]{:S(2)}) %collective-permute-start) | collective-permute-done | bytes 196640 | tf_op jit(solution)/shard_map/ppermute | solution.py:63
  86.6 26.4 %while.40 = (s32[]{:T(128)}, f32[4,256]{1,0:T(4,128)S(1)}, f32[4,256]{1,0:T(4,128)S(1)}, f32[4,256,128]{2,1,0:T(8,128)}, s32[]{:T(128)}, /*index=5*/s32[]{:T(128...) while((s32[]{:T(128)}, f32[4,256]{1,0:T(4,128)S(1)}, ...), condition=%wide.region_3.4_spmd.clone, body=%wide.region_0.3_spmd.clone.sunk | while | flops 274613248 | bytes 12126475 | solution.py:125
  97.1 1.9 convolution_add_fusion.6
  103.7 1.9 convolution_add_fusion.6
  116.1 2.2 collective-permute-start.2
  118.4 3.6 collective-permute-start.3
  122.0 2.2 collective-permute-start.1
  125.3 2.1 collective-permute-done.1
  129.3 13.6 %while.41 = (s32[]{:T(128)}, f32[4,128]{1,0:T(4,128)S(1)}, f32[4,128]{1,0:T(4,128)S(1)}, f32[4,128,128]{2,1,0:T(8,128)S(1)}, s32[]{:T(128)}, /*index=5*/s32[]{:T...) while((s32[]{:T(128)}, f32[4,128]{1,0:T(4,128)S(1)}, ...), condition=%wide.region_12.13_spmd.clone, body=%wide.region_9.12_spmd.clone.sunk | while | flops 136264192 | bytes 4097235 | solution.py:125
  143.4 2.2 collective-permute-start.6
  145.7 3.6 collective-permute-start.4
  149.6 2.2 collective-permute-start.5
  151.9 5.4 %collective-permute-done.5 = f32[2,128,128]{1,2,0:T(8,128)S(1)} collective-permute-done((f32[2,128,128]{1,2,0:T(8,128)S(1)}, f32[2,128,128]{1,2,0:T(8,128)S(1)}, u32[]{:S(2)}, u32[]{:S(2)}) %collective-permute-start.5) | collective-permute-done | bytes 131104 | tf_op jit(solution)/shard_map/ppermute | solution.py:129
  159.6 40.5 %reduce-scatter.5.cloned.1.call-done = bf16[16,2560]{1,0:T(8,128)(2,1)} async-done(((bf16[256,2560]{1,0:T(8,128)(2,1)}), bf16[16,2560]{1,0:T(8,128)(2,1)}) %reduce-scatter.5.cloned.1.call-update) | async-done | bytes 81936 | tf_op jit(solution)/shard_map/reduce_scatter | solution.py:142
  202.0 68.3 %reduce-scatter.9.cloned.1.call-done = bf16[8,2560]{1,0:T(8,128)(2,1)} async-done(((bf16[128,2560]{1,0:T(8,128)(2,1)}), bf16[8,2560]{1,0:T(8,128)(2,1)}) %reduce-scatter.9.cloned.1.call-update) | async-done | bytes 40976 | tf_op jit(solution)/shard_map/reduce_scatter | solution.py:142
  271.3 32.5 %all_gather.11 = bf16[128,2560]{1,0:T(8,128)(2,1)S(1)} all-gather(bf16[8,2560]{1,0:T(8,128)(2,1)S(1)} %fusion.105), channel_id=1, replica_groups=mesh['req'=32,'mlp'=16] {'mlp'}, dimensions={0}, use_global_device_ids=true | all-gather | bytes 696320 | tf_op jit(solution)/shard_map/all_gather | solution.py:151
  303.9 3.3 fusion.49
  307.2 8.9 %convolution_convert_fusion.2 = bf16[128,2560]{1,0:T(8,128)(2,1)} fusion(bf16[2560,1824]{1,0:T(8,128)(2,1)} %all-gather.5.cloned.1.call-done, bf16[128,2560]{1,0:T(8,128)(2,1)S(1)} %all_gather.11, f32[128,608]{0,1:T(8,128)S(1)} %fusion.49), kind=kOutput, calls=%fused_computation.72 | convolution fusion | flops 797712384 | bytes 8175616 | tf_op jit(solution)/shard_map/dot_general | solution.py:157
  316.4 3.8 fusion.51
  320.2 9.3 %convolution_convert_fusion = bf16[256,2560]{1,0:T(8,128)(2,1)} fusion(bf16[2560,1824]{1,0:T(8,128)(2,1)} %all-gather.5.cloned.1.call-done, bf16[256,2560]{1,0:T(8,128)(2,1)S(1)} %copy-done.15, f32[256,608]{0,1:T(8,128)S(1)} %fusion.51), kind=kOutput, calls=%fused_computation.70 | convolution fusion | flops 1595424768 | bytes 9797632 | tf_op jit(solution)/shard_map/dot_general | solution.py:157
  329.5 55.0 %reduce-scatter.11.cloned.1.call-done = bf16[8,2560]{1,0:T(8,128)(2,1)} async-done(((bf16[128,2560]{1,0:T(8,128)(2,1)}), bf16[8,2560]{1,0:T(8,128)(2,1)}) %reduce-scatter.11.cloned.1.call-update) | async-done | bytes 40976 | tf_op jit(solution)/shard_map/reduce_scatter | solution.py:163
  385.3 70.7 %reduce-scatter.7.cloned.1.call-done = bf16[16,2560]{1,0:T(8,128)(2,1)} async-done(((bf16[256,2560]{1,0:T(8,128)(2,1)}), bf16[16,2560]{1,0:T(8,128)(2,1)}) %reduce-scatter.7.cloned.1.call-update) | async-done | bytes 81936 | tf_op jit(solution)/shard_map/reduce_scatter | solution.py:163
  (192 shorter events, 60.8 us)
Async XLA Ops:
  7.4 120.2 %copy-start = (bf16[256,2560]{1,0:T(8,128)(2,1)S(1)}, bf16[256,2560]{1,0:T(8,128)(2,1)}, u32[]{:S(2)}) copy-start(bf16[256,2560]{1,0:T(8,128)(2,1)} %param.23) | copy-start | bytes 3932164
  10.7 16.4 %copy-start.8 = (bf16[384,256]{1,0:T(8,128)(2,1)S(1)}, bf16[384,256]{1,0:T(8,128)(2,1)}, u32[]{:S(2)}) copy-start(bf16[384,256]{1,0:T(8,128)(2,1)} %param.16) | copy-start | bytes 589828
  11.9 72.4 %all-to-all-start = ((bf16[280,16,128]{2,0,1:T(8,128)(2,1)}), bf16[280,16,128]{2,0,1:T(8,128)(2,1)S(1)}, u32[]{:S(2)}, u32[]{:S(2)}) async-start(bf16[280,16,128]{2,0,1:T(8,128)(2,1)} %pad_maximum_fusion), calls=%async_computation | async-start | bytes 2293760 | tf_op jit(solution)/shard_map/all_to_all | solution.py:54
  27.1 173.1 %reduce-scatter.5.cloned.1.call-start = ((), (), s32[]{:S(2)}) async-start(), calls=%async_computation.5 | async-start | bytes 1392640 | tf_op jit(solution)/shard_map/reduce_scatter | solution.py:142
  27.1 55.7 %collective-permute-start = (bf16[384,256]{1,0:T(8,128)(2,1)S(1)}, bf16[384,256]{1,0:T(8,128)(2,1)S(1)}, u32[]{:S(2)}, u32[]{:S(2)}) collective-permute-start(bf16[384,256]{1,0:T(8,128)(2,1)S(1)} %copy-done.8), channel_id=1, source_target_pairs={{0,1},{1,0},{2,3},{3,2},{4,5},{5,4},{6,7},{7,6},{8,9},{9,8},{10,11... | collective-permute-start | bytes 589832 | tf_op jit(solution)/shard_map/ppermute | solution.py:63
  114.3 9.9 %copy-start.7 = (bf16[128,2,128]{2,1,0:T(2,128)(2,1)S(1)}, bf16[128,2,128]{2,1,0:T(2,128)(2,1)}, u32[]{:S(2)}) copy-start(bf16[128,2,128]{2,1,0:T(2,128)(2,1)} %concatenate.31) | copy-start | bytes 196612
  116.1 11.4 %collective-permute-start.2 = (f32[2,256,128]{1,2,0:T(8,128)S(1)}, f32[2,256,128]{1,2,0:T(8,128)S(1)}, u32[]{:S(2)}, u32[]{:S(2)}) collective-permute-start(f32[2,256,128]{1,2,0:T(8,128)S(1)} %slice.113), channel_id=1, source_target_pairs={{0,1},{1,0},{2,3},{3,2},{4,5},{5,4},{6,7},{7,6},{8,9},{9,8},{10,11... | collective-permute-start | bytes 786440 | tf_op jit(solution)/shard_map/ppermute | solution.py:129
  118.4 7.0 %collective-permute-start.3 = (f32[2,256]{1,0:T(2,128)S(1)}, f32[2,256]{1,0:T(2,128)S(1)}, u32[]{:S(2)}, u32[]{:S(2)}) collective-permute-start(f32[2,256]{1,0:T(2,128)S(1)} %slice.115), channel_id=1, source_target_pairs={{0,1},{1,0},{2,3},{3,2},{4,5},{5,4},{6,7},{7,6},{8,9},{9,8},{10,11... | collective-permute-start | bytes 6152 | tf_op jit(solution)/shard_map/ppermute | solution.py:129
  122.0 5.5 %collective-permute-start.1 = (f32[2,256]{1,0:T(2,128)S(1)}, f32[2,256]{1,0:T(2,128)S(1)}, u32[]{:S(2)}, u32[]{:S(2)}) collective-permute-start(f32[2,256]{1,0:T(2,128)S(1)} %slice.112), channel_id=1, source_target_pairs={{0,1},{1,0},{2,3},{3,2},{4,5},{5,4},{6,7},{7,6},{8,9},{9,8},{10,11... | collective-permute-start | bytes 6152 | tf_op jit(solution)/shard_map/ppermute | solution.py:129
  129.2 141.1 %reduce-scatter.9.cloned.1.call-start = ((), (), s32[]{:S(2)}) async-start(), calls=%async_computation.9 | async-start | bytes 696320 | tf_op jit(solution)/shard_map/reduce_scatter | solution.py:142
  129.2 13.8 %copy-start.5 = (bf16[192,128,1]{1,0,2:T(8,128)(2,1)S(1)}, bf16[192,128,1]{1,0,2:T(8,128)(2,1)}, u32[]{:S(2)}) copy-start(bf16[192,128,1]{1,0,2:T(8,128)(2,1)} %reshape.149) | copy-start | bytes 147460
  129.2 13.8 %copy-start.12 = (pred[128,192]{0,1:T(8,128)(4,1)S(1)}, pred[128,192]{0,1:T(8,128)(4,1)}, u32[]{:S(2)}) copy-start(pred[128,192]{0,1:T(8,128)(4,1)} %broadcast_compare_fusion.1) | copy-start | bytes 73732
  143.4 8.4 %collective-permute-start.6 = (f32[2,128]{1,0:T(2,128)S(1)}, f32[2,128]{1,0:T(2,128)S(1)}, u32[]{:S(2)}, u32[]{:S(2)}) collective-permute-start(f32[2,128]{1,0:T(2,128)S(1)} %slice.102), channel_id=1, source_target_pairs={{0,1},{1,0},{2,3},{3,2},{4,5},{5,4},{6,7},{7,6},{8,9},{9,8},{10,11... | collective-permute-start | bytes 3080 | tf_op jit(solution)/shard_map/ppermute | solution.py:129
  145.7 6.2 %collective-permute-start.4 = (f32[2,128]{1,0:T(2,128)S(1)}, f32[2,128]{1,0:T(2,128)S(1)}, u32[]{:S(2)}, u32[]{:S(2)}) collective-permute-start(f32[2,128]{1,0:T(2,128)S(1)} %slice.99), channel_id=1, source_target_pairs={{0,1},{1,0},{2,3},{3,2},{4,5},{5,4},{6,7},{7,6},{8,9},{9,8},{10,11... | collective-permute-start | bytes 3080 | tf_op jit(solution)/shard_map/ppermute | solution.py:129
  149.3 9.3 %copy-start.9 = (bf16[80,608]{1,0:T(8,128)(2,1)S(1)}, bf16[80,608]{1,0:T(8,128)(2,1)}, u32[]{:S(2)}) copy-start(bf16[80,608]{1,0:T(8,128)(2,1)} %param.25) | copy-start | bytes 291844
  149.3 9.3 %copy-start.10 = (bf16[80,608]{1,0:T(8,128)(2,1)S(1)}, bf16[80,608]{1,0:T(8,128)(2,1)}, u32[]{:S(2)}) copy-start(bf16[80,608]{1,0:T(8,128)(2,1)} %param.26) | copy-start | bytes 291844
  149.3 9.3 %copy-start.11 = (bf16[80,608]{1,0:T(8,128)(2,1)S(1)}, bf16[80,608]{1,0:T(8,128)(2,1)}, u32[]{:S(2)}) copy-start(bf16[80,608]{1,0:T(8,128)(2,1)} %param.27) | copy-start | bytes 291844
  149.5 10.1 %copy-start.14 = (bf16[2560]{0:T(1024)(128)(2,1)S(1)}, bf16[2560]{0:T(1024)(128)(2,1)}, u32[]{:S(2)}) copy-start(bf16[2560]{0:T(1024)(128)(2,1)} %param.24) | copy-start | bytes 15364
  149.6 7.7 %collective-permute-start.5 = (f32[2,128,128]{1,2,0:T(8,128)S(1)}, f32[2,128,128]{1,2,0:T(8,128)S(1)}, u32[]{:S(2)}, u32[]{:S(2)}) collective-permute-start(f32[2,128,128]{1,2,0:T(8,128)S(1)} %slice.123), channel_id=1, source_target_pairs={{0,1},{1,0},{2,3},{3,2},{4,5},{5,4},{6,7},{7,6},{8,9},{9,8},{10,11... | collective-permute-start | bytes 393224 | tf_op jit(solution)/shard_map/ppermute | solution.py:129
  158.6 145.3 %all-gather.5.cloned.1.call-start = ((), (), s32[]{:S(2)}) async-start(), calls=%async_computation.7 | async-start | bytes 10137600 | tf_op jit(solution)/shard_map/all_gather | solution.py:103
  159.6 156.8 %all-gather.3.cloned.1.call-start = ((), (), s32[]{:S(2)}) async-start(), calls=%async_computation.6 | async-start | bytes 1392640 | tf_op jit(solution)/shard_map/all_gather | solution.py:151
  202.0 182.5 %reduce-scatter.11.cloned.1.call-start = ((), (), s32[]{:S(2)}) async-start(), calls=%async_computation.10 | async-start | bytes 696320 | tf_op jit(solution)/shard_map/reduce_scatter | solution.py:163
  316.1 139.9 %reduce-scatter.7.cloned.1.call-start = ((), (), s32[]{:S(2)}) async-start(), calls=%async_computation.8 | async-start | bytes 1392640 | tf_op jit(solution)/shard_map/reduce_scatter | solution.py:163
  316.4 3.8 copy-start.15
  (12 other events, 17.4 us)
Sparse Core Ops, SparseCore 0:
  129.3 70.8 reduce-scatter.4
  202.9 67.3 reduce-scatter.8
  316.2 68.2 reduce-scatter.10
  387.2 68.7 reduce-scatter.6
Sparse Core Ops, SparseCore 1:
  162.7 71.1 all-gather.4
  235.9 72.5 all-gather.2

commit v4 on v2

--- a/solution.py
+++ b/solution.py
@@ -64,50 +64,33 @@
     grouped = jnp.concatenate([queries, partner_q], axis=1).reshape(query_rows, group_size, HD)
     score_scale = HD ** (-0.5)
 
-    def absorb(running, key_part, value_part, allowed):
-        row_max, row_sum, weighted = running
-        scores = (
-            jnp.einsum("tqd,kd->qtk", grouped, key_part, preferred_element_type=jnp.float32)
-            * score_scale
-        )
-        scores = jnp.where(allowed, scores, -jnp.inf)
-        new_max = jnp.maximum(row_max, jnp.max(scores, axis=-1))
-        shrink = jnp.exp(row_max - new_max)
-        weights = jnp.exp(scores - new_max[..., None])
-        row_sum = row_sum * shrink + jnp.sum(weights, axis=-1)
-        weighted = weighted * shrink[..., None] + jnp.einsum(
-            "qtk,kd->qtd",
-            weights.astype(jnp.bfloat16),
-            value_part,
-            preferred_element_type=jnp.float32,
-        )
-        return (new_max, row_sum, weighted)
-
-    start_state = (
-        jnp.full((group_size, query_rows), -jnp.inf, jnp.float32),
-        jnp.zeros((group_size, query_rows), jnp.float32),
-        jnp.zeros((group_size, query_rows, HD), jnp.float32),
-    )
     length = cache_len[0]
     cache_count = n_mlp * cache_half
-    key_block = min(512, cache_count)
-
-    def cached_positions(idx):
-        return (idx // cache_half) * cache_dev + my_half * cache_half + idx % cache_half
-
-    def visit(turn_index, running):
-        offset = turn_index * key_block
-        key_part = lax.dynamic_slice_in_dim(keys_old, offset, key_block, 0)
-        value_part = lax.dynamic_slice_in_dim(values_old, offset, key_block, 0)
-        positions = cached_positions(offset + lax.iota(jnp.int32, key_block))
-        return absorb(running, key_part, value_part, (positions < length)[None, :])
-
-    running = lax.fori_loop(0, cache_count // key_block, visit, start_state)
+    keys_all = jnp.concatenate([keys_old, keys_new], axis=0)
+    values_all = jnp.concatenate([values_old, values_new], axis=0)
+    cached_idx = lax.iota(jnp.int32, cache_count)
+    cached_pos = (cached_idx // cache_half) * cache_dev + my_half * cache_half + cached_idx % cache_half
     new_idx = lax.iota(jnp.int32, n_mlp * new_half)
     new_pos = (new_idx // new_half) * rows_dev + my_half * new_half + new_idx % new_half
     token_ids = lax.iota(jnp.int32, query_rows)
-    causal = new_pos[None, :] <= token_ids[:, None]
-    row_max, row_sum, weighted = absorb(running, keys_new, values_new, causal)
+    allowed = jnp.concatenate(
+        [
+            jnp.broadcast_to((cached_pos < length)[None, :], (query_rows, cache_count)),
+            new_pos[None, :] <= token_ids[:, None],
+        ],
+        axis=1,
+    )
+    scores = (
+        jnp.einsum("tqd,kd->qtk", grouped, keys_all, preferred_element_type=jnp.float32)
+        * score_scale
+    )
+    scores = jnp.where(allowed[None], scores, -jnp.inf)
+    row_max = jnp.max(scores, axis=-1)
+    weights = jnp.exp(scores - row_max[..., None])
+    row_sum = jnp.sum(weights, axis=-1)
+    weighted = jnp.einsum(
+        "qtk,kd->qtd", weights.astype(jnp.bfloat16), values_all, preferred_element_type=jnp.float32
+    )
 
     sent = lax.ppermute(
         (weighted[heads_dev:], row_max[heads_dev:], row_sum[heads_dev:]), "mlp", pair

time: 380 us -> 355 us (0.934)
  matrix products: 39.8 us -> 24.5 us
  local copies, waits for them, and re-layouts: 9.76 us -> 5.65 us
  waiting for transfers between devices: 267 us -> 263 us
    dot_general x10 -> x2, matrix products: 22.6 us -> 7.35 us  [the longest x1 4.03 us: shards(): jnp.einsum('tqd,kd->qtk', grouped, keys_all, preferred_element_type=jnp.f...]
    while x29 -> x0, local copies, waits for them, and re-layouts: 5.11 us -> none
    reduce_sum x5 -> x1, other arithmetic: 11.2 us -> 7.81 us  [shards(): row_sum = jnp.sum(weights, axis=-1)]
  transfers between devices with their start and end apart: 8 -> 8, of which waited for: 4 -> 4; matrix products, arithmetic and copies ran while one was open for 1% -> 4% of each run, Pallas kernels for 0% -> 0%
where the time goes in v4:
time: 355 us; the launch traced here: 354 us
  waiting for transfers between devices  263 us (74%)
  starting transfers between devices  27.4 us (8%)
  matrix products  24.5 us (7%)
  other arithmetic  17.6 us (5%)
  between operations  15.9 us (4%)
  local copies, waits for them, and re-layouts  5.65 us (2%)
    psum x1, waiting for transfers between devices, shards(): lax.psum(partial_value.astype(jnp.bfloat16), 'mlp').astype(jnp.float32)  142 us
    reduce_scatter x1, waiting for transfers between devices, shards(): lax.psum_scatter(mlp_part.astype(jnp.bfloat16), 'mlp', scatter_dimension=...  69 us
    ppermute x1, waiting for transfers between devices, shards(): partner_q = lax.ppermute(queries, 'mlp', pair)  48.9 us
    all_to_all x1, starting transfers between devices, shards(): lax.all_to_all(send, 'mlp', split_axis=1, concat_axis=0, tiled=True)  15.2 us
    dot_general x1, matrix products, shards(): lax.dot_general(hidden, weights_full[:, 2 * units:], (((1,), (1,)), ((),...  10.3 us
    ppermute x3, starting transfers between devices, shards(): lax.ppermute((weighted[heads_dev:], row_max[heads_dev:], row_sum[heads_de...  8.08 us
    reduce_sum x1, other arithmetic, shards(): row_sum = jnp.sum(weights, axis=-1)  7.81 us
  transfers between devices with their start and end apart: 8, of which 4 were waited for; matrix products, arithmetic and copies ran while one was open for 4% of the time, Pallas kernels for 0%

profile of v4, /device:TPU:6, one launch (start us, length us, event | category | flops | bytes accessed | tf_op | source)
XLA Modules:
  0.0 354.1 jit_solution(9728811819291925658)
XLA Ops:
  7.4 1.3 copy.25
  9.2 1.1 pad_maximum_fusion
  10.3 15.2 %all-to-all-start = ((bf16[280,16,128]{2,0,1:T(8,128)(2,1)}), bf16[280,16,128]{2,0,1:T(8,128)(2,1)S(1)}, u32[]{:S(2)}, u32[]{:S(2)}) async-start(bf16[280,16,128]{2,0,1:T(8,128)(2,1)} %pad_maximum_fusion), calls=%async_computation | async-start | bytes 2293760 | tf_op jit(solution)/shard_map/all_to_all | solution.py:54
  25.7 3.8 %collective-permute-start = (bf16[384,256]{0,1:T(8,128)(2,1)S(1)}, bf16[384,256]{0,1:T(8,128)(2,1)}, u32[]{:S(2)}, u32[]{:S(2)}) collective-permute-start(bf16[384,256]{0,1:T(8,128)(2,1)S(1)} %copy.22), channel_id=1, source_target_pairs={{0,1},{1,0},{2,3},{3,2},{4,5},{5,4},{6,7},{7,6},{8,9},{9,8},{10,11... | collective-permute-start | bytes 589832 | tf_op jit(solution)/shard_map/ppermute | solution.py:63
  30.4 2.1 pad_add_fusion
  32.5 48.9 %collective-permute-done = bf16[384,256]{0,1:T(8,128)(2,1)} collective-permute-done((bf16[384,256]{0,1:T(8,128)(2,1)S(1)}, bf16[384,256]{0,1:T(8,128)(2,1)}, u32[]{:S(2)}, u32[]{:S(2)}) %collective-permute-start) | collective-permute-done | bytes 196640 | tf_op jit(solution)/shard_map/ppermute | solution.py:63
  81.4 1.7 pad_maximum_fusion.1
  83.1 1.1 fusion.65
  84.3 4.0 %fusion.2 = (f32[4,384]{1,0:T(4,128)S(1)}, f32[2240,384,4]{1,0,2:T(8,128)S(1)}) fusion(pred[384,2240]{0,1:T(8,128)(4,1)S(1)} %pad_add_fusion, bf16[384,4,128]{0,2,1:T(8,128)(2,1)} %bitcast.74, bf16[192,128]{1,0:T(8,128)(2,1)S(1)} %reshape.106, bf16[2048,128]{1,0:T(8,128)(2,1)} %bitcast.73), kind=kOutput, calls=%fused_computation.4 | convolution fusion | flops 892271104 | bytes 15595520 | tf_op jit(solution)/shard_map/tqd,kd->qtk/dot_general | solution.py:84
  88.4 3.3 fusion.3
  91.7 1.6 copy-done.1
  93.4 2.2 collective-permute-start.2
  95.6 7.8 %fusion = f32[4,384]{1,0:T(4,128)S(1)} fusion(f32[2240,384,4]{1,0,2:T(8,128)} %copy-done.1, f32[4,384]{1,0:T(4,128)S(1)} %get-tuple-element.14, pred[384,2240]{0,1:T(8,128)(4,1)S(1)} %pad_add_fusion), kind=kLoop, calls=%fused_computation.2 | loop fusion | flops 13761024 | bytes 14635008 | tf_op jit(solution)/shard_map/reduce_sum | solution.py:90
  103.4 3.6 %collective-permute-start.3 = (f32[2,384]{1,0:T(2,128)S(1)}, f32[2,384]{1,0:T(2,128)S(1)}, u32[]{:S(2)}, u32[]{:S(2)}) collective-permute-start(f32[2,384]{1,0:T(2,128)S(1)} %slice.61), channel_id=1, source_target_pairs={{0,1},{1,0},{2,3},{3,2},{4,5},{5,4},{6,7},{7,6},{8,9},{9,8},{10,11... | collective-permute-start | bytes 9224 | tf_op jit(solution)/shard_map/ppermute | solution.py:95
  107.1 2.2 collective-permute-start.1
  109.3 3.2 collective-permute-done.1
  112.7 2.1 convolution_convert_fusion.1
  114.9 0.9 concatenate.23
  116.1 141.9 %all-reduce.2.cloned.1.call-done = bf16[384,2560]{1,0:T(8,128)(2,1)} async-done(((bf16[384,2560]{1,0:T(8,128)(2,1)}), bf16[384,2560]{1,0:T(8,128)(2,1)}) %all-reduce.2.cloned.1.call-update) | async-done | bytes 1966096 | tf_op jit(solution)/shard_map/psum | solution.py:109
  258.0 3.0 fusion.6
  261.1 4.8 %fusion.12 = f32[384,608]{0,1:T(8,128)} fusion(bf16[2560,1824]{1,0:T(8,128)(2,1)} %all-gather.2.cloned.1.call-done, bf16[384,2560]{1,0:T(8,128)(2,1)S(1)} %get-tuple-element.6, f32[2560]{0:T(1024)S(1)} %convert_element_type.50, f32[384]{0:T(512)S(1)} %add_rsqrt_fusion), kind=kOutput, calls=%fused_computation.19 | convolution fusion | flops 1199308800 | bytes 6188544 | tf_op jit(solution)/shard_map/dot_general | solution.py:119
  265.8 10.3 %convolution_convert_fusion = bf16[384,2560]{1,0:T(8,128)(2,1)} fusion(bf16[2560,1824]{1,0:T(8,128)(2,1)} %all-gather.2.cloned.1.call-done, f32[384,608]{0,1:T(8,128)} %fusion.12, bf16[384,2560]{1,0:T(8,128)(2,1)S(1)} %get-tuple-element.6, f32[2560]{0:T(1024)S(1)} %convert_element_type.50, f32[384]{0:T(512)S(1)} %add_rsqrt_fusion), kind=kOutput, calls=%fused_computation.9 | convolution fusion | flops 2397069312 | bytes 11431424 | tf_op jit(solution)/shard_map/dot_general | solution.py:122
  276.1 69.0 %reduce-scatter.2.cloned.1.call-done = bf16[24,2560]{1,0:T(8,128)(2,1)} async-done(((bf16[384,2560]{1,0:T(8,128)(2,1)}), bf16[24,2560]{1,0:T(8,128)(2,1)}) %reduce-scatter.2.cloned.1.call-update) | async-done | bytes 122896 | tf_op jit(solution)/shard_map/reduce_scatter | solution.py:128
  345.1 1.6 add_convert_fusion.1
  (55 shorter events, 1.3 us)
Async XLA Ops:
  7.4 105.3 %copy-start = (bf16[256,2560]{1,0:T(8,128)(2,1)S(1)}, bf16[256,2560]{1,0:T(8,128)(2,1)}, u32[]{:S(2)}) copy-start(bf16[256,2560]{1,0:T(8,128)(2,1)} %param.19) | copy-start | bytes 3932164
  7.4 1.4 copy-start.2
  7.4 1.7 copy-start.8
  7.4 1.7 copy-start.9
  8.9 16.6 %copy-start.4 = (bf16[384,256]{1,0:T(8,128)(2,1)S(1)}, bf16[384,256]{1,0:T(8,128)(2,1)}, u32[]{:S(2)}) copy-start(bf16[384,256]{1,0:T(8,128)(2,1)} %param.12) | copy-start | bytes 589828
  10.3 72.8 %all-to-all-start = ((bf16[280,16,128]{2,0,1:T(8,128)(2,1)}), bf16[280,16,128]{2,0,1:T(8,128)(2,1)S(1)}, u32[]{:S(2)}, u32[]{:S(2)}) async-start(bf16[280,16,128]{2,0,1:T(8,128)(2,1)} %pad_maximum_fusion), calls=%async_computation | async-start | bytes 2293760 | tf_op jit(solution)/shard_map/all_to_all | solution.py:54
  25.5 232.5 %all-reduce.2.cloned.1.call-start = ((), (), s32[]{:S(2)}) async-start(), calls=%async_computation.2 | async-start | bytes 3932160 | tf_op jit(solution)/shard_map/psum | solution.py:109
  25.7 55.7 %collective-permute-start = (bf16[384,256]{0,1:T(8,128)(2,1)S(1)}, bf16[384,256]{0,1:T(8,128)(2,1)}, u32[]{:S(2)}, u32[]{:S(2)}) collective-permute-start(bf16[384,256]{0,1:T(8,128)(2,1)S(1)} %copy.22), channel_id=1, source_target_pairs={{0,1},{1,0},{2,3},{3,2},{4,5},{5,4},{6,7},{7,6},{8,9},{9,8},{10,11... | collective-permute-start | bytes 589832 | tf_op jit(solution)/shard_map/ppermute | solution.py:63
  84.3 4.1 %copy-start.3 = (bf16[16,128,128]{2,1,0:T(8,128)(2,1)S(1)}, bf16[16,128,128]{2,1,0:T(8,128)(2,1)}, u32[]{:S(2)}) copy-start(bf16[16,128,128]{2,1,0:T(8,128)(2,1)} %get-tuple-element.10) | copy-start | bytes 1572868
  88.4 5.0 %copy-start.1 = (f32[2240,384,4]{1,0,2:T(8,128)}, f32[2240,384,4]{1,0,2:T(8,128)S(1)}, u32[]{:S(2)}) copy-start(f32[2240,384,4]{1,0,2:T(8,128)S(1)} %get-tuple-element.15) | copy-start | bytes 41287684
  93.4 19.2 %collective-permute-start.2 = (f32[2,384,128]{1,2,0:T(8,128)S(1)}, f32[2,384,128]{1,2,0:T(8,128)S(1)}, u32[]{:S(2)}, u32[]{:S(2)}) collective-permute-start(f32[2,384,128]{1,2,0:T(8,128)S(1)} %slice.59), channel_id=1, source_target_pairs={{0,1},{1,0},{2,3},{3,2},{4,5},{5,4},{6,7},{7,6},{8,9},{9,8},{10,11... | collective-permute-start | bytes 1179656 | tf_op jit(solution)/shard_map/ppermute | solution.py:95
  103.4 5.9 %collective-permute-start.3 = (f32[2,384]{1,0:T(2,128)S(1)}, f32[2,384]{1,0:T(2,128)S(1)}, u32[]{:S(2)}, u32[]{:S(2)}) collective-permute-start(f32[2,384]{1,0:T(2,128)S(1)} %slice.61), channel_id=1, source_target_pairs={{0,1},{1,0},{2,3},{3,2},{4,5},{5,4},{6,7},{7,6},{8,9},{9,8},{10,11... | collective-permute-start | bytes 9224 | tf_op jit(solution)/shard_map/ppermute | solution.py:95
  107.1 5.5 %collective-permute-start.1 = (f32[2,384]{1,0:T(2,128)S(1)}, f32[2,384]{1,0:T(2,128)S(1)}, u32[]{:S(2)}, u32[]{:S(2)}) collective-permute-start(f32[2,384]{1,0:T(2,128)S(1)} %slice.58), channel_id=1, source_target_pairs={{0,1},{1,0},{2,3},{3,2},{4,5},{5,4},{6,7},{7,6},{8,9},{9,8},{10,11... | collective-permute-start | bytes 9224 | tf_op jit(solution)/shard_map/ppermute | solution.py:95
  112.6 2.3 copy-start.5
  112.6 2.3 copy-start.6
  112.6 2.3 copy-start.7
  112.7 3.4 copy-start.10
  114.8 146.2 %all-gather.2.cloned.1.call-start = ((), (), s32[]{:S(2)}) async-start(), calls=%async_computation.3 | async-start | bytes 10137600 | tf_op jit(solution)/shard_map/all_gather | solution.py:116
  115.9 229.2 %reduce-scatter.2.cloned.1.call-start = ((), (), s32[]{:S(2)}) async-start(), calls=%async_computation.4 | async-start | bytes 2088960 | tf_op jit(solution)/shard_map/reduce_scatter | solution.py:128
Sparse Core Ops, SparseCore 0:
  114.9 143.0 all-reduce.1
  276.3 68.7 reduce-scatter.1
Sparse Core Ops, SparseCore 1:
  119.0 71.2 all-gather.1

commit v5 on v4

--- a/solution.py
+++ b/solution.py
@@ -92,10 +92,21 @@
         "qtk,kd->qtd", weights.astype(jnp.bfloat16), values_all, preferred_element_type=jnp.float32
     )
 
-    sent = lax.ppermute(
-        (weighted[heads_dev:], row_max[heads_dev:], row_sum[heads_dev:]), "mlp", pair
+    stats_rows = 2 * query_rows // HD
+    packed = jnp.concatenate(
+        [
+            weighted[heads_dev:],
+            jnp.stack([row_max[heads_dev:], row_sum[heads_dev:]], axis=1).reshape(
+                heads_dev, stats_rows, HD
+            ),
+        ],
+        axis=1,
     )
-    other_weighted, other_max, other_sum = sent
+    sent = lax.ppermute(packed, "mlp", pair)
+    other_weighted = sent[:, :query_rows]
+    other_stats = sent[:, query_rows:].reshape(heads_dev, 2, query_rows)
+    other_max = other_stats[:, 0]
+    other_sum = other_stats[:, 1]
     mine_max = row_max[:heads_dev]
     top = jnp.maximum(mine_max, other_max)
     scale_a = jnp.exp(mine_max - top)

time: 355 us -> 365 us (1.028)
  matrix products: 24.5 us -> 32.3 us
  waiting for transfers between devices: 263 us -> 270 us
  starting transfers between devices: 27.4 us -> 21.6 us
    ppermute x3 -> x1, waiting for transfers between devices: 3.24 us -> 9.89 us  [shards(): sent = lax.ppermute(packed, 'mlp', pair)]
    ppermute x3 -> x1, starting transfers between devices: 8.08 us -> 2.26 us  [shards(): sent = lax.ppermute(packed, 'mlp', pair)]
    dot_general x1, matrix products: 4.03 us -> 8.37 us  [shards(): jnp.einsum('tqd,kd->qtk', grouped, keys_all, preferred_element_type=jnp.f...]
  transfers between devices with their start and end apart: 8 -> 6, of which waited for: 4 -> 4; matrix products, arithmetic and copies ran while one was open for 4% -> 2% of each run, Pallas kernels for 0% -> 0%
where the time goes in v5:
time: 365 us; the launch traced here: 364 us
  waiting for transfers between devices  270 us (74%)
  matrix products  32.3 us (9%)
  starting transfers between devices  21.6 us (6%)
  other arithmetic  19 us (5%)
  between operations  15.9 us (4%)
  local copies, waits for them, and re-layouts  5.14 us (1%)
    psum x1, waiting for transfers between devices, shards(): lax.psum(partial_value.astype(jnp.bfloat16), 'mlp').astype(jnp.float32)  143 us
    reduce_scatter x1, waiting for transfers between devices, shards(): lax.psum_scatter(mlp_part.astype(jnp.bfloat16), 'mlp', scatter_dimension=...  68.9 us
    ppermute x1, waiting for transfers between devices, shards(): partner_q = lax.ppermute(queries, 'mlp', pair)  48.9 us
    all_to_all x1, starting transfers between devices, shards(): lax.all_to_all(send, 'mlp', split_axis=1, concat_axis=0, tiled=True)  15.2 us
    dot_general x1, matrix products, shards(): lax.dot_general(hidden, weights_full[:, 2 * units:], (((1,), (1,)), ((),...  10.3 us
    ppermute x1, waiting for transfers between devices, shards(): sent = lax.ppermute(packed, 'mlp', pair)  9.89 us
    dot_general x1, matrix products, shards(): jnp.einsum('tqd,kd->qtk', grouped, keys_all, preferred_element_type=jnp.f...  8.37 us
    reduce_sum x1, other arithmetic, shards(): row_sum = jnp.sum(weights, axis=-1)  7.89 us
  transfers between devices with their start and end apart: 6, of which 4 were waited for; matrix products, arithmetic and copies ran while one was open for 2% of the time, Pallas kernels for 0%

profile of v5, /device:TPU:6, one launch (start us, length us, event | category | flops | bytes accessed | tf_op | source)
XLA Modules:
  0.0 364.4 jit_solution(1221951235959626254)
XLA Ops:
  7.4 1.3 copy.33
  9.2 1.1 pad_maximum_fusion
  10.3 15.2 %all-to-all-start = ((bf16[280,16,128]{2,0,1:T(8,128)(2,1)}), bf16[280,16,128]{2,0,1:T(8,128)(2,1)S(1)}, u32[]{:S(2)}, u32[]{:S(2)}) async-start(bf16[280,16,128]{2,0,1:T(8,128)(2,1)} %pad_maximum_fusion), calls=%async_computation | async-start | bytes 2293760 | tf_op jit(solution)/shard_map/all_to_all | solution.py:54
  25.7 3.8 %collective-permute-start = (bf16[384,256]{0,1:T(8,128)(2,1)S(1)}, bf16[384,256]{0,1:T(8,128)(2,1)}, u32[]{:S(2)}, u32[]{:S(2)}) collective-permute-start(bf16[384,256]{0,1:T(8,128)(2,1)S(1)} %copy.25), channel_id=1, source_target_pairs={{0,1},{1,0},{2,3},{3,2},{4,5},{5,4},{6,7},{7,6},{8,9},{9,8},{10,11... | collective-permute-start | bytes 589832 | tf_op jit(solution)/shard_map/ppermute | solution.py:63
  30.4 2.1 pad_add_fusion
  32.5 48.9 %collective-permute-done = bf16[384,256]{0,1:T(8,128)(2,1)} collective-permute-done((bf16[384,256]{0,1:T(8,128)(2,1)S(1)}, bf16[384,256]{0,1:T(8,128)(2,1)}, u32[]{:S(2)}, u32[]{:S(2)}) %collective-permute-start) | collective-permute-done | bytes 196640 | tf_op jit(solution)/shard_map/ppermute | solution.py:63
  81.4 1.7 pad_maximum_fusion.2
  83.1 1.1 fusion.66
  84.3 8.4 %fusion.2 = (f32[4,384]{1,0:T(4,128)S(1)}, f32[2240,384,4]{1,0,2:T(8,128)}) fusion(pred[384,2240]{0,1:T(8,128)(4,1)S(1)} %pad_add_fusion, bf16[384,4,128]{0,2,1:T(8,128)(2,1)} %bitcast.90, bf16[192,128]{1,0:T(8,128)(2,1)S(1)} %reshape.112, bf16[2048,128]{1,0:T(8,128)(2,1)} %bitcast.89), kind=kOutput, calls=%fused_computation.4 | convolution fusion | flops 892271104 | bytes 15595520 | tf_op jit(solution)/shard_map/tqd,kd->qtk/dot_general | solution.py:84
  92.7 7.9 %fusion = f32[4,384]{1,0:T(4,128)S(1)} fusion(f32[2240,384,4]{1,0,2:T(8,128)} %get-tuple-element.17, f32[4,384]{1,0:T(4,128)S(1)} %get-tuple-element.16, pred[384,2240]{0,1:T(8,128)(4,1)S(1)} %pad_add_fusion), kind=kLoop, calls=%fused_computation.2 | loop fusion | flops 13761024 | bytes 14635008 | tf_op jit(solution)/shard_map/reduce_sum | solution.py:90
  100.6 6.8 %fusion.3 = f32[4,384,128]{2,1,0:T(8,128)S(1)} fusion(f32[2240,384,4]{1,0,2:T(8,128)} %get-tuple-element.17, f32[4,384]{1,0:T(4,128)S(1)} %get-tuple-element.16, pred[384,2240]{0,1:T(8,128)(4,1)S(1)} %pad_add_fusion, bf16[192,128]{1,0:T(8,128)(2,1)S(1)} %reshape.115, bf16[2048,128]{1,0:T(8,128)(2,1)S(1)} %bitcast.88), kind=kOutput, calls=%fused_computation.5 | convolution fusion | flops 895713280 | bytes 15988736 | tf_op jit(solution)/shard_map/qtk,kd->qtd/dot_general | solution.py:91
  107.5 0.9 copy-done.1
  108.5 2.3 collective-permute-start.1
  110.7 9.9 %collective-permute-done.1 = f32[2,390,128]{2,1,0:T(8,128)S(1)} collective-permute-done((f32[2,390,128]{2,1,0:T(8,128)S(1)}, f32[2,390,128]{2,1,0:T(8,128)S(1)}, u32[]{:S(2)}, u32[]{:S(2)}) %collective-permute-start.1) | collective-permute-done | bytes 399392 | tf_op jit(solution)/shard_map/ppermute | solution.py:105
  120.7 1.4 fusion.39
  122.3 2.1 convolution_convert_fusion.1
  124.5 0.9 concatenate.27
  125.4 0.2 reduce-scatter.2.cloned.1.call-start
  125.7 142.7 %all-reduce.2.cloned.1.call-done = bf16[384,2560]{1,0:T(8,128)(2,1)} async-done(((bf16[384,2560]{1,0:T(8,128)(2,1)}), bf16[384,2560]{1,0:T(8,128)(2,1)}) %all-reduce.2.cloned.1.call-update) | async-done | bytes 1966096 | tf_op jit(solution)/shard_map/psum | solution.py:120
  268.4 3.0 fusion.6
  271.4 4.8 %fusion.12 = f32[384,608]{0,1:T(8,128)} fusion(bf16[2560,1824]{1,0:T(8,128)(2,1)} %all-gather.2.cloned.1.call-done, bf16[384,2560]{1,0:T(8,128)(2,1)S(1)} %get-tuple-element.6, f32[2560]{0:T(1024)S(1)} %convert_element_type.50, f32[384]{0:T(512)S(1)} %add_rsqrt_fusion), kind=kOutput, calls=%fused_computation.19 | convolution fusion | flops 1199308800 | bytes 6188544 | tf_op jit(solution)/shard_map/dot_general | solution.py:130
  276.2 10.3 %convolution_convert_fusion = bf16[384,2560]{1,0:T(8,128)(2,1)} fusion(bf16[2560,1824]{1,0:T(8,128)(2,1)} %all-gather.2.cloned.1.call-done, f32[384,608]{0,1:T(8,128)} %fusion.12, bf16[384,2560]{1,0:T(8,128)(2,1)S(1)} %get-tuple-element.6, f32[2560]{0:T(1024)S(1)} %convert_element_type.50, f32[384]{0:T(512)S(1)} %add_rsqrt_fusion), kind=kOutput, calls=%fused_computation.9 | convolution fusion | flops 2397069312 | bytes 11431424 | tf_op jit(solution)/shard_map/dot_general | solution.py:133
  286.5 68.9 %reduce-scatter.2.cloned.1.call-done = bf16[24,2560]{1,0:T(8,128)(2,1)} async-done(((bf16[384,2560]{1,0:T(8,128)(2,1)}), bf16[24,2560]{1,0:T(8,128)(2,1)}) %reduce-scatter.2.cloned.1.call-update) | async-done | bytes 122896 | tf_op jit(solution)/shard_map/reduce_scatter | solution.py:139
  355.4 1.6 add_convert_fusion.1
  (58 shorter events, 1.3 us)
Async XLA Ops:
  7.4 114.9 %copy-start = (bf16[256,2560]{1,0:T(8,128)(2,1)S(1)}, bf16[256,2560]{1,0:T(8,128)(2,1)}, u32[]{:S(2)}) copy-start(bf16[256,2560]{1,0:T(8,128)(2,1)} %param.19) | copy-start | bytes 3932164
  7.4 1.4 copy-start.2
  7.4 1.7 copy-start.8
  7.4 1.7 copy-start.9
  8.9 16.6 %copy-start.4 = (bf16[384,256]{1,0:T(8,128)(2,1)S(1)}, bf16[384,256]{1,0:T(8,128)(2,1)}, u32[]{:S(2)}) copy-start(bf16[384,256]{1,0:T(8,128)(2,1)} %param.12) | copy-start | bytes 589828
  10.3 72.8 %all-to-all-start = ((bf16[280,16,128]{2,0,1:T(8,128)(2,1)}), bf16[280,16,128]{2,0,1:T(8,128)(2,1)S(1)}, u32[]{:S(2)}, u32[]{:S(2)}) async-start(bf16[280,16,128]{2,0,1:T(8,128)(2,1)} %pad_maximum_fusion), calls=%async_computation | async-start | bytes 2293760 | tf_op jit(solution)/shard_map/all_to_all | solution.py:54
  25.5 242.9 %all-reduce.2.cloned.1.call-start = ((), (), s32[]{:S(2)}) async-start(), calls=%async_computation.2 | async-start | bytes 3932160 | tf_op jit(solution)/shard_map/psum | solution.py:120
  25.7 55.7 %collective-permute-start = (bf16[384,256]{0,1:T(8,128)(2,1)S(1)}, bf16[384,256]{0,1:T(8,128)(2,1)}, u32[]{:S(2)}, u32[]{:S(2)}) collective-permute-start(bf16[384,256]{0,1:T(8,128)(2,1)S(1)} %copy.25), channel_id=1, source_target_pairs={{0,1},{1,0},{2,3},{3,2},{4,5},{5,4},{6,7},{7,6},{8,9},{9,8},{10,11... | collective-permute-start | bytes 589832 | tf_op jit(solution)/shard_map/ppermute | solution.py:63
  92.7 7.9 %copy-start.3 = (bf16[16,128,128]{2,1,0:T(8,128)(2,1)S(1)}, bf16[16,128,128]{2,1,0:T(8,128)(2,1)}, u32[]{:S(2)}) copy-start(bf16[16,128,128]{2,1,0:T(8,128)(2,1)} %get-tuple-element.10) | copy-start | bytes 1572868
  107.4 0.9 copy-start.1
  108.5 12.2 %collective-permute-start.1 = (f32[2,390,128]{2,1,0:T(8,128)S(1)}, f32[2,390,128]{2,1,0:T(8,128)S(1)}, u32[]{:S(2)}, u32[]{:S(2)}) collective-permute-start(f32[2,390,128]{2,1,0:T(8,128)S(1)} %pad_maximum_fusion.1), channel_id=1, source_target_pairs={{0,1},{1,0},{2,3},{3,2},{4,5},{5,4},{6,7},{7,6},{8,9},{9,8},{10,11... | collective-permute-start | bytes 1198088 | tf_op jit(solution)/shard_map/ppermute | solution.py:105
  122.0 2.4 copy-start.5
  122.1 2.4 copy-start.6
  122.1 2.4 copy-start.7
  122.3 3.4 copy-start.10
  124.4 147.0 %all-gather.2.cloned.1.call-start = ((), (), s32[]{:S(2)}) async-start(), calls=%async_computation.3 | async-start | bytes 10137600 | tf_op jit(solution)/shard_map/all_gather | solution.py:127
  125.4 230.0 %reduce-scatter.2.cloned.1.call-start = ((), (), s32[]{:S(2)}) async-start(), calls=%async_computation.4 | async-start | bytes 2088960 | tf_op jit(solution)/shard_map/reduce_scatter | solution.py:139
Sparse Core Ops, SparseCore 0:
  124.5 143.8 all-reduce.1
  286.6 68.7 reduce-scatter.1
Sparse Core Ops, SparseCore 1:
  128.5 72.1 all-gather.1

commit v6 on v4

--- a/solution.py
+++ b/solution.py
@@ -113,15 +113,25 @@
     normed = (stream_full * factor * norm_gain.astype(jnp.float32)).astype(jnp.bfloat16)
     stream_rows = lax.dynamic_slice_in_dim(stream, row_start, rows_dev, 0)
     units = gate_weight.shape[1]
+    width = -(-units // 128) * 128
+
+    def padded(block):
+        return jnp.pad(block, ((0, 0), (0, width - units)))
+
     weights_full = lax.all_gather(
-        jnp.concatenate([gate_weight, up_weight, down_weight], axis=1), "req", axis=0, tiled=True
+        jnp.concatenate([padded(gate_weight), padded(up_weight), padded(down_weight)], axis=1),
+        "req",
+        axis=0,
+        tiled=True,
     )
     gate_sum = jnp.dot(normed, weights_full[:, :units], preferred_element_type=jnp.float32)
-    up_sum = jnp.dot(normed, weights_full[:, units : 2 * units], preferred_element_type=jnp.float32)
+    up_sum = jnp.dot(
+        normed, weights_full[:, width : width + units], preferred_element_type=jnp.float32
+    )
     hidden = (jax.nn.silu(gate_sum) * up_sum).astype(jnp.bfloat16)
     mlp_part = lax.dot_general(
         hidden,
-        weights_full[:, 2 * units :],
+        weights_full[:, 2 * width : 2 * width + units],
         (((1,), (1,)), ((), ())),
         preferred_element_type=jnp.float32,
     )

time: 355 us -> 352 us (level)
  no operation moved by 1% of the time
where the time goes in v6:
time: 352 us
  waiting for transfers between devices  263 us (75%)
  starting transfers between devices  27.4 us (8%)
  matrix products  22.3 us (6%)
  other arithmetic  18.4 us (5%)
  between operations  15.9 us (5%)
  local copies, waits for them, and re-layouts  4.71 us (1%)
    psum x1, waiting for transfers between devices, shards(): lax.psum(partial_value.astype(jnp.bfloat16), 'mlp').astype(jnp.float32)  142 us
    reduce_scatter x1, waiting for transfers between devices, shards(): lax.psum_scatter(mlp_part.astype(jnp.bfloat16), 'mlp', scatter_dimension=...  69 us
    ppermute x1, waiting for transfers between devices, shards(): partner_q = lax.ppermute(queries, 'mlp', pair)  48.9 us
    all_to_all x1, starting transfers between devices, shards(): lax.all_to_all(send, 'mlp', split_axis=1, concat_axis=0, tiled=True)  15.2 us
    dot_general x1, matrix products, shards(): lax.dot_general(hidden, weights_full[:, 2 * width:2 * width + units], (((...  8.09 us
    ppermute x3, starting transfers between devices, shards(): lax.ppermute((weighted[heads_dev:], row_max[heads_dev:], row_sum[heads_de...  8.08 us
    reduce_sum x1, other arithmetic, shards(): row_sum = jnp.sum(weights, axis=-1)  7.81 us
  transfers between devices with their start and end apart: 8, of which 4 were waited for; matrix products, arithmetic and copies ran while one was open for 4% of the time, Pallas kernels for 0%

profile of v6, /device:TPU:6, one launch (start us, length us, event | category | flops | bytes accessed | tf_op | source)
XLA Modules:
  0.0 352.0 jit_solution(12471295468356548149)
XLA Ops:
  7.4 1.3 copy.25
  9.2 1.1 pad_maximum_fusion
  10.3 15.2 %all-to-all-start = ((bf16[280,16,128]{2,0,1:T(8,128)(2,1)}), bf16[280,16,128]{2,0,1:T(8,128)(2,1)S(1)}, u32[]{:S(2)}, u32[]{:S(2)}) async-start(bf16[280,16,128]{2,0,1:T(8,128)(2,1)} %pad_maximum_fusion), calls=%async_computation | async-start | bytes 2293760 | tf_op jit(solution)/shard_map/all_to_all | solution.py:54
  25.7 3.8 %collective-permute-start = (bf16[384,256]{0,1:T(8,128)(2,1)S(1)}, bf16[384,256]{0,1:T(8,128)(2,1)}, u32[]{:S(2)}, u32[]{:S(2)}) collective-permute-start(bf16[384,256]{0,1:T(8,128)(2,1)S(1)} %copy.22), channel_id=1, source_target_pairs={{0,1},{1,0},{2,3},{3,2},{4,5},{5,4},{6,7},{7,6},{8,9},{9,8},{10,11... | collective-permute-start | bytes 589832 | tf_op jit(solution)/shard_map/ppermute | solution.py:63
  30.4 2.1 pad_add_fusion
  32.5 48.9 %collective-permute-done = bf16[384,256]{0,1:T(8,128)(2,1)} collective-permute-done((bf16[384,256]{0,1:T(8,128)(2,1)S(1)}, bf16[384,256]{0,1:T(8,128)(2,1)}, u32[]{:S(2)}, u32[]{:S(2)}) %collective-permute-start) | collective-permute-done | bytes 196640 | tf_op jit(solution)/shard_map/ppermute | solution.py:63
  81.4 1.7 pad_maximum_fusion.1
  83.1 1.1 fusion.71
  84.3 4.0 %fusion.2 = (f32[4,384]{1,0:T(4,128)S(1)}, f32[2240,384,4]{1,0,2:T(8,128)S(1)}) fusion(pred[384,2240]{0,1:T(8,128)(4,1)S(1)} %pad_add_fusion, bf16[384,4,128]{0,2,1:T(8,128)(2,1)} %bitcast.74, bf16[192,128]{1,0:T(8,128)(2,1)S(1)} %reshape.106, bf16[2048,128]{1,0:T(8,128)(2,1)} %bitcast.73), kind=kOutput, calls=%fused_computation.4 | convolution fusion | flops 892271104 | bytes 15595520 | tf_op jit(solution)/shard_map/tqd,kd->qtk/dot_general | solution.py:84
  88.4 3.3 fusion.3
  91.7 1.6 copy-done.1
  93.4 2.2 collective-permute-start.2
  95.6 7.8 %fusion = f32[4,384]{1,0:T(4,128)S(1)} fusion(f32[2240,384,4]{1,0,2:T(8,128)} %copy-done.1, f32[4,384]{1,0:T(4,128)S(1)} %get-tuple-element.14, pred[384,2240]{0,1:T(8,128)(4,1)S(1)} %pad_add_fusion), kind=kLoop, calls=%fused_computation.2 | loop fusion | flops 13761024 | bytes 14635008 | tf_op jit(solution)/shard_map/reduce_sum | solution.py:90
  103.4 3.6 %collective-permute-start.3 = (f32[2,384]{1,0:T(2,128)S(1)}, f32[2,384]{1,0:T(2,128)S(1)}, u32[]{:S(2)}, u32[]{:S(2)}) collective-permute-start(f32[2,384]{1,0:T(2,128)S(1)} %slice.61), channel_id=1, source_target_pairs={{0,1},{1,0},{2,3},{3,2},{4,5},{5,4},{6,7},{7,6},{8,9},{9,8},{10,11... | collective-permute-start | bytes 9224 | tf_op jit(solution)/shard_map/ppermute | solution.py:95
  107.1 2.2 collective-permute-start.1
  109.3 3.2 collective-permute-done.1
  112.7 2.1 convolution_convert_fusion.1
  114.9 0.8 fusion.44
  115.9 142.1 %all-reduce.5.cloned.1.call-done = bf16[384,2560]{1,0:T(8,128)(2,1)} async-done(((bf16[384,2560]{1,0:T(8,128)(2,1)}), bf16[384,2560]{1,0:T(8,128)(2,1)}) %all-reduce.5.cloned.1.call-update) | async-done | bytes 1966096 | tf_op jit(solution)/shard_map/psum | solution.py:109
  258.0 3.0 fusion.6
  261.1 4.8 %fusion.12 = f32[384,608]{0,1:T(8,128)} fusion(bf16[2560,1920]{1,0:T(8,128)(2,1)} %all-gather.2.cloned.1.call-done, bf16[384,2560]{1,0:T(8,128)(2,1)S(1)} %get-tuple-element.6, f32[2560]{0:T(1024)S(1)} %convert_element_type.54, f32[384]{0:T(512)S(1)} %add_rsqrt_fusion), kind=kOutput, calls=%fused_computation.19 | convolution fusion | flops 1199308800 | bytes 6188544 | tf_op jit(solution)/shard_map/dot_general | solution.py:127
  265.8 8.1 %convolution_convert_fusion = bf16[384,2560]{1,0:T(8,128)(2,1)} fusion(bf16[2560,1920]{1,0:T(8,128)(2,1)} %all-gather.2.cloned.1.call-done, f32[384,608]{0,1:T(8,128)} %fusion.12, bf16[384,2560]{1,0:T(8,128)(2,1)S(1)} %get-tuple-element.6, f32[2560]{0:T(1024)S(1)} %convert_element_type.54, f32[384]{0:T(512)S(1)} %add_rsqrt_fusion), kind=kOutput, calls=%fused_computation.9 | convolution fusion | flops 2397069312 | bytes 11431424 | tf_op jit(solution)/shard_map/dot_general | solution.py:132
  273.9 69.0 %reduce-scatter.2.cloned.1.call-done = bf16[24,2560]{1,0:T(8,128)(2,1)} async-done(((bf16[384,2560]{1,0:T(8,128)(2,1)}), bf16[24,2560]{1,0:T(8,128)(2,1)}) %reduce-scatter.2.cloned.1.call-update) | async-done | bytes 122896 | tf_op jit(solution)/shard_map/reduce_scatter | solution.py:138
  343.0 1.6 add_convert_fusion.1
  (55 shorter events, 1.3 us)
Async XLA Ops:
  7.4 105.3 %copy-start = (bf16[256,2560]{1,0:T(8,128)(2,1)S(1)}, bf16[256,2560]{1,0:T(8,128)(2,1)}, u32[]{:S(2)}) copy-start(bf16[256,2560]{1,0:T(8,128)(2,1)} %param.19) | copy-start | bytes 3932164
  7.4 1.4 copy-start.2
  7.4 1.7 copy-start.8
  7.4 1.7 copy-start.9
  8.9 16.6 %copy-start.4 = (bf16[384,256]{1,0:T(8,128)(2,1)S(1)}, bf16[384,256]{1,0:T(8,128)(2,1)}, u32[]{:S(2)}) copy-start(bf16[384,256]{1,0:T(8,128)(2,1)} %param.12) | copy-start | bytes 589828
  10.3 72.8 %all-to-all-start = ((bf16[280,16,128]{2,0,1:T(8,128)(2,1)}), bf16[280,16,128]{2,0,1:T(8,128)(2,1)S(1)}, u32[]{:S(2)}, u32[]{:S(2)}) async-start(bf16[280,16,128]{2,0,1:T(8,128)(2,1)} %pad_maximum_fusion), calls=%async_computation | async-start | bytes 2293760 | tf_op jit(solution)/shard_map/all_to_all | solution.py:54
  25.5 232.5 %all-reduce.5.cloned.1.call-start = ((), (), s32[]{:S(2)}) async-start(), calls=%async_computation.2 | async-start | bytes 3932160 | tf_op jit(solution)/shard_map/psum | solution.py:109
  25.7 55.7 %collective-permute-start = (bf16[384,256]{0,1:T(8,128)(2,1)S(1)}, bf16[384,256]{0,1:T(8,128)(2,1)}, u32[]{:S(2)}, u32[]{:S(2)}) collective-permute-start(bf16[384,256]{0,1:T(8,128)(2,1)S(1)} %copy.22), channel_id=1, source_target_pairs={{0,1},{1,0},{2,3},{3,2},{4,5},{5,4},{6,7},{7,6},{8,9},{9,8},{10,11... | collective-permute-start | bytes 589832 | tf_op jit(solution)/shard_map/ppermute | solution.py:63
  84.3 4.1 %copy-start.3 = (bf16[16,128,128]{2,1,0:T(8,128)(2,1)S(1)}, bf16[16,128,128]{2,1,0:T(8,128)(2,1)}, u32[]{:S(2)}) copy-start(bf16[16,128,128]{2,1,0:T(8,128)(2,1)} %get-tuple-element.10) | copy-start | bytes 1572868
  88.4 5.0 %copy-start.1 = (f32[2240,384,4]{1,0,2:T(8,128)}, f32[2240,384,4]{1,0,2:T(8,128)S(1)}, u32[]{:S(2)}) copy-start(f32[2240,384,4]{1,0,2:T(8,128)S(1)} %get-tuple-element.15) | copy-start | bytes 41287684
  93.4 19.2 %collective-permute-start.2 = (f32[2,384,128]{1,2,0:T(8,128)S(1)}, f32[2,384,128]{1,2,0:T(8,128)S(1)}, u32[]{:S(2)}, u32[]{:S(2)}) collective-permute-start(f32[2,384,128]{1,2,0:T(8,128)S(1)} %slice.59), channel_id=1, source_target_pairs={{0,1},{1,0},{2,3},{3,2},{4,5},{5,4},{6,7},{7,6},{8,9},{9,8},{10,11... | collective-permute-start | bytes 1179656 | tf_op jit(solution)/shard_map/ppermute | solution.py:95
  103.4 5.9 %collective-permute-start.3 = (f32[2,384]{1,0:T(2,128)S(1)}, f32[2,384]{1,0:T(2,128)S(1)}, u32[]{:S(2)}, u32[]{:S(2)}) collective-permute-start(f32[2,384]{1,0:T(2,128)S(1)} %slice.61), channel_id=1, source_target_pairs={{0,1},{1,0},{2,3},{3,2},{4,5},{5,4},{6,7},{7,6},{8,9},{9,8},{10,11... | collective-permute-start | bytes 9224 | tf_op jit(solution)/shard_map/ppermute | solution.py:95
  107.1 5.5 %collective-permute-start.1 = (f32[2,384]{1,0:T(2,128)S(1)}, f32[2,384]{1,0:T(2,128)S(1)}, u32[]{:S(2)}, u32[]{:S(2)}) collective-permute-start(f32[2,384]{1,0:T(2,128)S(1)} %slice.58), channel_id=1, source_target_pairs={{0,1},{1,0},{2,3},{3,2},{4,5},{5,4},{6,7},{7,6},{8,9},{9,8},{10,11... | collective-permute-start | bytes 9224 | tf_op jit(solution)/shard_map/ppermute | solution.py:95
  112.6 2.3 copy-start.5
  112.6 2.3 copy-start.6
  112.6 2.3 copy-start.7
  112.7 3.2 copy-start.10
  114.8 146.2 %all-gather.2.cloned.1.call-start = ((), (), s32[]{:S(2)}) async-start(), calls=%async_computation.3 | async-start | bytes 10137600 | tf_op jit(solution)/shard_map/all_gather | solution.py:121
  115.7 227.3 %reduce-scatter.2.cloned.1.call-start = ((), (), s32[]{:S(2)}) async-start(), calls=%async_computation.4 | async-start | bytes 2088960 | tf_op jit(solution)/shard_map/reduce_scatter | solution.py:138
Sparse Core Ops, SparseCore 0:
  114.9 143.0 all-reduce.4
  274.1 68.8 reduce-scatter.1
Sparse Core Ops, SparseCore 1:
  119.0 71.2 all-gather.1

commit v7 on v6

--- a/solution.py
+++ b/solution.py
@@ -92,10 +92,12 @@
         "qtk,kd->qtd", weights.astype(jnp.bfloat16), values_all, preferred_element_type=jnp.float32
     )
 
-    sent = lax.ppermute(
-        (weighted[heads_dev:], row_max[heads_dev:], row_sum[heads_dev:]), "mlp", pair
+    other_weighted = lax.ppermute(weighted[heads_dev:], "mlp", pair)
+    other_stats = lax.ppermute(
+        jnp.stack([row_max[heads_dev:], row_sum[heads_dev:]]), "mlp", pair
     )
-    other_weighted, other_max, other_sum = sent
+    other_max = other_stats[0]
+    other_sum = other_stats[1]
     mine_max = row_max[:heads_dev]
     top = jnp.maximum(mine_max, other_max)
     scale_a = jnp.exp(mine_max - top)

time: 352 us -> 360 us (1.023)
  matrix products: 22.3 us -> 30 us
  waiting for transfers between devices: 263 us -> 267 us
    dot_general x1, matrix products: 4.03 us -> 8.36 us  [shards(): jnp.einsum('tqd,kd->qtk', grouped, keys_all, preferred_element_type=jnp.f...]
    ppermute x3 -> x2, starting transfers between devices: 8.08 us -> 5.84 us  [the longest x1 3.59 us: shards(): lax.ppermute(jnp.stack([row_max[heads_dev:], row_sum[heads_dev:]]), 'mlp'...]
  transfers between devices with their start and end apart: 8 -> 7, of which waited for: 4 -> 4; matrix products, arithmetic and copies ran while one was open for 4% -> 2% of each run, Pallas kernels for 0% -> 0%
where the time goes in v7:
time: 360 us
  waiting for transfers between devices  267 us (74%)
  matrix products  30 us (8%)
  starting transfers between devices  25.2 us (7%)
  other arithmetic  18.4 us (5%)
  between operations  15.9 us (4%)
    psum x1, waiting for transfers between devices, shards(): lax.psum(partial_value.astype(jnp.bfloat16), 'mlp').astype(jnp.float32)  143 us
    reduce_scatter x1, waiting for transfers between devices, shards(): lax.psum_scatter(mlp_part.astype(jnp.bfloat16), 'mlp', scatter_dimension=...  68.8 us
    ppermute x1, waiting for transfers between devices, shards(): partner_q = lax.ppermute(queries, 'mlp', pair)  48.9 us
    all_to_all x1, starting transfers between devices, shards(): lax.all_to_all(send, 'mlp', split_axis=1, concat_axis=0, tiled=True)  15.2 us
    dot_general x1, matrix products, shards(): jnp.einsum('tqd,kd->qtk', grouped, keys_all, preferred_element_type=jnp.f...  8.36 us
    dot_general x1, matrix products, shards(): lax.dot_general(hidden, weights_full[:, 2 * width:2 * width + units], (((...  8.07 us
    reduce_sum x1, other arithmetic, shards(): row_sum = jnp.sum(weights, axis=-1)  7.87 us
  transfers between devices with their start and end apart: 7, of which 4 were waited for; matrix products, arithmetic and copies ran while one was open for 2% of the time, Pallas kernels for 0%

profile of v7, /device:TPU:6, one launch (start us, length us, event | category | flops | bytes accessed | tf_op | source)
XLA Modules:
  0.0 359.5 jit_solution(15282653035411526524)
XLA Ops:
  7.4 1.3 copy.25
  9.2 1.1 pad_maximum_fusion
  10.3 15.2 %all-to-all-start = ((bf16[280,16,128]{2,0,1:T(8,128)(2,1)}), bf16[280,16,128]{2,0,1:T(8,128)(2,1)S(1)}, u32[]{:S(2)}, u32[]{:S(2)}) async-start(bf16[280,16,128]{2,0,1:T(8,128)(2,1)} %pad_maximum_fusion), calls=%async_computation | async-start | bytes 2293760 | tf_op jit(solution)/shard_map/all_to_all | solution.py:54
  25.6 0.2 copy.22
  25.7 3.8 %collective-permute-start = (bf16[384,256]{0,1:T(8,128)(2,1)S(1)}, bf16[384,256]{0,1:T(8,128)(2,1)}, u32[]{:S(2)}, u32[]{:S(2)}) collective-permute-start(bf16[384,256]{0,1:T(8,128)(2,1)S(1)} %copy.22), channel_id=1, source_target_pairs={{0,1},{1,0},{2,3},{3,2},{4,5},{5,4},{6,7},{7,6},{8,9},{9,8},{10,11... | collective-permute-start | bytes 589832 | tf_op jit(solution)/shard_map/ppermute | solution.py:63
  30.4 2.1 pad_add_fusion
  32.5 48.9 %collective-permute-done = bf16[384,256]{0,1:T(8,128)(2,1)} collective-permute-done((bf16[384,256]{0,1:T(8,128)(2,1)S(1)}, bf16[384,256]{0,1:T(8,128)(2,1)}, u32[]{:S(2)}, u32[]{:S(2)}) %collective-permute-start) | collective-permute-done | bytes 196640 | tf_op jit(solution)/shard_map/ppermute | solution.py:63
  81.4 1.7 pad_maximum_fusion.1
  83.1 1.1 fusion.72
  84.3 8.4 %fusion.2 = (f32[4,384]{1,0:T(4,128)S(1)}, f32[2240,384,4]{1,0,2:T(8,128)}) fusion(pred[384,2240]{0,1:T(8,128)(4,1)S(1)} %pad_add_fusion, bf16[384,4,128]{0,2,1:T(8,128)(2,1)} %bitcast.92, bf16[192,128]{1,0:T(8,128)(2,1)S(1)} %reshape.106, bf16[2048,128]{1,0:T(8,128)(2,1)} %bitcast.91), kind=kOutput, calls=%fused_computation.4 | convolution fusion | flops 892271104 | bytes 15595520 | tf_op jit(solution)/shard_map/tqd,kd->qtk/dot_general | solution.py:84
  92.7 7.9 %fusion = f32[4,384]{1,0:T(4,128)S(1)} fusion(f32[2240,384,4]{1,0,2:T(8,128)} %get-tuple-element.15, f32[4,384]{1,0:T(4,128)S(1)} %get-tuple-element.14, pred[384,2240]{0,1:T(8,128)(4,1)S(1)} %pad_add_fusion), kind=kLoop, calls=%fused_computation.2 | loop fusion | flops 13761024 | bytes 14635008 | tf_op jit(solution)/shard_map/reduce_sum | solution.py:90
  100.5 6.7 %fusion.3 = f32[4,384,128]{1,2,0:T(8,128)S(1)} fusion(f32[2240,384,4]{1,0,2:T(8,128)} %get-tuple-element.15, f32[4,384]{1,0:T(4,128)S(1)} %get-tuple-element.14, pred[384,2240]{0,1:T(8,128)(4,1)S(1)} %pad_add_fusion, bf16[192,128]{1,0:T(8,128)(2,1)S(1)} %reshape.109, bf16[2048,128]{1,0:T(8,128)(2,1)S(1)} %bitcast.90), kind=kOutput, calls=%fused_computation.5 | convolution fusion | flops 895713280 | bytes 15988736 | tf_op jit(solution)/shard_map/qtk,kd->qtd/dot_general | solution.py:91
  107.3 2.3 collective-permute-start.2
  109.6 3.6 collective-permute-start.1
  113.2 6.2 %collective-permute-done.1 = f32[2,2,384]{2,1,0:T(2,128)S(1)} collective-permute-done((f32[2,2,384]{2,1,0:T(2,128)S(1)}, f32[2,2,384]{2,1,0:T(2,128)S(1)}, u32[]{:S(2)}, u32[]{:S(2)}) %collective-permute-start.1) | collective-permute-done | bytes 6176 | tf_op jit(solution)/shard_map/ppermute | solution.py:96
  119.6 2.1 convolution_convert_fusion.1
  121.8 0.8 fusion.44
  122.6 0.2 reduce-scatter.2.cloned.1.call-start
  122.8 143.0 %all-reduce.5.cloned.1.call-done = bf16[384,2560]{1,0:T(8,128)(2,1)} async-done(((bf16[384,2560]{1,0:T(8,128)(2,1)}), bf16[384,2560]{1,0:T(8,128)(2,1)}) %all-reduce.5.cloned.1.call-update) | async-done | bytes 1966096 | tf_op jit(solution)/shard_map/psum | solution.py:111
  265.8 3.0 fusion.6
  268.8 4.8 %fusion.12 = f32[384,608]{0,1:T(8,128)} fusion(bf16[2560,1920]{1,0:T(8,128)(2,1)} %all-gather.2.cloned.1.call-done, bf16[384,2560]{1,0:T(8,128)(2,1)S(1)} %get-tuple-element.6, f32[2560]{0:T(1024)S(1)} %convert_element_type.54, f32[384]{0:T(512)S(1)} %add_rsqrt_fusion), kind=kOutput, calls=%fused_computation.19 | convolution fusion | flops 1199308800 | bytes 6188544 | tf_op jit(solution)/shard_map/dot_general | solution.py:129
  273.6 8.1 %convolution_convert_fusion = bf16[384,2560]{1,0:T(8,128)(2,1)} fusion(bf16[2560,1920]{1,0:T(8,128)(2,1)} %all-gather.2.cloned.1.call-done, f32[384,608]{0,1:T(8,128)} %fusion.12, bf16[384,2560]{1,0:T(8,128)(2,1)S(1)} %get-tuple-element.6, f32[2560]{0:T(1024)S(1)} %convert_element_type.54, f32[384]{0:T(512)S(1)} %add_rsqrt_fusion), kind=kOutput, calls=%fused_computation.9 | convolution fusion | flops 2397069312 | bytes 11431424 | tf_op jit(solution)/shard_map/dot_general | solution.py:134
  281.7 68.8 %reduce-scatter.2.cloned.1.call-done = bf16[24,2560]{1,0:T(8,128)(2,1)} async-done(((bf16[384,2560]{1,0:T(8,128)(2,1)}), bf16[24,2560]{1,0:T(8,128)(2,1)}) %reduce-scatter.2.cloned.1.call-update) | async-done | bytes 122896 | tf_op jit(solution)/shard_map/reduce_scatter | solution.py:140
  350.5 1.6 add_convert_fusion.1
  (51 shorter events, 0.9 us)
Async XLA Ops:
  7.4 112.2 %copy-start = (bf16[256,2560]{1,0:T(8,128)(2,1)S(1)}, bf16[256,2560]{1,0:T(8,128)(2,1)}, u32[]{:S(2)}) copy-start(bf16[256,2560]{1,0:T(8,128)(2,1)} %param.19) | copy-start | bytes 3932164
  7.4 1.4 copy-start.1
  7.4 1.7 copy-start.7
  7.4 1.7 copy-start.8
  8.9 16.6 %copy-start.3 = (bf16[384,256]{1,0:T(8,128)(2,1)S(1)}, bf16[384,256]{1,0:T(8,128)(2,1)}, u32[]{:S(2)}) copy-start(bf16[384,256]{1,0:T(8,128)(2,1)} %param.12) | copy-start | bytes 589828
  10.3 72.8 %all-to-all-start = ((bf16[280,16,128]{2,0,1:T(8,128)(2,1)}), bf16[280,16,128]{2,0,1:T(8,128)(2,1)S(1)}, u32[]{:S(2)}, u32[]{:S(2)}) async-start(bf16[280,16,128]{2,0,1:T(8,128)(2,1)} %pad_maximum_fusion), calls=%async_computation | async-start | bytes 2293760 | tf_op jit(solution)/shard_map/all_to_all | solution.py:54
  25.5 240.3 %all-reduce.5.cloned.1.call-start = ((), (), s32[]{:S(2)}) async-start(), calls=%async_computation.2 | async-start | bytes 3932160 | tf_op jit(solution)/shard_map/psum | solution.py:111
  25.7 55.7 %collective-permute-start = (bf16[384,256]{0,1:T(8,128)(2,1)S(1)}, bf16[384,256]{0,1:T(8,128)(2,1)}, u32[]{:S(2)}, u32[]{:S(2)}) collective-permute-start(bf16[384,256]{0,1:T(8,128)(2,1)S(1)} %copy.22), channel_id=1, source_target_pairs={{0,1},{1,0},{2,3},{3,2},{4,5},{5,4},{6,7},{7,6},{8,9},{9,8},{10,11... | collective-permute-start | bytes 589832 | tf_op jit(solution)/shard_map/ppermute | solution.py:63
  92.7 7.9 %copy-start.2 = (bf16[16,128,128]{2,1,0:T(8,128)(2,1)S(1)}, bf16[16,128,128]{2,1,0:T(8,128)(2,1)}, u32[]{:S(2)}) copy-start(bf16[16,128,128]{2,1,0:T(8,128)(2,1)} %get-tuple-element.10) | copy-start | bytes 1572868
  107.3 12.1 %collective-permute-start.2 = (f32[2,384,128]{1,2,0:T(8,128)S(1)}, f32[2,384,128]{1,2,0:T(8,128)S(1)}, u32[]{:S(2)}, u32[]{:S(2)}) collective-permute-start(f32[2,384,128]{1,2,0:T(8,128)S(1)} %slice.69), channel_id=1, source_target_pairs={{0,1},{1,0},{2,3},{3,2},{4,5},{5,4},{6,7},{7,6},{8,9},{9,8},{10,11... | collective-permute-start | bytes 1179656 | tf_op jit(solution)/shard_map/ppermute | solution.py:95
  109.6 9.8 %collective-permute-start.1 = (f32[2,2,384]{2,1,0:T(2,128)S(1)}, f32[2,2,384]{2,1,0:T(2,128)S(1)}, u32[]{:S(2)}, u32[]{:S(2)}) collective-permute-start(f32[2,2,384]{2,1,0:T(2,128)S(1)} %pad_maximum_fusion.2), channel_id=1, source_target_pairs={{0,1},{1,0},{2,3},{3,2},{4,5},{5,4},{6,7},{7,6},{8,9},{9,8},{10,11... | collective-permute-start | bytes 18440 | tf_op jit(solution)/shard_map/ppermute | solution.py:96
  119.5 2.3 copy-start.4
  119.5 2.3 copy-start.5
  119.5 2.3 copy-start.6
  119.6 3.2 copy-start.9
  121.7 147.1 %all-gather.2.cloned.1.call-start = ((), (), s32[]{:S(2)}) async-start(), calls=%async_computation.3 | async-start | bytes 10137600 | tf_op jit(solution)/shard_map/all_gather | solution.py:123
  122.6 228.0 %reduce-scatter.2.cloned.1.call-start = ((), (), s32[]{:S(2)}) async-start(), calls=%async_computation.4 | async-start | bytes 2088960 | tf_op jit(solution)/shard_map/reduce_scatter | solution.py:140
Sparse Core Ops, SparseCore 0:
  121.8 143.9 all-reduce.4
  281.8 68.6 reduce-scatter.1
Sparse Core Ops, SparseCore 1:
  125.9 72.1 all-gather.1

commit v8 on v6

--- a/solution.py
+++ b/solution.py
@@ -68,17 +68,15 @@
     cache_count = n_mlp * cache_half
     keys_all = jnp.concatenate([keys_old, keys_new], axis=0)
     values_all = jnp.concatenate([values_old, values_new], axis=0)
-    cached_idx = lax.iota(jnp.int32, cache_count)
-    cached_pos = (cached_idx // cache_half) * cache_dev + my_half * cache_half + cached_idx % cache_half
-    new_idx = lax.iota(jnp.int32, n_mlp * new_half)
+    key_idx = lax.iota(jnp.int32, cache_count + n_mlp * new_half)
+    cached_pos = (key_idx // cache_half) * cache_dev + my_half * cache_half + key_idx % cache_half
+    new_idx = key_idx - cache_count
     new_pos = (new_idx // new_half) * rows_dev + my_half * new_half + new_idx % new_half
     token_ids = lax.iota(jnp.int32, query_rows)
-    allowed = jnp.concatenate(
-        [
-            jnp.broadcast_to((cached_pos < length)[None, :], (query_rows, cache_count)),
-            new_pos[None, :] <= token_ids[:, None],
-        ],
-        axis=1,
+    allowed = jnp.where(
+        (key_idx < cache_count)[None, :],
+        (cached_pos < length)[None, :],
+        new_pos[None, :] <= token_ids[:, None],
     )
     scores = (
         jnp.einsum("tqd,kd->qtk", grouped, keys_all, preferred_element_type=jnp.float32)

time: 352 us -> 352 us (level)
  no operation moved by 1% of the time
where the time goes in v8:
time: 352 us
  waiting for transfers between devices  264 us (75%)
  starting transfers between devices  27.4 us (8%)
  matrix products  22.3 us (6%)
  other arithmetic  18.1 us (5%)
  between operations  15.9 us (5%)
  local copies, waits for them, and re-layouts  4.71 us (1%)
    psum x1, waiting for transfers between devices, shards(): lax.psum(partial_value.astype(jnp.bfloat16), 'mlp').astype(jnp.float32)  142 us
    reduce_scatter x1, waiting for transfers between devices, shards(): lax.psum_scatter(mlp_part.astype(jnp.bfloat16), 'mlp', scatter_dimension=...  69 us
    ppermute x1, waiting for transfers between devices, shards(): partner_q = lax.ppermute(queries, 'mlp', pair)  49.1 us
    all_to_all x1, starting transfers between devices, shards(): lax.all_to_all(send, 'mlp', split_axis=1, concat_axis=0, tiled=True)  15.2 us
    ppermute x3, starting transfers between devices, shards(): lax.ppermute((weighted[heads_dev:], row_max[heads_dev:], row_sum[heads_de...  8.08 us
    dot_general x1, matrix products, shards(): lax.dot_general(hidden, weights_full[:, 2 * width:2 * width + units], (((...  8.08 us
    reduce_sum x1, other arithmetic, shards(): row_sum = jnp.sum(weights, axis=-1)  7.81 us
  transfers between devices with their start and end apart: 8, of which 4 were waited for; matrix products, arithmetic and copies ran while one was open for 4% of the time, Pallas kernels for 0%

profile of v8, /device:TPU:6, one launch (start us, length us, event | category | flops | bytes accessed | tf_op | source)
XLA Modules:
  0.0 351.9 jit_solution(17133240008332151741)
XLA Ops:
  7.4 1.3 copy.25
  9.2 1.1 pad_maximum_fusion
  10.3 15.2 %all-to-all-start = ((bf16[280,16,128]{2,0,1:T(8,128)(2,1)}), bf16[280,16,128]{2,0,1:T(8,128)(2,1)S(1)}, u32[]{:S(2)}, u32[]{:S(2)}) async-start(bf16[280,16,128]{2,0,1:T(8,128)(2,1)} %pad_maximum_fusion), calls=%async_computation | async-start | bytes 2293760 | tf_op jit(solution)/shard_map/all_to_all | solution.py:54
  25.7 3.8 %collective-permute-start = (bf16[384,256]{0,1:T(8,128)(2,1)S(1)}, bf16[384,256]{0,1:T(8,128)(2,1)}, u32[]{:S(2)}, u32[]{:S(2)}) collective-permute-start(bf16[384,256]{0,1:T(8,128)(2,1)S(1)} %copy.22), channel_id=1, source_target_pairs={{0,1},{1,0},{2,3},{3,2},{4,5},{5,4},{6,7},{7,6},{8,9},{9,8},{10,11... | collective-permute-start | bytes 589832 | tf_op jit(solution)/shard_map/ppermute | solution.py:63
  30.3 2.0 fusion.9
  32.2 49.1 %collective-permute-done = bf16[384,256]{0,1:T(8,128)(2,1)} collective-permute-done((bf16[384,256]{0,1:T(8,128)(2,1)S(1)}, bf16[384,256]{0,1:T(8,128)(2,1)}, u32[]{:S(2)}, u32[]{:S(2)}) %collective-permute-start) | collective-permute-done | bytes 196640 | tf_op jit(solution)/shard_map/ppermute | solution.py:63
  81.4 1.7 pad_maximum_fusion.1
  83.1 1.1 fusion.75
  84.3 4.0 %fusion.2 = (f32[4,384]{1,0:T(4,128)S(1)}, f32[2240,384,4]{1,0,2:T(8,128)S(1)}) fusion(pred[384,2240]{0,1:T(8,128)(4,1)S(1)} %fusion.9, bf16[384,4,128]{0,2,1:T(8,128)(2,1)} %bitcast.74, bf16[192,128]{1,0:T(8,128)(2,1)S(1)} %reshape.157, bf16[2048,128]{1,0:T(8,128)(2,1)} %bitcast.73), kind=kOutput, calls=%fused_computation.4 | convolution fusion | flops 892271104 | bytes 15595520 | tf_op jit(solution)/shard_map/tqd,kd->qtk/dot_general | solution.py:82
  88.4 3.3 fusion.3
  91.7 1.6 copy-done.1
  93.4 2.2 collective-permute-start.2
  95.6 7.8 %fusion = f32[4,384]{1,0:T(4,128)S(1)} fusion(f32[2240,384,4]{1,0,2:T(8,128)} %copy-done.1, f32[4,384]{1,0:T(4,128)S(1)} %get-tuple-element.14, pred[384,2240]{0,1:T(8,128)(4,1)S(1)} %fusion.9), kind=kLoop, calls=%fused_computation.2 | loop fusion | flops 13761024 | bytes 14635008 | tf_op jit(solution)/shard_map/reduce_sum | solution.py:88
  103.4 3.6 %collective-permute-start.3 = (f32[2,384]{1,0:T(2,128)S(1)}, f32[2,384]{1,0:T(2,128)S(1)}, u32[]{:S(2)}, u32[]{:S(2)}) collective-permute-start(f32[2,384]{1,0:T(2,128)S(1)} %slice.61), channel_id=1, source_target_pairs={{0,1},{1,0},{2,3},{3,2},{4,5},{5,4},{6,7},{7,6},{8,9},{9,8},{10,11... | collective-permute-start | bytes 9224 | tf_op jit(solution)/shard_map/ppermute | solution.py:93
  107.1 2.2 collective-permute-start.1
  109.3 3.2 collective-permute-done.1
  112.7 2.1 convolution_convert_fusion.1
  114.9 0.8 fusion.45
  115.9 142.1 %all-reduce.5.cloned.1.call-done = bf16[384,2560]{1,0:T(8,128)(2,1)} async-done(((bf16[384,2560]{1,0:T(8,128)(2,1)}), bf16[384,2560]{1,0:T(8,128)(2,1)}) %all-reduce.5.cloned.1.call-update) | async-done | bytes 1966096 | tf_op jit(solution)/shard_map/psum | solution.py:107
  258.0 3.0 fusion.6
  261.0 4.8 %fusion.13 = f32[384,608]{0,1:T(8,128)} fusion(bf16[2560,1920]{1,0:T(8,128)(2,1)} %all-gather.2.cloned.1.call-done, bf16[384,2560]{1,0:T(8,128)(2,1)S(1)} %get-tuple-element.6, f32[2560]{0:T(1024)S(1)} %convert_element_type.54, f32[384]{0:T(512)S(1)} %add_rsqrt_fusion), kind=kOutput, calls=%fused_computation.20 | convolution fusion | flops 1199308800 | bytes 6188544 | tf_op jit(solution)/shard_map/dot_general | solution.py:125
  265.8 8.1 %convolution_convert_fusion = bf16[384,2560]{1,0:T(8,128)(2,1)} fusion(bf16[2560,1920]{1,0:T(8,128)(2,1)} %all-gather.2.cloned.1.call-done, f32[384,608]{0,1:T(8,128)} %fusion.13, bf16[384,2560]{1,0:T(8,128)(2,1)S(1)} %get-tuple-element.6, f32[2560]{0:T(1024)S(1)} %convert_element_type.54, f32[384]{0:T(512)S(1)} %add_rsqrt_fusion), kind=kOutput, calls=%fused_computation.9 | convolution fusion | flops 2397069312 | bytes 11431424 | tf_op jit(solution)/shard_map/dot_general | solution.py:130
  273.9 69.0 %reduce-scatter.2.cloned.1.call-done = bf16[24,2560]{1,0:T(8,128)(2,1)} async-done(((bf16[384,2560]{1,0:T(8,128)(2,1)}), bf16[24,2560]{1,0:T(8,128)(2,1)}) %reduce-scatter.2.cloned.1.call-update) | async-done | bytes 122896 | tf_op jit(solution)/shard_map/reduce_scatter | solution.py:136
  342.9 1.6 add_convert_fusion.1
  (53 shorter events, 1.2 us)
Async XLA Ops:
  7.4 105.3 %copy-start = (bf16[256,2560]{1,0:T(8,128)(2,1)S(1)}, bf16[256,2560]{1,0:T(8,128)(2,1)}, u32[]{:S(2)}) copy-start(bf16[256,2560]{1,0:T(8,128)(2,1)} %param.19) | copy-start | bytes 3932164
  7.4 1.4 copy-start.2
  7.4 1.7 copy-start.8
  7.4 1.7 copy-start.9
  8.9 16.6 %copy-start.4 = (bf16[384,256]{1,0:T(8,128)(2,1)S(1)}, bf16[384,256]{1,0:T(8,128)(2,1)}, u32[]{:S(2)}) copy-start(bf16[384,256]{1,0:T(8,128)(2,1)} %param.12) | copy-start | bytes 589828
  10.3 72.8 %all-to-all-start = ((bf16[280,16,128]{2,0,1:T(8,128)(2,1)}), bf16[280,16,128]{2,0,1:T(8,128)(2,1)S(1)}, u32[]{:S(2)}, u32[]{:S(2)}) async-start(bf16[280,16,128]{2,0,1:T(8,128)(2,1)} %pad_maximum_fusion), calls=%async_computation | async-start | bytes 2293760 | tf_op jit(solution)/shard_map/all_to_all | solution.py:54
  25.5 232.5 %all-reduce.5.cloned.1.call-start = ((), (), s32[]{:S(2)}) async-start(), calls=%async_computation.2 | async-start | bytes 3932160 | tf_op jit(solution)/shard_map/psum | solution.py:107
  25.7 55.7 %collective-permute-start = (bf16[384,256]{0,1:T(8,128)(2,1)S(1)}, bf16[384,256]{0,1:T(8,128)(2,1)}, u32[]{:S(2)}, u32[]{:S(2)}) collective-permute-start(bf16[384,256]{0,1:T(8,128)(2,1)S(1)} %copy.22), channel_id=1, source_target_pairs={{0,1},{1,0},{2,3},{3,2},{4,5},{5,4},{6,7},{7,6},{8,9},{9,8},{10,11... | collective-permute-start | bytes 589832 | tf_op jit(solution)/shard_map/ppermute | solution.py:63
  84.3 4.1 %copy-start.3 = (bf16[16,128,128]{2,1,0:T(8,128)(2,1)S(1)}, bf16[16,128,128]{2,1,0:T(8,128)(2,1)}, u32[]{:S(2)}) copy-start(bf16[16,128,128]{2,1,0:T(8,128)(2,1)} %get-tuple-element.10) | copy-start | bytes 1572868
  88.4 5.0 %copy-start.1 = (f32[2240,384,4]{1,0,2:T(8,128)}, f32[2240,384,4]{1,0,2:T(8,128)S(1)}, u32[]{:S(2)}) copy-start(f32[2240,384,4]{1,0,2:T(8,128)S(1)} %get-tuple-element.15) | copy-start | bytes 41287684
  93.4 19.2 %collective-permute-start.2 = (f32[2,384,128]{1,2,0:T(8,128)S(1)}, f32[2,384,128]{1,2,0:T(8,128)S(1)}, u32[]{:S(2)}, u32[]{:S(2)}) collective-permute-start(f32[2,384,128]{1,2,0:T(8,128)S(1)} %slice.59), channel_id=1, source_target_pairs={{0,1},{1,0},{2,3},{3,2},{4,5},{5,4},{6,7},{7,6},{8,9},{9,8},{10,11... | collective-permute-start | bytes 1179656 | tf_op jit(solution)/shard_map/ppermute | solution.py:93
  103.4 5.9 %collective-permute-start.3 = (f32[2,384]{1,0:T(2,128)S(1)}, f32[2,384]{1,0:T(2,128)S(1)}, u32[]{:S(2)}, u32[]{:S(2)}) collective-permute-start(f32[2,384]{1,0:T(2,128)S(1)} %slice.61), channel_id=1, source_target_pairs={{0,1},{1,0},{2,3},{3,2},{4,5},{5,4},{6,7},{7,6},{8,9},{9,8},{10,11... | collective-permute-start | bytes 9224 | tf_op jit(solution)/shard_map/ppermute | solution.py:93
  107.1 5.5 %collective-permute-start.1 = (f32[2,384]{1,0:T(2,128)S(1)}, f32[2,384]{1,0:T(2,128)S(1)}, u32[]{:S(2)}, u32[]{:S(2)}) collective-permute-start(f32[2,384]{1,0:T(2,128)S(1)} %slice.58), channel_id=1, source_target_pairs={{0,1},{1,0},{2,3},{3,2},{4,5},{5,4},{6,7},{7,6},{8,9},{9,8},{10,11... | collective-permute-start | bytes 9224 | tf_op jit(solution)/shard_map/ppermute | solution.py:93
  112.6 2.3 copy-start.5
  112.6 2.3 copy-start.6
  112.6 2.3 copy-start.7
  112.7 3.2 copy-start.10
  114.8 146.2 %all-gather.2.cloned.1.call-start = ((), (), s32[]{:S(2)}) async-start(), calls=%async_computation.3 | async-start | bytes 10137600 | tf_op jit(solution)/shard_map/all_gather | solution.py:119
  115.7 227.2 %reduce-scatter.2.cloned.1.call-start = ((), (), s32[]{:S(2)}) async-start(), calls=%async_computation.4 | async-start | bytes 2088960 | tf_op jit(solution)/shard_map/reduce_scatter | solution.py:136
Sparse Core Ops, SparseCore 0:
  114.9 143.0 all-reduce.4
  274.0 68.7 reduce-scatter.1
Sparse Core Ops, SparseCore 1:
  119.0 71.2 all-gather.1

commit v9 on v8

--- a/solution.py
+++ b/solution.py
@@ -127,12 +127,8 @@
         normed, weights_full[:, width : width + units], preferred_element_type=jnp.float32
     )
     hidden = (jax.nn.silu(gate_sum) * up_sum).astype(jnp.bfloat16)
-    mlp_part = lax.dot_general(
-        hidden,
-        weights_full[:, 2 * width : 2 * width + units],
-        (((1,), (1,)), ((), ())),
-        preferred_element_type=jnp.float32,
-    )
+    down_t = lax.optimization_barrier(weights_full[:, 2 * width : 2 * width + units].T)
+    mlp_part = jnp.dot(hidden, down_t, preferred_element_type=jnp.float32)
     mlp_rows = lax.psum_scatter(
         mlp_part.astype(jnp.bfloat16), "mlp", scatter_dimension=0, tiled=True
     ).astype(jnp.float32)

time: 352 us -> 356 us (1.011)
  local copies, waits for them, and re-layouts: 4.71 us -> 8.69 us
    transpose x0 -> x1, local copies, waits for them, and re-layouts: none -> 3.98 us  [shards(): weights_full[:, 2 * width:2 * width + units]]
where the time goes in v9:
time: 356 us
  waiting for transfers between devices  264 us (74%)
  starting transfers between devices  27.4 us (8%)
  matrix products  22.3 us (6%)
  other arithmetic  18.1 us (5%)
  between operations  15.9 us (4%)
  local copies, waits for them, and re-layouts  8.69 us (2%)
    psum x1, waiting for transfers between devices, shards(): lax.psum(partial_value.astype(jnp.bfloat16), 'mlp').astype(jnp.float32)  142 us
    reduce_scatter x1, waiting for transfers between devices, shards(): lax.psum_scatter(mlp_part.astype(jnp.bfloat16), 'mlp', scatter_dimension=...  69 us
    ppermute x1, waiting for transfers between devices, shards(): partner_q = lax.ppermute(queries, 'mlp', pair)  49.1 us
    all_to_all x1, starting transfers between devices, shards(): lax.all_to_all(send, 'mlp', split_axis=1, concat_axis=0, tiled=True)  15.2 us
    dot_general x1, matrix products, shards(): mlp_part = jnp.dot(hidden, down_t, preferred_element_type=jnp.float32)  8.09 us
    ppermute x3, starting transfers between devices, shards(): lax.ppermute((weighted[heads_dev:], row_max[heads_dev:], row_sum[heads_de...  8.08 us
    reduce_sum x1, other arithmetic, shards(): row_sum = jnp.sum(weights, axis=-1)  7.81 us
  transfers between devices with their start and end apart: 8, of which 4 were waited for; matrix products, arithmetic and copies ran while one was open for 4% of the time, Pallas kernels for 0%

profile of v9, /device:TPU:6, one launch (start us, length us, event | category | flops | bytes accessed | tf_op | source)
XLA Modules:
  0.0 355.9 jit_solution(12038195428069930252)
XLA Ops:
  7.4 1.3 copy.25
  9.2 1.1 pad_maximum_fusion
  10.3 15.2 %all-to-all-start = ((bf16[280,16,128]{2,0,1:T(8,128)(2,1)}), bf16[280,16,128]{2,0,1:T(8,128)(2,1)S(1)}, u32[]{:S(2)}, u32[]{:S(2)}) async-start(bf16[280,16,128]{2,0,1:T(8,128)(2,1)} %pad_maximum_fusion), calls=%async_computation | async-start | bytes 2293760 | tf_op jit(solution)/shard_map/all_to_all | solution.py:54
  25.7 3.8 %collective-permute-start = (bf16[384,256]{0,1:T(8,128)(2,1)S(1)}, bf16[384,256]{0,1:T(8,128)(2,1)}, u32[]{:S(2)}, u32[]{:S(2)}) collective-permute-start(bf16[384,256]{0,1:T(8,128)(2,1)S(1)} %copy.22), channel_id=1, source_target_pairs={{0,1},{1,0},{2,3},{3,2},{4,5},{5,4},{6,7},{7,6},{8,9},{9,8},{10,11... | collective-permute-start | bytes 589832 | tf_op jit(solution)/shard_map/ppermute | solution.py:63
  30.3 2.0 fusion.9
  32.2 49.1 %collective-permute-done = bf16[384,256]{0,1:T(8,128)(2,1)} collective-permute-done((bf16[384,256]{0,1:T(8,128)(2,1)S(1)}, bf16[384,256]{0,1:T(8,128)(2,1)}, u32[]{:S(2)}, u32[]{:S(2)}) %collective-permute-start) | collective-permute-done | bytes 196640 | tf_op jit(solution)/shard_map/ppermute | solution.py:63
  81.4 1.7 pad_maximum_fusion.1
  83.1 1.1 fusion.69
  84.3 4.0 %fusion.2 = (f32[4,384]{1,0:T(4,128)S(1)}, f32[2240,384,4]{1,0,2:T(8,128)S(1)}) fusion(pred[384,2240]{0,1:T(8,128)(4,1)S(1)} %fusion.9, bf16[384,4,128]{0,2,1:T(8,128)(2,1)} %bitcast.77, bf16[192,128]{1,0:T(8,128)(2,1)S(1)} %reshape.157, bf16[2048,128]{1,0:T(8,128)(2,1)} %bitcast.76), kind=kOutput, calls=%fused_computation.4 | convolution fusion | flops 892271104 | bytes 15595520 | tf_op jit(solution)/shard_map/tqd,kd->qtk/dot_general | solution.py:82
  88.4 3.3 fusion.3
  91.7 1.6 copy-done.1
  93.4 2.2 collective-permute-start.2
  95.6 7.8 %fusion = f32[4,384]{1,0:T(4,128)S(1)} fusion(f32[2240,384,4]{1,0,2:T(8,128)} %copy-done.1, f32[4,384]{1,0:T(4,128)S(1)} %get-tuple-element.14, pred[384,2240]{0,1:T(8,128)(4,1)S(1)} %fusion.9), kind=kLoop, calls=%fused_computation.2 | loop fusion | flops 13761024 | bytes 14635008 | tf_op jit(solution)/shard_map/reduce_sum | solution.py:88
  103.4 3.6 %collective-permute-start.3 = (f32[2,384]{1,0:T(2,128)S(1)}, f32[2,384]{1,0:T(2,128)S(1)}, u32[]{:S(2)}, u32[]{:S(2)}) collective-permute-start(f32[2,384]{1,0:T(2,128)S(1)} %slice.61), channel_id=1, source_target_pairs={{0,1},{1,0},{2,3},{3,2},{4,5},{5,4},{6,7},{7,6},{8,9},{9,8},{10,11... | collective-permute-start | bytes 9224 | tf_op jit(solution)/shard_map/ppermute | solution.py:93
  107.1 2.2 collective-permute-start.1
  109.3 3.2 collective-permute-done.1
  112.7 2.1 convolution_convert_fusion.1
  115.9 142.1 %all-reduce.5.cloned.1.call-done = bf16[384,2560]{1,0:T(8,128)(2,1)} async-done(((bf16[384,2560]{1,0:T(8,128)(2,1)}), bf16[384,2560]{1,0:T(8,128)(2,1)}) %all-reduce.5.cloned.1.call-update) | async-done | bytes 1966096 | tf_op jit(solution)/shard_map/psum | solution.py:107
  258.0 3.0 fusion.6
  261.0 4.0 %slice_bitcast_fusion = bf16[608,2560]{0,1:T(8,128)(2,1)} fusion(bf16[2560,1920]{1,0:T(8,128)(2,1)} %all-gather.2.cloned.1.call-done), kind=kLoop, calls=%fused_computation.17 | loop fusion | bytes 6225920 | tf_op jit(solution)/shard_map/transpose | solution.py:130
  265.0 4.7 %fusion.12 = f32[384,608]{0,1:T(8,128)} fusion(bf16[2560,1920]{1,0:T(8,128)(2,1)} %all-gather.2.cloned.1.call-done, bf16[384,2560]{1,0:T(8,128)(2,1)S(1)} %get-tuple-element.6, f32[2560]{0:T(1024)S(1)} %convert_element_type.54, f32[384]{0:T(512)S(1)} %add_rsqrt_fusion), kind=kOutput, calls=%fused_computation.20 | convolution fusion | flops 1199308800 | bytes 6188544 | tf_op jit(solution)/shard_map/dot_general | solution.py:125
  269.8 8.1 %convolution_convert_fusion = bf16[384,2560]{1,0:T(8,128)(2,1)} fusion(bf16[608,2560]{0,1:T(8,128)(2,1)} %slice_bitcast_fusion, bf16[2560,1920]{1,0:T(8,128)(2,1)} %all-gather.2.cloned.1.call-done, f32[384,608]{0,1:T(8,128)} %fusion.12, bf16[384,2560]{1,0:T(8,128)(2,1)S(1)} %get-tuple-element.6, f32[2560]{0:T(1024)S(1)} %convert_element_type.54, ...), kind=kOutput, calls=%fused_computation.9 | convolution fusion | flops 2397069312 | bytes 11431424 | tf_op jit(solution)/shard_map/dot_general | solution.py:131
  277.9 69.0 %reduce-scatter.2.cloned.1.call-done = bf16[24,2560]{1,0:T(8,128)(2,1)} async-done(((bf16[384,2560]{1,0:T(8,128)(2,1)}), bf16[24,2560]{1,0:T(8,128)(2,1)}) %reduce-scatter.2.cloned.1.call-update) | async-done | bytes 122896 | tf_op jit(solution)/shard_map/reduce_scatter | solution.py:132
  346.9 1.6 add_convert_fusion.1
  (54 shorter events, 2.0 us)
Async XLA Ops:
  7.4 105.3 %copy-start = (bf16[256,2560]{1,0:T(8,128)(2,1)S(1)}, bf16[256,2560]{1,0:T(8,128)(2,1)}, u32[]{:S(2)}) copy-start(bf16[256,2560]{1,0:T(8,128)(2,1)} %param.19) | copy-start | bytes 3932164
  7.4 1.4 copy-start.2
  7.4 1.7 copy-start.8
  7.4 1.7 copy-start.9
  9.0 16.6 %copy-start.4 = (bf16[384,256]{1,0:T(8,128)(2,1)S(1)}, bf16[384,256]{1,0:T(8,128)(2,1)}, u32[]{:S(2)}) copy-start(bf16[384,256]{1,0:T(8,128)(2,1)} %param.12) | copy-start | bytes 589828
  10.3 72.8 %all-to-all-start = ((bf16[280,16,128]{2,0,1:T(8,128)(2,1)}), bf16[280,16,128]{2,0,1:T(8,128)(2,1)S(1)}, u32[]{:S(2)}, u32[]{:S(2)}) async-start(bf16[280,16,128]{2,0,1:T(8,128)(2,1)} %pad_maximum_fusion), calls=%async_computation | async-start | bytes 2293760 | tf_op jit(solution)/shard_map/all_to_all | solution.py:54
  25.5 232.5 %all-reduce.5.cloned.1.call-start = ((), (), s32[]{:S(2)}) async-start(), calls=%async_computation.2 | async-start | bytes 3932160 | tf_op jit(solution)/shard_map/psum | solution.py:107
  25.7 55.7 %collective-permute-start = (bf16[384,256]{0,1:T(8,128)(2,1)S(1)}, bf16[384,256]{0,1:T(8,128)(2,1)}, u32[]{:S(2)}, u32[]{:S(2)}) collective-permute-start(bf16[384,256]{0,1:T(8,128)(2,1)S(1)} %copy.22), channel_id=1, source_target_pairs={{0,1},{1,0},{2,3},{3,2},{4,5},{5,4},{6,7},{7,6},{8,9},{9,8},{10,11... | collective-permute-start | bytes 589832 | tf_op jit(solution)/shard_map/ppermute | solution.py:63
  84.3 4.1 %copy-start.3 = (bf16[16,128,128]{2,1,0:T(8,128)(2,1)S(1)}, bf16[16,128,128]{2,1,0:T(8,128)(2,1)}, u32[]{:S(2)}) copy-start(bf16[16,128,128]{2,1,0:T(8,128)(2,1)} %get-tuple-element.10) | copy-start | bytes 1572868
  88.4 5.0 %copy-start.1 = (f32[2240,384,4]{1,0,2:T(8,128)}, f32[2240,384,4]{1,0,2:T(8,128)S(1)}, u32[]{:S(2)}) copy-start(f32[2240,384,4]{1,0,2:T(8,128)S(1)} %get-tuple-element.15) | copy-start | bytes 41287684
  93.4 19.2 %collective-permute-start.2 = (f32[2,384,128]{1,2,0:T(8,128)S(1)}, f32[2,384,128]{1,2,0:T(8,128)S(1)}, u32[]{:S(2)}, u32[]{:S(2)}) collective-permute-start(f32[2,384,128]{1,2,0:T(8,128)S(1)} %slice.59), channel_id=1, source_target_pairs={{0,1},{1,0},{2,3},{3,2},{4,5},{5,4},{6,7},{7,6},{8,9},{9,8},{10,11... | collective-permute-start | bytes 1179656 | tf_op jit(solution)/shard_map/ppermute | solution.py:93
  103.4 5.9 %collective-permute-start.3 = (f32[2,384]{1,0:T(2,128)S(1)}, f32[2,384]{1,0:T(2,128)S(1)}, u32[]{:S(2)}, u32[]{:S(2)}) collective-permute-start(f32[2,384]{1,0:T(2,128)S(1)} %slice.61), channel_id=1, source_target_pairs={{0,1},{1,0},{2,3},{3,2},{4,5},{5,4},{6,7},{7,6},{8,9},{9,8},{10,11... | collective-permute-start | bytes 9224 | tf_op jit(solution)/shard_map/ppermute | solution.py:93
  107.1 5.5 %collective-permute-start.1 = (f32[2,384]{1,0:T(2,128)S(1)}, f32[2,384]{1,0:T(2,128)S(1)}, u32[]{:S(2)}, u32[]{:S(2)}) collective-permute-start(f32[2,384]{1,0:T(2,128)S(1)} %slice.58), channel_id=1, source_target_pairs={{0,1},{1,0},{2,3},{3,2},{4,5},{5,4},{6,7},{7,6},{8,9},{9,8},{10,11... | collective-permute-start | bytes 9224 | tf_op jit(solution)/shard_map/ppermute | solution.py:93
  112.6 2.2 copy-start.5
  112.7 2.2 copy-start.6
  112.7 2.2 copy-start.7
  112.7 3.2 copy-start.10
  114.8 146.2 %all-gather.2.cloned.1.call-start = ((), (), s32[]{:S(2)}) async-start(), calls=%async_computation.3 | async-start | bytes 10137600 | tf_op jit(solution)/shard_map/all_gather | solution.py:119
  115.7 231.2 %reduce-scatter.2.cloned.1.call-start = ((), (), s32[]{:S(2)}) async-start(), calls=%async_computation.4 | async-start | bytes 2088960 | tf_op jit(solution)/shard_map/reduce_scatter | solution.py:132
Sparse Core Ops, SparseCore 0:
  114.9 143.0 all-reduce.4
  278.0 68.8 reduce-scatter.1
Sparse Core Ops, SparseCore 1:
  119.0 71.2 all-gather.1

commit v10 on v8

--- a/solution.py
+++ b/solution.py
@@ -45,19 +45,17 @@
     send = jnp.concatenate(
         [
             to_slots(cache_keys[0], cache_half),
+            to_slots(new_keys, new_half),
             to_slots(cache_values[0], cache_half),
-            to_slots(new_keys, new_half),
             to_slots(new_values, new_half),
         ],
         axis=0,
     )
     arrived = lax.all_to_all(send, "mlp", split_axis=1, concat_axis=0, tiled=True)
-    per_src = 2 * cache_half + 2 * new_half
-    arrived = arrived.reshape(n_mlp, per_src, HD)
-    keys_old = arrived[:, :cache_half].reshape(n_mlp * cache_half, HD)
-    values_old = arrived[:, cache_half : 2 * cache_half].reshape(n_mlp * cache_half, HD)
-    keys_new = arrived[:, 2 * cache_half : 2 * cache_half + new_half].reshape(n_mlp * new_half, HD)
-    values_new = arrived[:, 2 * cache_half + new_half :].reshape(n_mlp * new_half, HD)
+    per_kind = cache_half + new_half
+    arrived = arrived.reshape(n_mlp, 2 * per_kind, HD)
+    keys_all = arrived[:, :per_kind].reshape(n_mlp * per_kind, HD)
+    values_all = arrived[:, per_kind:].reshape(n_mlp * per_kind, HD)
 
     pair = [(d, d ^ 1) for d in range(n_mlp)]
     partner_q = lax.ppermute(queries, "mlp", pair)
@@ -65,16 +63,14 @@
     score_scale = HD ** (-0.5)
 
     length = cache_len[0]
-    cache_count = n_mlp * cache_half
-    keys_all = jnp.concatenate([keys_old, keys_new], axis=0)
-    values_all = jnp.concatenate([values_old, values_new], axis=0)
-    key_idx = lax.iota(jnp.int32, cache_count + n_mlp * new_half)
-    cached_pos = (key_idx // cache_half) * cache_dev + my_half * cache_half + key_idx % cache_half
-    new_idx = key_idx - cache_count
-    new_pos = (new_idx // new_half) * rows_dev + my_half * new_half + new_idx % new_half
+    key_idx = lax.iota(jnp.int32, n_mlp * per_kind)
+    source = key_idx // per_kind
+    within = key_idx % per_kind
+    cached_pos = source * cache_dev + my_half * cache_half + within
+    new_pos = source * rows_dev + my_half * new_half + (within - cache_half)
     token_ids = lax.iota(jnp.int32, query_rows)
     allowed = jnp.where(
-        (key_idx < cache_count)[None, :],
+        (within < cache_half)[None, :],
         (cached_pos < length)[None, :],
         new_pos[None, :] <= token_ids[:, None],
     )

time: 352 us -> 354 us (level)
  no operation moved by 1% of the time
where the time goes in v10:
time: 354 us; the launch traced here: 353 us
  waiting for transfers between devices  263 us (74%)
  starting transfers between devices  27.4 us (8%)
  matrix products  21.8 us (6%)
  other arithmetic  18.2 us (5%)
  between operations  15.9 us (4%)
  local copies, waits for them, and re-layouts  6.75 us (2%)
    psum x1, waiting for transfers between devices, shards(): lax.psum(partial_value.astype(jnp.bfloat16), 'mlp').astype(jnp.float32)  142 us
    reduce_scatter x1, waiting for transfers between devices, shards(): lax.psum_scatter(mlp_part.astype(jnp.bfloat16), 'mlp', scatter_dimension=...  69 us
    ppermute x1, waiting for transfers between devices, shards(): partner_q = lax.ppermute(queries, 'mlp', pair)  49.1 us
    all_to_all x1, starting transfers between devices, shards(): lax.all_to_all(send, 'mlp', split_axis=1, concat_axis=0, tiled=True)  15.2 us
    dot_general x1, matrix products, shards(): lax.dot_general(hidden, weights_full[:, 2 * width:2 * width + units], (((...  8.08 us
    ppermute x3, starting transfers between devices, shards(): lax.ppermute((weighted[heads_dev:], row_max[heads_dev:], row_sum[heads_de...  8.07 us
    reduce_sum x1, other arithmetic, shards(): row_sum = jnp.sum(weights, axis=-1)  7.83 us
  transfers between devices with their start and end apart: 8, of which 4 were waited for; matrix products, arithmetic and copies ran while one was open for 4% of the time, Pallas kernels for 0%

profile of v10, /device:TPU:6, one launch (start us, length us, event | category | flops | bytes accessed | tf_op | source)
XLA Modules:
  0.0 353.5 jit_solution(5190473232153872071)
XLA Ops:
  7.4 1.3 copy.25
  9.2 1.2 pad_maximum_fusion
  10.4 15.2 %all-to-all-start = ((bf16[280,16,128]{2,0,1:T(8,128)(2,1)}), bf16[280,16,128]{2,0,1:T(8,128)(2,1)S(1)}, u32[]{:S(2)}, u32[]{:S(2)}) async-start(bf16[280,16,128]{2,0,1:T(8,128)(2,1)} %pad_maximum_fusion), calls=%async_computation | async-start | bytes 2293760 | tf_op jit(solution)/shard_map/all_to_all | solution.py:54
  25.8 3.8 %collective-permute-start = (bf16[384,256]{0,1:T(8,128)(2,1)S(1)}, bf16[384,256]{0,1:T(8,128)(2,1)}, u32[]{:S(2)}, u32[]{:S(2)}) collective-permute-start(bf16[384,256]{0,1:T(8,128)(2,1)S(1)} %copy.22), channel_id=1, source_target_pairs={{0,1},{1,0},{2,3},{3,2},{4,5},{5,4},{6,7},{7,6},{8,9},{9,8},{10,11... | collective-permute-start | bytes 589832 | tf_op jit(solution)/shard_map/ppermute | solution.py:61
  30.4 2.0 fusion.9
  32.4 49.1 %collective-permute-done = bf16[384,256]{0,1:T(8,128)(2,1)} collective-permute-done((bf16[384,256]{0,1:T(8,128)(2,1)S(1)}, bf16[384,256]{0,1:T(8,128)(2,1)}, u32[]{:S(2)}, u32[]{:S(2)}) %collective-permute-start) | collective-permute-done | bytes 196640 | tf_op jit(solution)/shard_map/ppermute | solution.py:61
  81.5 1.7 pad_maximum_fusion.1
  84.3 1.2 reshape.139
  85.5 1.2 reshape.140
  86.7 3.3 fusion.2
  90.0 3.5 %fusion.3 = f32[4,384,128]{1,2,0:T(8,128)S(1)} fusion(bf16[2240,128,1]{1,0,2:T(8,128)(2,1)S(1)} %reshape.140, f32[2240,384,4]{1,0,2:T(8,128)S(1)} %get-tuple-element.13, f32[4,384]{1,0:T(4,128)S(1)} %get-tuple-element.12, pred[384,2240]{0,1:T(8,128)(4,1)S(1)} %fusion.9), kind=kOutput, calls=%fused_computation.5 | convolution fusion | flops 894566400 | bytes 15988736 | tf_op jit(solution)/shard_map/qtk,kd->qtd/dot_general | solution.py:85
  93.5 1.4 copy-done.1
  95.0 2.2 collective-permute-start.2
  97.2 7.8 %fusion = f32[4,384]{1,0:T(4,128)S(1)} fusion(f32[2240,384,4]{1,0,2:T(8,128)} %copy-done.1, f32[4,384]{1,0:T(4,128)S(1)} %get-tuple-element.12, pred[384,2240]{0,1:T(8,128)(4,1)S(1)} %fusion.9), kind=kLoop, calls=%fused_computation.2 | loop fusion | flops 13761024 | bytes 14635008 | tf_op jit(solution)/shard_map/reduce_sum | solution.py:84
  105.0 3.6 %collective-permute-start.3 = (f32[2,384]{1,0:T(2,128)S(1)}, f32[2,384]{1,0:T(2,128)S(1)}, u32[]{:S(2)}, u32[]{:S(2)}) collective-permute-start(f32[2,384]{1,0:T(2,128)S(1)} %slice.51), channel_id=1, source_target_pairs={{0,1},{1,0},{2,3},{3,2},{4,5},{5,4},{6,7},{7,6},{8,9},{9,8},{10,11... | collective-permute-start | bytes 9224 | tf_op jit(solution)/shard_map/ppermute | solution.py:89
  108.7 2.2 collective-permute-start.1
  110.9 3.2 collective-permute-done.1
  114.3 2.1 convolution_convert_fusion.1
  117.5 142.0 %all-reduce.5.cloned.1.call-done = bf16[384,2560]{1,0:T(8,128)(2,1)} async-done(((bf16[384,2560]{1,0:T(8,128)(2,1)}), bf16[384,2560]{1,0:T(8,128)(2,1)}) %all-reduce.5.cloned.1.call-update) | async-done | bytes 1966096 | tf_op jit(solution)/shard_map/psum | solution.py:103
  259.5 3.0 fusion.6
  262.6 4.8 %fusion.13 = f32[384,608]{0,1:T(8,128)} fusion(bf16[2560,1920]{1,0:T(8,128)(2,1)} %all-gather.2.cloned.1.call-done, bf16[384,2560]{1,0:T(8,128)(2,1)S(1)} %get-tuple-element.6, f32[2560]{0:T(1024)S(1)} %convert_element_type.54, f32[384]{0:T(512)S(1)} %add_rsqrt_fusion), kind=kOutput, calls=%fused_computation.20 | convolution fusion | flops 1199308800 | bytes 6188544 | tf_op jit(solution)/shard_map/dot_general | solution.py:121
  267.3 8.1 %convolution_convert_fusion = bf16[384,2560]{1,0:T(8,128)(2,1)} fusion(bf16[2560,1920]{1,0:T(8,128)(2,1)} %all-gather.2.cloned.1.call-done, f32[384,608]{0,1:T(8,128)} %fusion.13, bf16[384,2560]{1,0:T(8,128)(2,1)S(1)} %get-tuple-element.6, f32[2560]{0:T(1024)S(1)} %convert_element_type.54, f32[384]{0:T(512)S(1)} %add_rsqrt_fusion), kind=kOutput, calls=%fused_computation.9 | convolution fusion | flops 2397069312 | bytes 11431424 | tf_op jit(solution)/shard_map/dot_general | solution.py:126
  275.4 69.0 %reduce-scatter.2.cloned.1.call-done = bf16[24,2560]{1,0:T(8,128)(2,1)} async-done(((bf16[384,2560]{1,0:T(8,128)(2,1)}), bf16[24,2560]{1,0:T(8,128)(2,1)}) %reduce-scatter.2.cloned.1.call-update) | async-done | bytes 122896 | tf_op jit(solution)/shard_map/reduce_scatter | solution.py:132
  344.4 1.6 add_convert_fusion.1
  (50 shorter events, 3.1 us)
Async XLA Ops:
  7.4 106.9 %copy-start = (bf16[256,2560]{1,0:T(8,128)(2,1)S(1)}, bf16[256,2560]{1,0:T(8,128)(2,1)}, u32[]{:S(2)}) copy-start(bf16[256,2560]{1,0:T(8,128)(2,1)} %param.19) | copy-start | bytes 3932164
  7.4 1.4 copy-start.2
  7.4 1.7 copy-start.7
  7.4 1.7 copy-start.8
  8.9 16.7 %copy-start.3 = (bf16[384,256]{1,0:T(8,128)(2,1)S(1)}, bf16[384,256]{1,0:T(8,128)(2,1)}, u32[]{:S(2)}) copy-start(bf16[384,256]{1,0:T(8,128)(2,1)} %param.12) | copy-start | bytes 589828
  10.4 72.8 %all-to-all-start = ((bf16[280,16,128]{2,0,1:T(8,128)(2,1)}), bf16[280,16,128]{2,0,1:T(8,128)(2,1)S(1)}, u32[]{:S(2)}, u32[]{:S(2)}) async-start(bf16[280,16,128]{2,0,1:T(8,128)(2,1)} %pad_maximum_fusion), calls=%async_computation | async-start | bytes 2293760 | tf_op jit(solution)/shard_map/all_to_all | solution.py:54
  25.6 233.9 %all-reduce.5.cloned.1.call-start = ((), (), s32[]{:S(2)}) async-start(), calls=%async_computation.2 | async-start | bytes 3932160 | tf_op jit(solution)/shard_map/psum | solution.py:103
  25.8 55.7 %collective-permute-start = (bf16[384,256]{0,1:T(8,128)(2,1)S(1)}, bf16[384,256]{0,1:T(8,128)(2,1)}, u32[]{:S(2)}, u32[]{:S(2)}) collective-permute-start(bf16[384,256]{0,1:T(8,128)(2,1)S(1)} %copy.22), channel_id=1, source_target_pairs={{0,1},{1,0},{2,3},{3,2},{4,5},{5,4},{6,7},{7,6},{8,9},{9,8},{10,11... | collective-permute-start | bytes 589832 | tf_op jit(solution)/shard_map/ppermute | solution.py:61
  90.0 5.0 %copy-start.1 = (f32[2240,384,4]{1,0,2:T(8,128)}, f32[2240,384,4]{1,0,2:T(8,128)S(1)}, u32[]{:S(2)}) copy-start(f32[2240,384,4]{1,0,2:T(8,128)S(1)} %get-tuple-element.13) | copy-start | bytes 41287684
  95.0 19.2 %collective-permute-start.2 = (f32[2,384,128]{1,2,0:T(8,128)S(1)}, f32[2,384,128]{1,2,0:T(8,128)S(1)}, u32[]{:S(2)}, u32[]{:S(2)}) collective-permute-start(f32[2,384,128]{1,2,0:T(8,128)S(1)} %slice.49), channel_id=1, source_target_pairs={{0,1},{1,0},{2,3},{3,2},{4,5},{5,4},{6,7},{7,6},{8,9},{9,8},{10,11... | collective-permute-start | bytes 1179656 | tf_op jit(solution)/shard_map/ppermute | solution.py:89
  105.0 5.9 %collective-permute-start.3 = (f32[2,384]{1,0:T(2,128)S(1)}, f32[2,384]{1,0:T(2,128)S(1)}, u32[]{:S(2)}, u32[]{:S(2)}) collective-permute-start(f32[2,384]{1,0:T(2,128)S(1)} %slice.51), channel_id=1, source_target_pairs={{0,1},{1,0},{2,3},{3,2},{4,5},{5,4},{6,7},{7,6},{8,9},{9,8},{10,11... | collective-permute-start | bytes 9224 | tf_op jit(solution)/shard_map/ppermute | solution.py:89
  108.7 5.5 %collective-permute-start.1 = (f32[2,384]{1,0:T(2,128)S(1)}, f32[2,384]{1,0:T(2,128)S(1)}, u32[]{:S(2)}, u32[]{:S(2)}) collective-permute-start(f32[2,384]{1,0:T(2,128)S(1)} %slice.48), channel_id=1, source_target_pairs={{0,1},{1,0},{2,3},{3,2},{4,5},{5,4},{6,7},{7,6},{8,9},{9,8},{10,11... | collective-permute-start | bytes 9224 | tf_op jit(solution)/shard_map/ppermute | solution.py:89
  114.2 2.3 copy-start.4
  114.2 2.3 copy-start.5
  114.2 2.3 copy-start.6
  114.3 3.2 copy-start.9
  116.4 146.1 %all-gather.2.cloned.1.call-start = ((), (), s32[]{:S(2)}) async-start(), calls=%async_computation.3 | async-start | bytes 10137600 | tf_op jit(solution)/shard_map/all_gather | solution.py:115
  117.3 227.2 %reduce-scatter.2.cloned.1.call-start = ((), (), s32[]{:S(2)}) async-start(), calls=%async_computation.4 | async-start | bytes 2088960 | tf_op jit(solution)/shard_map/reduce_scatter | solution.py:132
Sparse Core Ops, SparseCore 0:
  116.5 142.9 all-reduce.4
  275.6 68.8 reduce-scatter.1
Sparse Core Ops, SparseCore 1:
  120.6 71.2 all-gather.1

commit v11 on v6

--- a/solution.py
+++ b/solution.py
@@ -124,10 +124,9 @@
         axis=0,
         tiled=True,
     )
-    gate_sum = jnp.dot(normed, weights_full[:, :units], preferred_element_type=jnp.float32)
-    up_sum = jnp.dot(
-        normed, weights_full[:, width : width + units], preferred_element_type=jnp.float32
-    )
+    both = jnp.dot(normed, weights_full[:, : 2 * width], preferred_element_type=jnp.float32)
+    gate_sum = both[:, :units]
+    up_sum = both[:, width : width + units]
     hidden = (jax.nn.silu(gate_sum) * up_sum).astype(jnp.bfloat16)
     mlp_part = lax.dot_general(
         hidden,

time: 352 us -> 350 us (level)
  transfers between devices with their start and end apart: 8 -> 8, of which waited for: 4 -> 4; matrix products, arithmetic and copies ran while one was open for 4% -> 5% of each run, Pallas kernels for 0% -> 0%
where the time goes in v11:
time: 350 us
  waiting for transfers between devices  263 us (75%)
  starting transfers between devices  27.4 us (8%)
  matrix products  20 us (6%)
  other arithmetic  18.4 us (5%)
  between operations  15.9 us (5%)
  local copies, waits for them, and re-layouts  4.71 us (1%)
    psum x1, waiting for transfers between devices, shards(): lax.psum(partial_value.astype(jnp.bfloat16), 'mlp').astype(jnp.float32)  142 us
    reduce_scatter x1, waiting for transfers between devices, shards(): lax.psum_scatter(mlp_part.astype(jnp.bfloat16), 'mlp', scatter_dimension=...  69.1 us
    ppermute x1, waiting for transfers between devices, shards(): partner_q = lax.ppermute(queries, 'mlp', pair)  48.9 us
    all_to_all x1, starting transfers between devices, shards(): lax.all_to_all(send, 'mlp', split_axis=1, concat_axis=0, tiled=True)  15.2 us
    ppermute x3, starting transfers between devices, shards(): lax.ppermute((weighted[heads_dev:], row_max[heads_dev:], row_sum[heads_de...  8.08 us
    reduce_sum x1, other arithmetic, shards(): row_sum = jnp.sum(weights, axis=-1)  7.81 us
  transfers between devices with their start and end apart: 8, of which 4 were waited for; matrix products, arithmetic and copies ran while one was open for 5% of the time, Pallas kernels for 0%

profile of v11, /device:TPU:6, one launch (start us, length us, event | category | flops | bytes accessed | tf_op | source)
XLA Modules:
  0.0 349.8 jit_solution(1346485430035505609)
XLA Ops:
  7.4 1.3 copy.25
  9.2 1.1 pad_maximum_fusion
  10.3 15.2 %all-to-all-start = ((bf16[280,16,128]{2,0,1:T(8,128)(2,1)}), bf16[280,16,128]{2,0,1:T(8,128)(2,1)S(1)}, u32[]{:S(2)}, u32[]{:S(2)}) async-start(bf16[280,16,128]{2,0,1:T(8,128)(2,1)} %pad_maximum_fusion), calls=%async_computation | async-start | bytes 2293760 | tf_op jit(solution)/shard_map/all_to_all | solution.py:54
  25.7 3.8 %collective-permute-start = (bf16[384,256]{0,1:T(8,128)(2,1)S(1)}, bf16[384,256]{0,1:T(8,128)(2,1)}, u32[]{:S(2)}, u32[]{:S(2)}) collective-permute-start(bf16[384,256]{0,1:T(8,128)(2,1)S(1)} %copy.22), channel_id=1, source_target_pairs={{0,1},{1,0},{2,3},{3,2},{4,5},{5,4},{6,7},{7,6},{8,9},{9,8},{10,11... | collective-permute-start | bytes 589832 | tf_op jit(solution)/shard_map/ppermute | solution.py:63
  30.4 2.1 pad_add_fusion
  32.5 48.9 %collective-permute-done = bf16[384,256]{0,1:T(8,128)(2,1)} collective-permute-done((bf16[384,256]{0,1:T(8,128)(2,1)S(1)}, bf16[384,256]{0,1:T(8,128)(2,1)}, u32[]{:S(2)}, u32[]{:S(2)}) %collective-permute-start) | collective-permute-done | bytes 196640 | tf_op jit(solution)/shard_map/ppermute | solution.py:63
  81.4 1.7 pad_maximum_fusion.1
  83.1 1.1 fusion.58
  84.3 4.0 %fusion.2 = (f32[4,384]{1,0:T(4,128)S(1)}, f32[2240,384,4]{1,0,2:T(8,128)S(1)}) fusion(pred[384,2240]{0,1:T(8,128)(4,1)S(1)} %pad_add_fusion, bf16[384,4,128]{0,2,1:T(8,128)(2,1)} %bitcast.74, bf16[192,128]{1,0:T(8,128)(2,1)S(1)} %reshape.106, bf16[2048,128]{1,0:T(8,128)(2,1)} %bitcast.73), kind=kOutput, calls=%fused_computation.4 | convolution fusion | flops 892271104 | bytes 15595520 | tf_op jit(solution)/shard_map/tqd,kd->qtk/dot_general | solution.py:84
  88.4 3.3 fusion.3
  91.7 1.6 copy-done.1
  93.4 2.2 collective-permute-start.2
  95.6 7.8 %fusion = f32[4,384]{1,0:T(4,128)S(1)} fusion(f32[2240,384,4]{1,0,2:T(8,128)} %copy-done.1, f32[4,384]{1,0:T(4,128)S(1)} %get-tuple-element.14, pred[384,2240]{0,1:T(8,128)(4,1)S(1)} %pad_add_fusion), kind=kLoop, calls=%fused_computation.2 | loop fusion | flops 13761024 | bytes 14635008 | tf_op jit(solution)/shard_map/reduce_sum | solution.py:90
  103.4 3.6 %collective-permute-start.3 = (f32[2,384]{1,0:T(2,128)S(1)}, f32[2,384]{1,0:T(2,128)S(1)}, u32[]{:S(2)}, u32[]{:S(2)}) collective-permute-start(f32[2,384]{1,0:T(2,128)S(1)} %slice.65), channel_id=1, source_target_pairs={{0,1},{1,0},{2,3},{3,2},{4,5},{5,4},{6,7},{7,6},{8,9},{9,8},{10,11... | collective-permute-start | bytes 9224 | tf_op jit(solution)/shard_map/ppermute | solution.py:95
  107.1 2.2 collective-permute-start.1
  109.3 3.2 collective-permute-done.1
  112.7 2.1 convolution_convert_fusion.1
  114.9 0.8 fusion.31
  115.9 142.1 %all-reduce.5.cloned.1.call-done = bf16[384,2560]{1,0:T(8,128)(2,1)} async-done(((bf16[384,2560]{1,0:T(8,128)(2,1)}), bf16[384,2560]{1,0:T(8,128)(2,1)}) %all-reduce.5.cloned.1.call-update) | async-done | bytes 1966096 | tf_op jit(solution)/shard_map/psum | solution.py:109
  258.0 3.0 fusion.8
  261.1 5.6 %fusion.6 = f32[384,1280]{1,0:T(8,128)S(1)} fusion(bf16[2560,1920]{1,0:T(8,128)(2,1)} %all-gather.2.cloned.1.call-done, bf16[384,2560]{1,0:T(8,128)(2,1)S(1)} %get-tuple-element.6, f32[2560]{0:T(1024)S(1)} %convert_element_type.54, f32[384]{0:T(512)S(1)} %add_rsqrt_fusion), kind=kOutput, calls=%fused_computation.7 | convolution fusion | flops 2520514560 | bytes 10497536 | tf_op jit(solution)/shard_map/dot_general | solution.py:127
  266.7 5.0 %convolution_convert_fusion = bf16[384,2560]{1,0:T(8,128)(2,1)} fusion(bf16[2560,1920]{1,0:T(8,128)(2,1)} %all-gather.2.cloned.1.call-done, f32[384,1280]{1,0:T(8,128)S(1)} %fusion.6), kind=kOutput, calls=%fused_computation.11 | convolution fusion | flops 1197760512 | bytes 7208960 | tf_op jit(solution)/shard_map/dot_general | solution.py:131
  271.7 69.1 %reduce-scatter.2.cloned.1.call-done = bf16[24,2560]{1,0:T(8,128)(2,1)} async-done(((bf16[384,2560]{1,0:T(8,128)(2,1)}), bf16[24,2560]{1,0:T(8,128)(2,1)}) %reduce-scatter.2.cloned.1.call-update) | async-done | bytes 122896 | tf_op jit(solution)/shard_map/reduce_scatter | solution.py:137
  340.7 1.6 add_convert_fusion.1
  (55 shorter events, 1.3 us)
Async XLA Ops:
  7.4 105.3 %copy-start = (bf16[256,2560]{1,0:T(8,128)(2,1)S(1)}, bf16[256,2560]{1,0:T(8,128)(2,1)}, u32[]{:S(2)}) copy-start(bf16[256,2560]{1,0:T(8,128)(2,1)} %param.19) | copy-start | bytes 3932164
  7.4 1.4 copy-start.2
  7.4 1.7 copy-start.8
  7.4 1.7 copy-start.9
  8.9 16.6 %copy-start.4 = (bf16[384,256]{1,0:T(8,128)(2,1)S(1)}, bf16[384,256]{1,0:T(8,128)(2,1)}, u32[]{:S(2)}) copy-start(bf16[384,256]{1,0:T(8,128)(2,1)} %param.12) | copy-start | bytes 589828
  10.3 72.8 %all-to-all-start = ((bf16[280,16,128]{2,0,1:T(8,128)(2,1)}), bf16[280,16,128]{2,0,1:T(8,128)(2,1)S(1)}, u32[]{:S(2)}, u32[]{:S(2)}) async-start(bf16[280,16,128]{2,0,1:T(8,128)(2,1)} %pad_maximum_fusion), calls=%async_computation | async-start | bytes 2293760 | tf_op jit(solution)/shard_map/all_to_all | solution.py:54
  25.5 232.5 %all-reduce.5.cloned.1.call-start = ((), (), s32[]{:S(2)}) async-start(), calls=%async_computation.2 | async-start | bytes 3932160 | tf_op jit(solution)/shard_map/psum | solution.py:109
  25.7 55.7 %collective-permute-start = (bf16[384,256]{0,1:T(8,128)(2,1)S(1)}, bf16[384,256]{0,1:T(8,128)(2,1)}, u32[]{:S(2)}, u32[]{:S(2)}) collective-permute-start(bf16[384,256]{0,1:T(8,128)(2,1)S(1)} %copy.22), channel_id=1, source_target_pairs={{0,1},{1,0},{2,3},{3,2},{4,5},{5,4},{6,7},{7,6},{8,9},{9,8},{10,11... | collective-permute-start | bytes 589832 | tf_op jit(solution)/shard_map/ppermute | solution.py:63
  84.3 4.1 %copy-start.3 = (bf16[16,128,128]{2,1,0:T(8,128)(2,1)S(1)}, bf16[16,128,128]{2,1,0:T(8,128)(2,1)}, u32[]{:S(2)}) copy-start(bf16[16,128,128]{2,1,0:T(8,128)(2,1)} %get-tuple-element.10) | copy-start | bytes 1572868
  88.4 5.0 %copy-start.1 = (f32[2240,384,4]{1,0,2:T(8,128)}, f32[2240,384,4]{1,0,2:T(8,128)S(1)}, u32[]{:S(2)}) copy-start(f32[2240,384,4]{1,0,2:T(8,128)S(1)} %get-tuple-element.15) | copy-start | bytes 41287684
  93.4 19.2 %collective-permute-start.2 = (f32[2,384,128]{1,2,0:T(8,128)S(1)}, f32[2,384,128]{1,2,0:T(8,128)S(1)}, u32[]{:S(2)}, u32[]{:S(2)}) collective-permute-start(f32[2,384,128]{1,2,0:T(8,128)S(1)} %slice.63), channel_id=1, source_target_pairs={{0,1},{1,0},{2,3},{3,2},{4,5},{5,4},{6,7},{7,6},{8,9},{9,8},{10,11... | collective-permute-start | bytes 1179656 | tf_op jit(solution)/shard_map/ppermute | solution.py:95
  103.4 5.9 %collective-permute-start.3 = (f32[2,384]{1,0:T(2,128)S(1)}, f32[2,384]{1,0:T(2,128)S(1)}, u32[]{:S(2)}, u32[]{:S(2)}) collective-permute-start(f32[2,384]{1,0:T(2,128)S(1)} %slice.65), channel_id=1, source_target_pairs={{0,1},{1,0},{2,3},{3,2},{4,5},{5,4},{6,7},{7,6},{8,9},{9,8},{10,11... | collective-permute-start | bytes 9224 | tf_op jit(solution)/shard_map/ppermute | solution.py:95
  107.1 5.5 %collective-permute-start.1 = (f32[2,384]{1,0:T(2,128)S(1)}, f32[2,384]{1,0:T(2,128)S(1)}, u32[]{:S(2)}, u32[]{:S(2)}) collective-permute-start(f32[2,384]{1,0:T(2,128)S(1)} %slice.62), channel_id=1, source_target_pairs={{0,1},{1,0},{2,3},{3,2},{4,5},{5,4},{6,7},{7,6},{8,9},{9,8},{10,11... | collective-permute-start | bytes 9224 | tf_op jit(solution)/shard_map/ppermute | solution.py:95
  112.6 2.3 copy-start.5
  112.6 2.3 copy-start.6
  112.6 2.3 copy-start.7
  112.7 3.2 copy-start.10
  114.8 146.2 %all-gather.2.cloned.1.call-start = ((), (), s32[]{:S(2)}) async-start(), calls=%async_computation.3 | async-start | bytes 10137600 | tf_op jit(solution)/shard_map/all_gather | solution.py:121
  115.7 225.1 %reduce-scatter.2.cloned.1.call-start = ((), (), s32[]{:S(2)}) async-start(), calls=%async_computation.4 | async-start | bytes 2088960 | tf_op jit(solution)/shard_map/reduce_scatter | solution.py:137
Sparse Core Ops, SparseCore 0:
  114.9 143.0 all-reduce.4
  271.8 68.9 reduce-scatter.1
Sparse Core Ops, SparseCore 1:
  119.0 71.2 all-gather.1

commit v12 on v11

--- a/solution.py
+++ b/solution.py
@@ -125,12 +125,12 @@
         tiled=True,
     )
     both = jnp.dot(normed, weights_full[:, : 2 * width], preferred_element_type=jnp.float32)
-    gate_sum = both[:, :units]
-    up_sum = both[:, width : width + units]
+    gate_sum = both[:, :width]
+    up_sum = both[:, width:]
     hidden = (jax.nn.silu(gate_sum) * up_sum).astype(jnp.bfloat16)
     mlp_part = lax.dot_general(
         hidden,
-        weights_full[:, 2 * width : 2 * width + units],
+        weights_full[:, 2 * width :],
         (((1,), (1,)), ((), ())),
         preferred_element_type=jnp.float32,
     )

time: 350 us -> 350 us (level)
  no operation moved by 1% of the time
where the time goes in v12:
time: 350 us
  waiting for transfers between devices  263 us (75%)
  starting transfers between devices  27.4 us (8%)
  matrix products  20 us (6%)
  other arithmetic  18.4 us (5%)
  between operations  15.9 us (5%)
  local copies, waits for them, and re-layouts  4.71 us (1%)
    psum x1, waiting for transfers between devices, shards(): lax.psum(partial_value.astype(jnp.bfloat16), 'mlp').astype(jnp.float32)  142 us
    reduce_scatter x1, waiting for transfers between devices, shards(): lax.psum_scatter(mlp_part.astype(jnp.bfloat16), 'mlp', scatter_dimension=...  69 us
    ppermute x1, waiting for transfers between devices, shards(): partner_q = lax.ppermute(queries, 'mlp', pair)  48.9 us
    all_to_all x1, starting transfers between devices, shards(): lax.all_to_all(send, 'mlp', split_axis=1, concat_axis=0, tiled=True)  15.2 us
    ppermute x3, starting transfers between devices, shards(): lax.ppermute((weighted[heads_dev:], row_max[heads_dev:], row_sum[heads_de...  8.08 us
    reduce_sum x1, other arithmetic, shards(): row_sum = jnp.sum(weights, axis=-1)  7.81 us
  transfers between devices with their start and end apart: 8, of which 4 were waited for; matrix products, arithmetic and copies ran while one was open for 5% of the time, Pallas kernels for 0%

profile of v12, /device:TPU:6, one launch (start us, length us, event | category | flops | bytes accessed | tf_op | source)
XLA Modules:
  0.0 349.7 jit_solution(10881288263603468844)
XLA Ops:
  7.4 1.3 copy.25
  9.2 1.1 pad_maximum_fusion
  10.3 15.2 %all-to-all-start = ((bf16[280,16,128]{2,0,1:T(8,128)(2,1)}), bf16[280,16,128]{2,0,1:T(8,128)(2,1)S(1)}, u32[]{:S(2)}, u32[]{:S(2)}) async-start(bf16[280,16,128]{2,0,1:T(8,128)(2,1)} %pad_maximum_fusion), calls=%async_computation | async-start | bytes 2293760 | tf_op jit(solution)/shard_map/all_to_all | solution.py:54
  25.7 3.8 %collective-permute-start = (bf16[384,256]{0,1:T(8,128)(2,1)S(1)}, bf16[384,256]{0,1:T(8,128)(2,1)}, u32[]{:S(2)}, u32[]{:S(2)}) collective-permute-start(bf16[384,256]{0,1:T(8,128)(2,1)S(1)} %copy.22), channel_id=1, source_target_pairs={{0,1},{1,0},{2,3},{3,2},{4,5},{5,4},{6,7},{7,6},{8,9},{9,8},{10,11... | collective-permute-start | bytes 589832 | tf_op jit(solution)/shard_map/ppermute | solution.py:63
  30.4 2.1 pad_add_fusion
  32.5 48.9 %collective-permute-done = bf16[384,256]{0,1:T(8,128)(2,1)} collective-permute-done((bf16[384,256]{0,1:T(8,128)(2,1)S(1)}, bf16[384,256]{0,1:T(8,128)(2,1)}, u32[]{:S(2)}, u32[]{:S(2)}) %collective-permute-start) | collective-permute-done | bytes 196640 | tf_op jit(solution)/shard_map/ppermute | solution.py:63
  81.4 1.7 pad_maximum_fusion.1
  83.1 1.1 fusion.58
  84.3 4.0 %fusion.2 = (f32[4,384]{1,0:T(4,128)S(1)}, f32[2240,384,4]{1,0,2:T(8,128)S(1)}) fusion(pred[384,2240]{0,1:T(8,128)(4,1)S(1)} %pad_add_fusion, bf16[384,4,128]{0,2,1:T(8,128)(2,1)} %bitcast.74, bf16[192,128]{1,0:T(8,128)(2,1)S(1)} %reshape.106, bf16[2048,128]{1,0:T(8,128)(2,1)} %bitcast.73), kind=kOutput, calls=%fused_computation.4 | convolution fusion | flops 892271104 | bytes 15595520 | tf_op jit(solution)/shard_map/tqd,kd->qtk/dot_general | solution.py:84
  88.4 3.3 fusion.3
  91.7 1.6 copy-done.1
  93.4 2.2 collective-permute-start.2
  95.6 7.8 %fusion = f32[4,384]{1,0:T(4,128)S(1)} fusion(f32[2240,384,4]{1,0,2:T(8,128)} %copy-done.1, f32[4,384]{1,0:T(4,128)S(1)} %get-tuple-element.14, pred[384,2240]{0,1:T(8,128)(4,1)S(1)} %pad_add_fusion), kind=kLoop, calls=%fused_computation.2 | loop fusion | flops 13761024 | bytes 14635008 | tf_op jit(solution)/shard_map/reduce_sum | solution.py:90
  103.4 3.6 %collective-permute-start.3 = (f32[2,384]{1,0:T(2,128)S(1)}, f32[2,384]{1,0:T(2,128)S(1)}, u32[]{:S(2)}, u32[]{:S(2)}) collective-permute-start(f32[2,384]{1,0:T(2,128)S(1)} %slice.65), channel_id=1, source_target_pairs={{0,1},{1,0},{2,3},{3,2},{4,5},{5,4},{6,7},{7,6},{8,9},{9,8},{10,11... | collective-permute-start | bytes 9224 | tf_op jit(solution)/shard_map/ppermute | solution.py:95
  107.1 2.2 collective-permute-start.1
  109.3 3.2 collective-permute-done.1
  112.7 2.1 convolution_convert_fusion.1
  114.9 0.8 fusion.31
  115.9 142.1 %all-reduce.5.cloned.1.call-done = bf16[384,2560]{1,0:T(8,128)(2,1)} async-done(((bf16[384,2560]{1,0:T(8,128)(2,1)}), bf16[384,2560]{1,0:T(8,128)(2,1)}) %all-reduce.5.cloned.1.call-update) | async-done | bytes 1966096 | tf_op jit(solution)/shard_map/psum | solution.py:109
  258.0 3.0 fusion.8
  261.1 5.6 %fusion.6 = f32[384,1280]{1,0:T(8,128)S(1)} fusion(bf16[2560,1920]{1,0:T(8,128)(2,1)} %all-gather.2.cloned.1.call-done, bf16[384,2560]{1,0:T(8,128)(2,1)S(1)} %get-tuple-element.6, f32[2560]{0:T(1024)S(1)} %convert_element_type.54, f32[384]{0:T(512)S(1)} %add_rsqrt_fusion), kind=kOutput, calls=%fused_computation.7 | convolution fusion | flops 2520514560 | bytes 10497536 | tf_op jit(solution)/shard_map/dot_general | solution.py:127
  266.7 5.0 %convolution_convert_fusion = bf16[384,2560]{1,0:T(8,128)(2,1)} fusion(bf16[2560,1920]{1,0:T(8,128)(2,1)} %all-gather.2.cloned.1.call-done, f32[384,1280]{1,0:T(8,128)S(1)} %fusion.6), kind=kOutput, calls=%fused_computation.11 | convolution fusion | flops 1260748800 | bytes 7208960 | tf_op jit(solution)/shard_map/dot_general | solution.py:131
  271.7 69.0 %reduce-scatter.2.cloned.1.call-done = bf16[24,2560]{1,0:T(8,128)(2,1)} async-done(((bf16[384,2560]{1,0:T(8,128)(2,1)}), bf16[24,2560]{1,0:T(8,128)(2,1)}) %reduce-scatter.2.cloned.1.call-update) | async-done | bytes 122896 | tf_op jit(solution)/shard_map/reduce_scatter | solution.py:137
  340.6 1.6 add_convert_fusion.1
  (55 shorter events, 1.3 us)
Async XLA Ops:
  7.4 105.3 %copy-start = (bf16[256,2560]{1,0:T(8,128)(2,1)S(1)}, bf16[256,2560]{1,0:T(8,128)(2,1)}, u32[]{:S(2)}) copy-start(bf16[256,2560]{1,0:T(8,128)(2,1)} %param.19) | copy-start | bytes 3932164
  7.4 1.4 copy-start.2
  7.4 1.7 copy-start.8
  7.4 1.7 copy-start.9
  8.9 16.6 %copy-start.4 = (bf16[384,256]{1,0:T(8,128)(2,1)S(1)}, bf16[384,256]{1,0:T(8,128)(2,1)}, u32[]{:S(2)}) copy-start(bf16[384,256]{1,0:T(8,128)(2,1)} %param.12) | copy-start | bytes 589828
  10.3 72.8 %all-to-all-start = ((bf16[280,16,128]{2,0,1:T(8,128)(2,1)}), bf16[280,16,128]{2,0,1:T(8,128)(2,1)S(1)}, u32[]{:S(2)}, u32[]{:S(2)}) async-start(bf16[280,16,128]{2,0,1:T(8,128)(2,1)} %pad_maximum_fusion), calls=%async_computation | async-start | bytes 2293760 | tf_op jit(solution)/shard_map/all_to_all | solution.py:54
  25.5 232.5 %all-reduce.5.cloned.1.call-start = ((), (), s32[]{:S(2)}) async-start(), calls=%async_computation.2 | async-start | bytes 3932160 | tf_op jit(solution)/shard_map/psum | solution.py:109
  25.7 55.7 %collective-permute-start = (bf16[384,256]{0,1:T(8,128)(2,1)S(1)}, bf16[384,256]{0,1:T(8,128)(2,1)}, u32[]{:S(2)}, u32[]{:S(2)}) collective-permute-start(bf16[384,256]{0,1:T(8,128)(2,1)S(1)} %copy.22), channel_id=1, source_target_pairs={{0,1},{1,0},{2,3},{3,2},{4,5},{5,4},{6,7},{7,6},{8,9},{9,8},{10,11... | collective-permute-start | bytes 589832 | tf_op jit(solution)/shard_map/ppermute | solution.py:63
  84.3 4.1 %copy-start.3 = (bf16[16,128,128]{2,1,0:T(8,128)(2,1)S(1)}, bf16[16,128,128]{2,1,0:T(8,128)(2,1)}, u32[]{:S(2)}) copy-start(bf16[16,128,128]{2,1,0:T(8,128)(2,1)} %get-tuple-element.10) | copy-start | bytes 1572868
  88.4 5.0 %copy-start.1 = (f32[2240,384,4]{1,0,2:T(8,128)}, f32[2240,384,4]{1,0,2:T(8,128)S(1)}, u32[]{:S(2)}) copy-start(f32[2240,384,4]{1,0,2:T(8,128)S(1)} %get-tuple-element.15) | copy-start | bytes 41287684
  93.4 19.2 %collective-permute-start.2 = (f32[2,384,128]{1,2,0:T(8,128)S(1)}, f32[2,384,128]{1,2,0:T(8,128)S(1)}, u32[]{:S(2)}, u32[]{:S(2)}) collective-permute-start(f32[2,384,128]{1,2,0:T(8,128)S(1)} %slice.63), channel_id=1, source_target_pairs={{0,1},{1,0},{2,3},{3,2},{4,5},{5,4},{6,7},{7,6},{8,9},{9,8},{10,11... | collective-permute-start | bytes 1179656 | tf_op jit(solution)/shard_map/ppermute | solution.py:95
  103.4 5.9 %collective-permute-start.3 = (f32[2,384]{1,0:T(2,128)S(1)}, f32[2,384]{1,0:T(2,128)S(1)}, u32[]{:S(2)}, u32[]{:S(2)}) collective-permute-start(f32[2,384]{1,0:T(2,128)S(1)} %slice.65), channel_id=1, source_target_pairs={{0,1},{1,0},{2,3},{3,2},{4,5},{5,4},{6,7},{7,6},{8,9},{9,8},{10,11... | collective-permute-start | bytes 9224 | tf_op jit(solution)/shard_map/ppermute | solution.py:95
  107.1 5.5 %collective-permute-start.1 = (f32[2,384]{1,0:T(2,128)S(1)}, f32[2,384]{1,0:T(2,128)S(1)}, u32[]{:S(2)}, u32[]{:S(2)}) collective-permute-start(f32[2,384]{1,0:T(2,128)S(1)} %slice.62), channel_id=1, source_target_pairs={{0,1},{1,0},{2,3},{3,2},{4,5},{5,4},{6,7},{7,6},{8,9},{9,8},{10,11... | collective-permute-start | bytes 9224 | tf_op jit(solution)/shard_map/ppermute | solution.py:95
  112.6 2.3 copy-start.5
  112.6 2.3 copy-start.6
  112.6 2.3 copy-start.7
  112.7 3.2 copy-start.10
  114.8 146.2 %all-gather.2.cloned.1.call-start = ((), (), s32[]{:S(2)}) async-start(), calls=%async_computation.3 | async-start | bytes 10137600 | tf_op jit(solution)/shard_map/all_gather | solution.py:121
  115.7 225.0 %reduce-scatter.2.cloned.1.call-start = ((), (), s32[]{:S(2)}) async-start(), calls=%async_computation.4 | async-start | bytes 2088960 | tf_op jit(solution)/shard_map/reduce_scatter | solution.py:137
Sparse Core Ops, SparseCore 0:
  114.9 143.0 all-reduce.4
  271.8 68.8 reduce-scatter.1
Sparse Core Ops, SparseCore 1:
  119.0 71.2 all-gather.1
